TPU v7x, 128 devices: a whole 4x4x4 slice. The times are simulated.
128 devices in a mesh: row: 4 (over x), col: 32 (over z, y, core).
Axes of the slice: x: 4, y: 4, z: 4, core: 2. Of those that a mesh axis runs over, the one named last changes fastest.
Arguments:
- child_factors: bfloat16 [2, 2048, 8192], P(None, 'col', 'row'), may hold values from -0.0625 to 0.0625
- child_tiles: int32 [2, 16], replicated, may hold values from 0 to 63, as said below
- root_diag: float32 [8192], P('col'), may hold values from 0.5 to 4
Outputs:
- front_out: float32 [8192, 8192], P('row', 'col')
Inputs may be any that keep to these rules, and one draw needn't show every extreme that they name: `child_tiles`: each row lists 2048 / 128 distinct root tiles in increasing order; the first child's list holds tile 0 and the second child's holds the last tile. For every r below 4, exactly 2048 / (128 * 4) tiles t of each row have ((t * 128) // 256) % 4 == r.
All inputs are finite; a program needn't handle non-finite values.
Results may differ from a plain program's by a relative error of at most 0.0003.
Values may be sent and summed in bfloat16 or wider, within the bound.
No kernel may reach another device: no remote copies, remote signals or barrier semaphores. Data moves between devices by JAX's collectives and lax.ppermute only.
A program may use at most 128 MiB of HBM per device.

v0:
```python
import jax
import jax.numpy as jnp
from jax import lax
from jax.sharding import PartitionSpec as P

TILE = 128
NPAN = 1


def broadcast(block, axis, source):
    block = jnp.where(lax.axis_index(axis) == source, block, jnp.zeros_like(block))
    return lax.psum(block, axis)


def pivot_factor(source, local_block, owner_row, block_size, identity, usable):
    diag_rows = source[local_block * block_size : (local_block + 1) * block_size]
    pivots = broadcast(diag_rows, "row", owner_row)
    return jnp.linalg.cholesky(jnp.where(usable, pivots, identity))


def solve_panel(source, factor, row_block, panel_step, blocks_here):
    solved = lax.linalg.triangular_solve(
        factor, source, left_side=False, lower=True, transpose_a=True
    )
    repeated = jnp.tile(jnp.tril(factor), (blocks_here, 1))
    later = (row_block > panel_step)[:, None]
    current = (row_block == panel_step)[:, None]
    return jnp.where(later, solved, jnp.where(current, repeated, 0.0))


def shards(child_factors, child_tiles, root_diag):
    highest = lax.Precision.HIGHEST
    row_count = lax.axis_size("row")
    col_count = lax.axis_size("col")
    block_size = root_diag.shape[0]
    order_total = block_size * col_count
    loc_rows = order_total // row_count
    blocks_here = loc_rows // block_size
    row_index = lax.axis_index("row")
    col_index = lax.axis_index("col")
    gathered = lax.all_gather(child_factors, "col", axis=1, tiled=True)
    tile_total = gathered.shape[1] // TILE
    tiles_per_col = block_size // TILE
    wanted = col_index * tiles_per_col + jnp.arange(tiles_per_col, dtype=jnp.int32)
    selector = (child_tiles[:, :, None] == wanted[None, None, :]).astype(jnp.bfloat16)
    tiled_rows = gathered.reshape(2, tile_total, TILE, gathered.shape[2])
    own_cols = jnp.einsum(
        "cui,cutk->citk", selector, tiled_rows, preferred_element_type=jnp.float32
    )
    own_cols = own_cols.astype(jnp.bfloat16).reshape(2, block_size, gathered.shape[2])
    partial_gram = jnp.einsum(
        "cnk,cmk->cnm", gathered, own_cols, preferred_element_type=jnp.float32
    )
    gram_tiles = partial_gram.reshape(2, tile_total, TILE, block_size)
    stored_tile = jnp.arange(lax.axis_size("row") * loc_rows // TILE, dtype=jnp.int32)
    stored_row = stored_tile * TILE
    owning = stored_row // loc_rows
    within = stored_row % loc_rows
    global_row = (owning + within // block_size * row_count) * block_size + within % block_size
    global_tile = global_row // TILE
    matches = (child_tiles[:, :, None] == global_tile[None, None, :]).astype(jnp.float32)
    placed = jnp.einsum("cus,cutm->stm", matches, gram_tiles, precision=highest)
    assembled = lax.psum_scatter(
        placed.reshape(lax.axis_size("row") * loc_rows, block_size),
        "row",
        scatter_dimension=0,
        tiled=True,
    )
    local_rows = jnp.arange(loc_rows, dtype=jnp.int32)
    row_block = row_index + local_rows // block_size * row_count
    glob_rows = row_block * block_size + local_rows % block_size
    glob_cols = col_index * block_size + jnp.arange(block_size, dtype=jnp.int32)
    front_now = assembled + jnp.where(
        glob_rows[:, None] == glob_cols[None, :], root_diag[None, :], 0.0
    )
    identity = jnp.eye(block_size, dtype=jnp.float32)
    owner_row = 0 % row_count
    local_block = 0 // row_count
    factor = pivot_factor(front_now, local_block, owner_row, block_size, identity, col_index == 0)
    own_panel = solve_panel(front_now, factor, row_block, 0, blocks_here)
    panel_block = broadcast(own_panel, "col", 0)
    own_block = lax.dynamic_slice_in_dim(
        panel_block, col_index // row_count * block_size, block_size, 0
    )
    across = broadcast(own_block.astype(jnp.bfloat16), "row", col_index % row_count).astype(
        own_block.dtype
    )
    update = jnp.dot(panel_block, across.T, precision=highest)
    front_now = jnp.where(col_index == 0, panel_block, front_now - update)
    upper_part = (row_block[:, None] < NPAN) & (col_index >= NPAN)
    return jnp.where(upper_part, 0.0, front_now)


def solution(mesh):
    placed = (P(None, "col", "row"), P(), P("col"))
    return jax.shard_map(
        shards, mesh=mesh, in_specs=placed, out_specs=P("row", "col"), check_vma=False
    )
```

profile of v0, /device:TPU:0, one launch (start us, length us, event | category | flops | bytes accessed | tf_op | source)
XLA Modules:
  0.0 501.5 jit_solution(1409809897628505502)
XLA Ops:
  6.5 0.7 all-gather.2.cloned.1.call-update
  7.3 0.0 reduce-scatter.2.cloned.1.call-start
  7.4 77.5 %all-gather.2.cloned.1.call-done = bf16[2,2048,2048]{2,1,0:T(8,128)(2,1)} async-done(((bf16[2,64,2048]{2,1,0:T(8,128)(2,1)}), bf16[2,2048,2048]{2,1,0:T(8,128)(2,1)}) %all-gather.2.cloned.1.call-update) | async-done | bytes 16777232 | tf_op jit(solution)/shard_map/all_gather | solution.py:41
  84.8 24.6 %fusion.2 = bf16[2,2,128,2048]{3,1,2,0:T(2,128)(2,1)S(1)} fusion(bf16[2,16,128,2048]{3,2,1,0:T(8,128)(2,1)} %bitcast.68, s32[2,16]{1,0:T(2,128)} %param.4, s32[2]{0:T(128)S(1)} %iota_add_fusion.1), kind=kOutput, calls=%fused_computation.5 | convolution fusion | flops 34603072 | bytes 18874504 | tf_op jit(solution)/shard_map/cui,cutk->citk/dot_general | solution.py:47
  109.5 2.2 copy.14
  111.7 13.0 %fusion.43 = f32[2,256,2048]{2,1,0:T(8,128)} fusion(bf16[2,256,2048]{2,1,0:T(8,128)(2,1)} %bitcast.73, bf16[2,2048,2048]{2,1,0:T(8,128)(2,1)} %all-gather.2.cloned.1.call-done), kind=kOutput, calls=%fused_computation.88 | convolution fusion | flops 4294967296 | bytes 23068672 | tf_op jit(solution)/shard_map/cnk,cmk->cnm/dot_general | solution.py:51
  124.7 3.1 copy.31
  127.9 3.6 fusion.21
  131.5 11.1 %copy.39 = f32[32,8,64,128]{3,1,2,0:T(8,128)} copy(f32[32,8,64,128]{3,2,1,0:T(8,128)S(1)} %bitcast.67) | data formatting | bytes 16777216
  142.6 0.0 all-reduce.5.cloned.1.call-start
  142.7 80.0 %reduce-scatter.2.cloned.1.call-done = f32[2048,256]{0,1:T(8,128)} async-done(((f32[8192,256]{0,1:T(8,128)}), f32[2048,256]{0,1:T(8,128)}) %reduce-scatter.2.cloned.1.call-update) | async-done | bytes 2097168 | tf_op jit(solution)/shard_map/reduce_scatter | solution.py:63
  222.7 1.9 select_add_fusion
  224.5 0.7 slice_select_fusion
  225.3 0.0 all-reduce.7.cloned.1.call-start
  225.4 41.6 %all-reduce.5.cloned.1.call-done = f32[256,256]{0,1:T(8,128)} async-done(((f32[256,256]{0,1:T(8,128)}), f32[256,256]{0,1:T(8,128)}) %all-reduce.5.cloned.1.call-update) | async-done | bytes 262160 | tf_op jit(solution)/shard_map/psum | solution.py:12
  267.0 1.0 convert_select_fusion
  267.9 0.1 copy.17
  268.1 1.0 fusion.10
  269.1 11.7 %cholesky.49 = f32[128,128]{1,0:T(8,128)S(1)} custom-call(f32[128,128]{1,0:T(8,128)S(1)} %cholesky.115), custom_call_target="Cholesky" | custom-call | tf_op jit(solution)/shard_map/jit(cholesky)/cholesky | solution.py:18
  280.8 9.8 %custom-call.14 = f32[1,128,128]{1,2,0:T(8,128)S(1)} custom-call(f32[1,128,128]{2,1,0:T(8,128)S(1)} %get-tuple-element.32), custom_call_target="InvertDiagBlocksLowerTriangular" | custom-call | tf_op jit(solution)/shard_map/jit(cholesky)/cholesky | solution.py:18
  290.7 0.2 fusion.14
  290.9 0.3 convolution_subtract_fusion.2
  291.1 11.7 %cholesky.103 = f32[128,128]{1,0:T(8,128)S(1)} custom-call(f32[128,128]{1,0:T(8,128)S(1)} %convolution_subtract_fusion.2), custom_call_target="Cholesky" | custom-call | tf_op jit(solution)/shard_map/jit(cholesky)/cholesky | solution.py:18
  302.9 0.1 copy.20
  303.0 0.1 copy.19
  303.1 0.1 copy.18
  303.2 0.7 compare_reduce_fusion
  305.4 0.1 tile.4
  305.5 2.2 copy.33
  307.7 0.1 triangular_solve.61
  307.8 4.5 while.1
  308.0 0.7 fusion.54
  308.7 1.3 dynamic-slice.7
  310.0 0.1 copy.41
  310.2 0.7 fusion.54
  310.8 1.3 dynamic-slice.7
  312.2 0.1 copy.41
  312.3 19.7 %custom-call.15 = f32[2,128,128]{1,2,0:T(8,128)S(1)} custom-call(f32[2,128,128]{2,1,0:T(8,128)S(1)} %get-tuple-element.12), custom_call_target="InvertDiagBlocksLowerTriangular" | custom-call | tf_op jit(solution)/shard_map/triangular_solve | solution.py:22
  332.0 1.1 fusion.8
  333.1 1.1 convolution_subtract_fusion.1
  334.2 1.1 fusion.12
  335.3 1.7 fusion.7
  337.0 0.0 all-reduce.9.cloned.1.call-start
  337.1 106.4 %all-reduce.7.cloned.1.call-done = f32[2048,256]{0,1:T(8,128)} async-done(((f32[2048,256]{0,1:T(8,128)}), f32[2048,256]{0,1:T(8,128)}) %all-reduce.7.cloned.1.call-update) | async-done | bytes 2097168 | tf_op jit(solution)/shard_map/psum | solution.py:12
  443.5 1.6 fusion.11
  445.1 41.5 %all-reduce.9.cloned.1.call-done = bf16[256,256]{0,1:T(8,128)(2,1)} async-done(((bf16[256,256]{0,1:T(8,128)(2,1)}), bf16[256,256]{0,1:T(8,128)(2,1)}) %all-reduce.9.cloned.1.call-update) | async-done | bytes 131088 | tf_op jit(solution)/shard_map/psum | solution.py:12
  486.7 5.0 fusion.6
  491.6 2.9 copy.23
  (30 shorter events, 0.3 us)
Async XLA Ops:
  6.5 78.3 %all-gather.2.cloned.1.call-start = ((), (), s32[]{:S(2)}) async-start(), calls=%async_computation.1 | async-start | bytes 17301504 | tf_op jit(solution)/shard_map/all_gather | solution.py:41
  7.3 215.4 %reduce-scatter.2.cloned.1.call-start = ((), (), s32[]{:S(2)}) async-start(), calls=%async_computation.2 | async-start | bytes 10485760 | tf_op jit(solution)/shard_map/reduce_scatter | solution.py:63
  124.7 3.1 copy-start.1
  142.6 80.1 %copy-start.2 = (f32[256]{0:T(256)S(1)}, f32[256]{0:T(256)}, u32[]{:S(2)}) copy-start(f32[256]{0:T(256)} %param.5) | copy-start | bytes 3076
  142.6 124.4 %all-reduce.5.cloned.1.call-start = ((), (), s32[]{:S(2)}) async-start(), calls=%async_computation.3 | async-start | bytes 524288 | tf_op jit(solution)/shard_map/psum | solution.py:12
  225.3 218.2 %all-reduce.7.cloned.1.call-start = ((), (), s32[]{:S(2)}) async-start(), calls=%async_computation.4 | async-start | bytes 4194304 | tf_op jit(solution)/shard_map/psum | solution.py:12
  333.1 2.2 copy-start
  337.0 149.7 %all-reduce.9.cloned.1.call-start = ((), (), s32[]{:S(2)}) async-start(), calls=%async_computation.5 | async-start | bytes 262144 | tf_op jit(solution)/shard_map/psum | solution.py:12
Sparse Core Ops, SparseCore 0:
  9.6 75.1 all-gather.1
  142.7 79.8 reduce-scatter.1
  225.4 41.5 all-reduce.4
  337.1 106.3 all-reduce.6
  445.6 40.9 all-reduce.8
where the time goes:
time: 510 us; the launch traced here: 501 us
  waiting for transfers between devices  348 us (68%)
  other arithmetic  61.7 us (12%)
  matrix products  50 us (10%)
  local copies, waits for them, and re-layouts  26.4 us (5%)
  between operations  15.2 us (3%)
    psum x3, waiting for transfers between devices, broadcast(): return lax.psum(block, axis)  190 us
    reduce_scatter x1, waiting for transfers between devices, shards(): lax.psum_scatter(placed.reshape(lax.axis_size('row') * loc_rows, block_si...  80 us
    all_gather x1, waiting for transfers between devices, shards(): gathered = lax.all_gather(child_factors, 'col', axis=1, tiled=True)  77.5 us
    another operation x6, other arithmetic, pivot_factor(): return jnp.linalg.cholesky(jnp.where(usable, pivots, identity))  34 us
    dot_general x1, matrix products, shards(): jnp.einsum('cui,cutk->citk', selector, tiled_rows, preferred_element_type...  24.6 us
    another operation x3, other arithmetic, solve_panel(): lax.linalg.triangular_solve(factor, source, left_side=False, lower=True,...  19.7 us
    unnamed x9, local copies, waits for them, and re-layouts  16.4 us
    dot_general x1, matrix products, shards(): jnp.einsum('cnk,cmk->cnm', gathered, own_cols, preferred_element_type=jnp...  13 us
  transfers between devices with their start and end apart: 5, of which 5 were waited for; matrix products, arithmetic and copies ran while one was open for 0% of the time, Pallas kernels for 0%

commit v1 on v0

v1 whole, which is shorter than its diff:
```python
import jax
import jax.numpy as jnp
from jax import lax
from jax.sharding import PartitionSpec as P

TILE = 128
NPAN = 1


def pick_tiles(tiles4, index):
    return jnp.take_along_axis(tiles4, index[:, :, None, None], axis=1)


def shards(child_factors, child_tiles, root_diag):
    highest = lax.Precision.HIGHEST
    row_count = lax.axis_size("row")
    block_size = root_diag.shape[0]
    col_count = lax.axis_size("col")
    order_total = block_size * col_count
    loc_rows = order_total // row_count
    row_index = lax.axis_index("row")
    col_index = lax.axis_index("col")
    n_child = child_tiles.shape[0]
    tiles_child = child_tiles.shape[1]
    per_group = tiles_child // row_count
    tiles_block = block_size // TILE
    loc_tiles = loc_rows // TILE

    gathered = lax.all_gather(child_factors, "col", axis=1, tiled=True)
    k_loc = gathered.shape[2]
    tiles4 = gathered.reshape(n_child, tiles_child, TILE, k_loc)
    full_diag = lax.all_gather(root_diag, "col", axis=0, tiled=True)

    owner = (child_tiles * TILE // block_size) % row_count
    position = jnp.arange(tiles_child, dtype=jnp.int32)
    key = owner * tiles_child + position[None, :]
    rank = jnp.sum(key[:, None, :] < key[:, :, None], axis=2).astype(jnp.int32)
    order = jnp.sum(
        jnp.where(rank[:, :, None] == position[None, None, :], position[None, :, None], 0),
        axis=1,
    ).astype(jnp.int32)
    grouped = pick_tiles(tiles4, order)

    own_tiles = col_index * tiles_block + jnp.arange(tiles_block, dtype=jnp.int32)
    pivot_tiles = jnp.arange(NPAN * tiles_block, dtype=jnp.int32)
    wanted = jnp.concatenate([own_tiles, pivot_tiles])
    match = child_tiles[:, :, None] == wanted[None, None, :]
    where_at = jnp.sum(jnp.where(match, position[None, :, None], 0), axis=1).astype(jnp.int32)
    present = jnp.any(match, axis=1)
    col_rows = pick_tiles(tiles4, where_at)
    col_rows = jnp.where(present[:, :, None, None], col_rows, jnp.zeros_like(col_rows))
    n_cols = wanted.shape[0] * TILE
    col_rows = col_rows.reshape(n_child, n_cols, k_loc)
    pivot_rows = col_rows[:, tiles_block * TILE :]

    grouped = grouped.reshape(n_child, row_count, per_group * TILE, k_loc)
    main = jnp.einsum(
        "cgnk,cmk->gcnm", grouped, col_rows, preferred_element_type=jnp.float32
    )
    extra = jnp.einsum(
        "cnk,cmk->cnm", pivot_rows, col_rows, preferred_element_type=jnp.float32
    )
    extra = jnp.broadcast_to(extra[None], (row_count,) + extra.shape)
    packed = jnp.concatenate([main, extra], axis=2)
    chunk_rows = packed.shape[2]
    reduced = lax.psum_scatter(
        packed.reshape(row_count * n_child * chunk_rows, n_cols),
        "row",
        scatter_dimension=0,
        tiled=True,
    ).reshape(n_child, chunk_rows, n_cols)
    mine = reduced[:, : per_group * TILE]
    pivot_part = jnp.sum(reduced[:, per_group * TILE :], axis=0)

    own_w = tiles_block * TILE
    lead_rows = NPAN * block_size
    pivot_diag = full_diag[:lead_rows]
    front00 = pivot_part[:, own_w:] + jnp.diag(pivot_diag)
    lead = jnp.tril(jnp.linalg.cholesky(front00))
    inv_t = lax.linalg.triangular_solve(
        lead, jnp.eye(lead_rows, dtype=jnp.float32), left_side=False, lower=True, transpose_a=True
    )
    cols_panel = jnp.where(col_index == 0, front00, pivot_part[:, :own_w]).T

    my_tiles = lax.dynamic_slice_in_dim(order, row_index * per_group, per_group, axis=1)
    my_root = jnp.take_along_axis(child_tiles, my_tiles, axis=1)
    my_local = (my_root * TILE // block_size) // row_count * tiles_block + my_root % tiles_block
    loc_index = jnp.arange(loc_tiles, dtype=jnp.int32)
    hit = my_local[:, None, :] == loc_index[None, :, None]
    src = jnp.sum(jnp.where(hit, jnp.arange(per_group, dtype=jnp.int32)[None, None, :], 0), axis=2)
    got = jnp.any(hit, axis=2)
    mine4 = mine.reshape(n_child, per_group, TILE, n_cols)
    placed = pick_tiles(mine4, src.astype(jnp.int32))
    placed = jnp.where(got[:, :, None, None], placed, jnp.zeros_like(placed))
    front_loc = jnp.sum(placed, axis=0).reshape(loc_rows, n_cols)

    local_rows = jnp.arange(loc_rows, dtype=jnp.int32)
    row_block = row_index + local_rows // block_size * row_count
    glob_rows = row_block * block_size + local_rows % block_size
    glob_cols = col_index * block_size + jnp.arange(block_size, dtype=jnp.int32)
    diag_own = jnp.where(glob_rows[:, None] == glob_cols[None, :], root_diag[None, :], 0.0)
    diag_pivot = jnp.where(
        glob_rows[:, None] == jnp.arange(lead_rows, dtype=jnp.int32)[None, :],
        pivot_diag[None, :],
        0.0,
    )
    front_own = front_loc[:, :own_w] + diag_own
    front_pivot = front_loc[:, own_w:] + diag_pivot

    below_rows = jnp.dot(front_pivot, inv_t, precision=highest)
    below_cols = jnp.dot(cols_panel, inv_t, precision=highest)
    schur = front_own - jnp.dot(below_rows, below_cols.T, precision=highest)

    in_lead = (row_block < NPAN)[:, None]
    lead_tiled = jnp.tile(lead, (loc_rows // lead_rows, 1))
    first_col = jnp.where(in_lead, lead_tiled, below_rows)
    rest = jnp.where(in_lead, 0.0, schur)
    return jnp.where(col_index < NPAN, first_col, rest)


def solution(mesh):
    placed = (P(None, "col", "row"), P(), P("col"))
    return jax.shard_map(
        shards, mesh=mesh, in_specs=placed, out_specs=P("row", "col"), check_vma=False
    )
```

time: 510 us -> 356 us (0.70); the launches traced: 501 us -> 355 us
  waiting for transfers between devices: 348 us -> 161 us
  matrix products: 50 us -> 25.5 us
  blocking collectives: 0 us -> 24.1 us
  local copies, waits for them, and re-layouts: 26.4 us -> 50.1 us
  other arithmetic: 61.7 us -> 79 us
    psum x3 -> x0, waiting for transfers between devices: 190 us -> none  [broadcast(): return lax.psum(block, axis)]
    gather x0 -> x9, local copies, waits for them, and re-layouts: none -> 27.1 us  [the longest x6 26.3 us: pick_tiles(): return jnp.take_along_axis(tiles4, index[:, :, None, None], axis=1)]
    all_gather x0 -> x1, blocking collectives: none -> 24.1 us  [shards(): full_diag = lax.all_gather(root_diag, 'col', axis=0, tiled=True)]
    dot_general x4 -> x5, matrix products: 46.3 us -> 23.3 us  [the longest x1 15.7 us: shards(): jnp.einsum('cgnk,cmk->gcnm', grouped, col_rows, preferred_element_type=jn...]
    unnamed x9 -> x26, local copies, waits for them, and re-layouts: 16.4 us -> 4.29 us
    concatenate x0 -> x1, local copies, waits for them, and re-layouts: none -> 10.7 us  [shards(): packed = jnp.concatenate([main, extra], axis=2)]
    reduce_sum x0 -> x6, other arithmetic: none -> 8.65 us  [the longest x1 6.07 us: shards(): front_loc = jnp.sum(placed, axis=0).reshape(loc_rows, n_cols)]
    concatenate x0 -> x2, other arithmetic: none -> 8.47 us  [the longest x1 8.39 us: shards(): packed = jnp.concatenate([main, extra], axis=2)]
  transfers between devices with their start and end apart: 5 -> 2, of which waited for: 5 -> 2; matrix products, arithmetic and copies ran while one was open for 0% -> 2% of each run, Pallas kernels for 0% -> 0%
where the time goes in v1:
time: 356 us; the launch traced here: 355 us
  waiting for transfers between devices  161 us (45%)
  other arithmetic  79 us (22%)
  local copies, waits for them, and re-layouts  50.1 us (14%)
  matrix products  25.5 us (7%)
  blocking collectives  24.1 us (7%)
  between operations  15.2 us (4%)
    reduce_scatter x1, waiting for transfers between devices, shards(): lax.psum_scatter(packed.reshape(row_count * n_child * chunk_rows, n_cols)...  85.8 us
    all_gather x1, waiting for transfers between devices, shards(): gathered = lax.all_gather(child_factors, 'col', axis=1, tiled=True)  74.3 us
    another operation x7, other arithmetic, shards(): lead = jnp.tril(jnp.linalg.cholesky(front00))  34.7 us
    gather x6, local copies, waits for them, and re-layouts, pick_tiles(): return jnp.take_along_axis(tiles4, index[:, :, None, None], axis=1)  26.3 us
    all_gather x1, blocking collectives, shards(): full_diag = lax.all_gather(root_diag, 'col', axis=0, tiled=True)  24.1 us
    another operation x3, other arithmetic, shards(): lax.linalg.triangular_solve(lead, jnp.eye(lead_rows, dtype=jnp.float32),...  21.1 us
    dot_general x1, matrix products, shards(): jnp.einsum('cgnk,cmk->gcnm', grouped, col_rows, preferred_element_type=jn...  15.7 us
    concatenate x1, local copies, waits for them, and re-layouts, shards(): packed = jnp.concatenate([main, extra], axis=2)  10.7 us
  transfers between devices with their start and end apart: 2, of which 2 were waited for; matrix products, arithmetic and copies ran while one was open for 2% of the time, Pallas kernels for 0%

profile of v1, /device:TPU:0, one launch (start us, length us, event | category | flops | bytes accessed | tf_op | source)
XLA Modules:
  0.0 354.8 jit_solution(1006790094316008561)
XLA Ops:
  6.5 0.7 all-gather.3.cloned.1.call-update
  7.4 0.9 fusion.44
  8.4 0.7 fusion.48
  9.5 0.9 compare_reduce_fusion
  10.6 74.3 %all-gather.3.cloned.1.call-done = bf16[2,2048,2048]{2,1,0:T(8,128)(2,1)} async-done(((bf16[2,64,2048]{2,1,0:T(8,128)(2,1)}), bf16[2,2048,2048]{2,1,0:T(8,128)(2,1)}) %all-gather.3.cloned.1.call-update) | async-done | bytes 16777232 | tf_op jit(solution)/shard_map/all_gather | solution.py:29
  84.8 8.6 %gather_fusion = bf16[8,128,2048]{2,1,0:T(8,128)(2,1)} fusion(bf16[2,16,128,2048]{3,2,1,0:T(8,128)(2,1)} %bitcast.84, s32[8]{0:T(128)S(1)} %reshape.246), kind=kCustom, calls=%fused_computation | custom fusion | bytes 8388672 | tf_op jit(solution)/shard_map/jit(take_along_axis)/gather | solution.py:11
  93.5 13.1 %gather_fusion.1 = bf16[32,128,2048]{2,1,0:T(8,128)(2,1)} fusion(bf16[2,16,128,2048]{3,2,1,0:T(8,128)(2,1)} %bitcast.85, s32[32]{0:T(128)S(1)} %reshape.252), kind=kCustom, calls=%fused_computation.1 | custom fusion | bytes 33554688 | tf_op jit(solution)/shard_map/jit(take_along_axis)/gather | solution.py:11
  106.6 2.6 fusion.5
  109.2 1.9 copy-done.1
  111.1 1.3 fusion.14
  112.4 15.7 %fusion.6 = f32[4,2,512,512]{3,2,0,1:T(8,128)} fusion(bf16[2,4,512,2048]{3,2,1,0:T(8,128)(2,1)} %bitcast.88, pred[2,4,512]{2,1,0:T(4,128)(4,1)S(1)} %broadcast_in_dim.194, bf16[2,512,2048]{2,1,0:T(8,128)(2,1)} %copy-done.1), kind=kOutput, calls=%fused_computation.15 | convolution fusion | flops 8598323200 | bytes 29364224 | tf_op jit(solution)/shard_map/cgnk,cmk->gcnm/dot_general | solution.py:57
  128.1 0.5 broadcast_in_dim.197
  128.6 8.4 %pad_maximum_fusion = f32[4,2,768,512]{3,2,0,1:T(8,128)} fusion(f32[4,2,256,512]{3,2,0,1:T(8,128)S(1)} %broadcast_in_dim.197, f32[4,2,512,512]{3,2,0,1:T(8,128)} %fusion.6), kind=kLoop, calls=%fused_computation.9 | loop fusion | flops 3145728 | bytes 25165824 | tf_op jit(solution)/shard_map/concatenate | solution.py:64
  137.0 10.7 %copy.27 = f32[4,2,768,512]{3,2,1,0:T(8,128)} copy(f32[4,2,768,512]{3,2,0,1:T(8,128)} %pad_maximum_fusion) | data formatting | bytes 25165824 | tf_op jit(solution)/shard_map/concatenate | solution.py:64
  147.7 0.6 copy-done.5
  148.4 24.1 %all-gather = f32[32,1,256]{2,1,0:T(1,128)S(1)} all-gather(f32[1,1,256]{2,1,0:T(1,128)S(1)} %bitcast.95), channel_id=1, replica_groups=mesh['row'=4,'col'=32] {'col'}, dimensions={0}, use_global_device_ids=true | all-gather | bytes 33792 | tf_op jit(solution)/shard_map/all_gather | solution.py:32
  172.6 0.7 gather_fusion.2
  173.7 0.6 iota_multiply_fusion
  174.2 0.6 iota_add_fusion
  174.8 0.6 fusion.45
  175.5 0.5 compare_and_fusion
  176.0 85.8 %reduce-scatter.2.cloned.1.call-done = f32[1536,512]{1,0:T(8,128)} async-done(((f32[6144,512]{1,0:T(8,128)}), f32[1536,512]{1,0:T(8,128)}) %reduce-scatter.2.cloned.1.call-update) | async-done | bytes 3145744 | tf_op jit(solution)/shard_map/reduce_scatter | solution.py:66
  261.8 1.4 slice_reduce_fusion
  263.5 11.7 %cholesky.49 = f32[128,128]{1,0:T(8,128)S(1)} custom-call(f32[128,128]{1,0:T(8,128)S(1)} %cholesky.115), custom_call_target="Cholesky" | custom-call | tf_op jit(solution)/shard_map/jit(cholesky)/cholesky | solution.py:79
  275.3 9.8 %custom-call.14 = f32[1,128,128]{1,2,0:T(8,128)S(1)} custom-call(f32[1,128,128]{2,1,0:T(8,128)S(1)} %get-tuple-element.44), custom_call_target="InvertDiagBlocksLowerTriangular" | custom-call | tf_op jit(solution)/shard_map/jit(cholesky)/cholesky | solution.py:79
  285.1 0.2 fusion.29
  285.3 0.3 convolution_subtract_fusion.2
  285.6 11.7 %cholesky.103 = f32[128,128]{1,0:T(8,128)S(1)} custom-call(f32[128,128]{1,0:T(8,128)S(1)} %convolution_subtract_fusion.2), custom_call_target="Cholesky" | custom-call | tf_op jit(solution)/shard_map/jit(cholesky)/cholesky | solution.py:79
  297.6 1.8 slice.99
  299.4 0.7 compare_reduce_fusion.1
  300.1 0.6 compare_reduce_fusion.2
  302.2 0.7 triangular_solve.45
  302.9 4.3 %while.1 = (s32[]{:T(128)}, f32[256,256]{0,1:T(8,128)S(1)}, s32[2,2]{1,0:T(2,128)S(1)}, f32[2,128,128]{2,1,0:T(8,128)S(1)}, s32[]{:T(128)}) while((s32[]{:T(128)}, f32[256,256]{0,1:T(8,128)S(1)}, s32[2,2]{1,0:T(2,128)S(1)}, f32[2,128,128]{2,1,0:T(8,128)S(1)}, s32[]{:T(128)}) %tuple.28), condition=%wide.while_cond, body=%wide.while_body.sunk | while | flops 2 | bytes 393321 | solution.py:80
  303.0 0.6 fusion.74
  303.6 1.4 dynamic-slice.7
  305.1 0.6 fusion.74
  305.7 1.4 dynamic-slice.7
  307.3 0.6 copy-done.10
  307.9 20.5 %custom-call.15 = f32[2,128,128]{1,2,0:T(8,128)S(1)} custom-call(f32[2,128,128]{2,1,0:T(8,128)} %copy-done.10), custom_call_target="InvertDiagBlocksLowerTriangular" | custom-call | tf_op jit(solution)/shard_map/triangular_solve | solution.py:80
  328.4 0.6 copy-done.2
  329.1 0.3 fusion.24
  329.4 0.3 convolution_subtract_fusion.1
  329.7 1.2 fusion.27
  331.1 4.3 %gather_fusion.3 = f32[32,128,512]{2,1,0:T(8,128)} fusion(f32[2,4,128,512]{3,2,1,0:T(8,128)S(1)} %bitcast.81, s32[32]{0:T(128)S(1)} %reshape.264), kind=kCustom, calls=%fused_computation.3 | custom fusion | bytes 16777472 | tf_op jit(solution)/shard_map/jit(take_along_axis)/gather | solution.py:11
  335.4 0.4 fusion.21
  335.9 6.1 %select_reduce_fusion = f32[16,128,512]{2,1,0:T(8,128)S(1)} fusion(f32[2,16,128,512]{3,2,1,0:T(8,128)} %bitcast.83, pred[2,16]{1,0:T(4,128)(4,1)S(1)} %copy-done.9, pred[2,16]{1,0:T(4,128)(4,1)S(1)} %copy-done.8), kind=kLoop, calls=%fused_computation.10 | loop fusion | flops 5242880 | bytes 12582976 | tf_op jit(solution)/shard_map/reduce_sum | solution.py:95
  342.0 2.0 bitcast_select_fusion.1
  344.1 3.9 %fusion.12 = f32[2048,256]{1,0:T(8,128)} fusion(f32[2048,256]{1,0:T(8,128)S(1)} %get-tuple-element.45, f32[2048,256]{1,0:T(8,128)S(1)} %get-tuple-element.46, f32[256,256]{1,0:T(8,128)S(1)} %fusion.21, f32[2048,512]{1,0:T(8,128)S(1)} %bitcast.87, f32[256]{0:T(256)S(1)} %copy-done.6, s32[256]{0:T(256)S(1)} %copy-done.7, s32[2048]{0:T(1024)S(1)} %fusion.40, ...), kind=kOutput, calls=%fused_computation.18 | convolution fusion | flops 1613758464 | bytes 8663041 | tf_op jit(solution)/shard_map/dot_general | solution.py:112
  (72 shorter events, 2.7 us)
Async XLA Ops:
  6.5 78.3 %all-gather.3.cloned.1.call-start = ((), (), s32[]{:S(2)}) async-start(), calls=%async_computation.1 | async-start | bytes 17301504 | tf_op jit(solution)/shard_map/all_gather | solution.py:29
  7.3 254.5 %reduce-scatter.2.cloned.1.call-start = ((), (), s32[]{:S(2)}) async-start(), calls=%async_computation.2 | async-start | bytes 15728640 | tf_op jit(solution)/shard_map/reduce_scatter | solution.py:66
  109.2 1.9 copy-start.1
  147.7 0.7 copy-start.5
  147.7 24.9 %copy-start = (s32[2,16]{1,0:T(2,128)S(1)}, s32[2,16]{1,0:T(2,128)}, u32[]{:S(2)}) copy-start(s32[2,16]{1,0:T(2,128)} %param.4) | copy-start | bytes 388
  172.5 91.0 %copy-start.3 = (f32[1,1,256]{2,1,0:T(1,128)}, f32[1,1,256]{2,1,0:T(1,128)S(1)}, u32[]{:S(2)}) copy-start(f32[1,1,256]{2,1,0:T(1,128)S(1)} %slice.98) | copy-start | bytes 3076
  307.3 0.7 copy-start.10
  328.4 0.7 copy-start.2
  331.1 4.8 %copy-start.8 = (pred[2,16]{1,0:T(4,128)(4,1)S(1)}, pred[2,16]{1,0:T(4,128)(4,1)}, u32[]{:S(2)}) copy-start(pred[2,16]{1,0:T(4,128)(4,1)} %fusion.45) | copy-start | bytes 100
  331.1 4.8 %copy-start.9 = (pred[2,16]{1,0:T(4,128)(4,1)S(1)}, pred[2,16]{1,0:T(4,128)(4,1)}, u32[]{:S(2)}) copy-start(pred[2,16]{1,0:T(4,128)(4,1)} %compare_and_fusion) | copy-start | bytes 100
  335.9 6.1 %copy-start.4 = (f32[1,1,256]{2,1,0:T(1,128)S(1)}, f32[1,1,256]{2,1,0:T(1,128)}, u32[]{:S(2)}) copy-start(f32[1,1,256]{2,1,0:T(1,128)} %copy-done.3) | copy-start | bytes 3076
  342.0 2.1 copy-start.6
  342.0 2.1 copy-start.7
Sparse Core Ops, SparseCore 0:
  9.6 75.1 all-gather.2
  147.9 113.8 reduce-scatter.1

commit v2 on v1

--- a/solution.py
+++ b/solution.py
@@ -53,24 +53,21 @@
     col_rows = col_rows.reshape(n_child, n_cols, k_loc)
     pivot_rows = col_rows[:, tiles_block * TILE :]
 
+    extra = jnp.einsum(
+        "cnk,cmk->nm", pivot_rows, col_rows, preferred_element_type=jnp.float32
+    )
+    pivot_part = lax.psum(extra, "row")
+
     grouped = grouped.reshape(n_child, row_count, per_group * TILE, k_loc)
     main = jnp.einsum(
         "cgnk,cmk->gcnm", grouped, col_rows, preferred_element_type=jnp.float32
     )
-    extra = jnp.einsum(
-        "cnk,cmk->cnm", pivot_rows, col_rows, preferred_element_type=jnp.float32
-    )
-    extra = jnp.broadcast_to(extra[None], (row_count,) + extra.shape)
-    packed = jnp.concatenate([main, extra], axis=2)
-    chunk_rows = packed.shape[2]
-    reduced = lax.psum_scatter(
-        packed.reshape(row_count * n_child * chunk_rows, n_cols),
+    mine = lax.psum_scatter(
+        main.reshape(row_count * n_child * per_group * TILE, n_cols),
         "row",
         scatter_dimension=0,
         tiled=True,
-    ).reshape(n_child, chunk_rows, n_cols)
-    mine = reduced[:, : per_group * TILE]
-    pivot_part = jnp.sum(reduced[:, per_group * TILE :], axis=0)
+    ).reshape(n_child, per_group * TILE, n_cols)
 
     own_w = tiles_block * TILE
     lead_rows = NPAN * block_size
@@ -99,13 +96,8 @@
     glob_rows = row_block * block_size + local_rows % block_size
     glob_cols = col_index * block_size + jnp.arange(block_size, dtype=jnp.int32)
     diag_own = jnp.where(glob_rows[:, None] == glob_cols[None, :], root_diag[None, :], 0.0)
-    diag_pivot = jnp.where(
-        glob_rows[:, None] == jnp.arange(lead_rows, dtype=jnp.int32)[None, :],
-        pivot_diag[None, :],
-        0.0,
-    )
     front_own = front_loc[:, :own_w] + diag_own
-    front_pivot = front_loc[:, own_w:] + diag_pivot
+    front_pivot = front_loc[:, own_w:]
 
     below_rows = jnp.dot(front_pivot, inv_t, precision=highest)
     below_cols = jnp.dot(cols_panel, inv_t, precision=highest)

time: 356 us -> 265 us (0.74)
  waiting for transfers between devices: 161 us -> 87.5 us
  other arithmetic: 79 us -> 68.2 us
  local copies, waits for them, and re-layouts: 50.1 us -> 43.6 us
    reduce_scatter x1, waiting for transfers between devices: 85.8 us -> 12.5 us  [shards(): lax.psum_scatter(main.reshape(row_count * n_child * per_group * TILE, n_c...]
    concatenate x1 -> x0, local copies, waits for them, and re-layouts: 10.7 us -> none  [shards(): packed = jnp.concatenate([main, extra], axis=2)]
    concatenate x1 -> x0, other arithmetic: 8.39 us -> none  [shards(): packed = jnp.concatenate([main, extra], axis=2)]
    transpose x0 -> x1, local copies, waits for them, and re-layouts: none -> 7.58 us  [shards(): jnp.einsum('cgnk,cmk->gcnm', grouped, col_rows, preferred_element_type=jn...]
  transfers between devices with their start and end apart: 2 -> 3, of which waited for: 2 -> 2; matrix products, arithmetic and copies ran while one was open for 2% -> 34% of each run, Pallas kernels for 0% -> 0%
where the time goes in v2:
time: 265 us; the launch traced here: 264 us
  waiting for transfers between devices  87.5 us (33%)
  other arithmetic  68.2 us (26%)
  local copies, waits for them, and re-layouts  43.6 us (16%)
  matrix products  25.4 us (10%)
  blocking collectives  24.1 us (9%)
  between operations  14.6 us (6%)
    all_gather x1, waiting for transfers between devices, shards(): gathered = lax.all_gather(child_factors, 'col', axis=1, tiled=True)  74.3 us
    another operation x7, other arithmetic, shards(): lead = jnp.tril(jnp.linalg.cholesky(front00))  34.6 us
    gather x6, local copies, waits for them, and re-layouts, pick_tiles(): return jnp.take_along_axis(tiles4, index[:, :, None, None], axis=1)  27.9 us
    all_gather x1, blocking collectives, shards(): full_diag = lax.all_gather(root_diag, 'col', axis=0, tiled=True)  24.1 us
    another operation x3, other arithmetic, shards(): lax.linalg.triangular_solve(lead, jnp.eye(lead_rows, dtype=jnp.float32),...  19.7 us
    dot_general x1, matrix products, shards(): jnp.einsum('cgnk,cmk->gcnm', grouped, col_rows, preferred_element_type=jn...  15.7 us
    reduce_scatter x1, waiting for transfers between devices, shards(): lax.psum_scatter(main.reshape(row_count * n_child * per_group * TILE, n_c...  12.5 us
    transpose x1, local copies, waits for them, and re-layouts, shards(): jnp.einsum('cgnk,cmk->gcnm', grouped, col_rows, preferred_element_type=jn...  7.58 us
  transfers between devices with their start and end apart: 3, of which 2 were waited for; matrix products, arithmetic and copies ran while one was open for 34% of the time, Pallas kernels for 0%

profile of v2, /device:TPU:0, one launch (start us, length us, event | category | flops | bytes accessed | tf_op | source)
XLA Modules:
  0.0 263.7 jit_solution(17079132194827854890)
XLA Ops:
  6.5 0.7 all-gather.3.cloned.1.call-update
  7.4 0.9 fusion.43
  8.4 0.7 fusion.47
  9.1 0.2 convert_reduce_fusion
  9.2 0.1 select_reduce_fusion.3
  9.5 0.9 compare_reduce_fusion
  10.6 74.3 %all-gather.3.cloned.1.call-done = bf16[2,2048,2048]{2,1,0:T(8,128)(2,1)} async-done(((bf16[2,64,2048]{2,1,0:T(8,128)(2,1)}), bf16[2,2048,2048]{2,1,0:T(8,128)(2,1)}) %all-gather.3.cloned.1.call-update) | async-done | bytes 16777232 | tf_op jit(solution)/shard_map/all_gather | solution.py:29
  84.8 8.6 %gather_fusion = bf16[8,128,2048]{2,1,0:T(8,128)(2,1)} fusion(bf16[2,16,128,2048]{3,2,1,0:T(8,128)(2,1)} %bitcast.85, s32[8]{0:T(128)S(1)} %reshape.236), kind=kCustom, calls=%fused_computation | custom fusion | bytes 8388672 | tf_op jit(solution)/shard_map/jit(take_along_axis)/gather | solution.py:11
  93.5 13.1 %gather_fusion.2 = bf16[32,128,2048]{2,1,0:T(8,128)(2,1)} fusion(bf16[2,16,128,2048]{3,2,1,0:T(8,128)(2,1)} %bitcast.86, s32[32]{0:T(128)S(1)} %reshape.248), kind=kCustom, calls=%fused_computation.2 | custom fusion | bytes 33554688 | tf_op jit(solution)/shard_map/jit(take_along_axis)/gather | solution.py:11
  106.6 2.6 fusion.5
  109.2 2.0 copy-done.1
  111.1 2.1 fusion.17
  113.3 15.7 %fusion.6 = f32[4,2,512,512]{3,2,0,1:T(8,128)} fusion(bf16[2,4,512,2048]{3,2,1,0:T(8,128)(2,1)} %bitcast.89, pred[2,4,512]{2,1,0:T(4,128)(4,1)S(1)} %broadcast_in_dim.185, bf16[2,512,2048]{2,1,0:T(8,128)(2,1)} %copy-done.1), kind=kOutput, calls=%fused_computation.14 | convolution fusion | flops 8598323200 | bytes 29364224 | tf_op jit(solution)/shard_map/cgnk,cmk->gcnm/dot_general | solution.py:62
  129.0 7.6 %copy.34 = f32[4,2,512,512]{3,2,1,0:T(8,128)} copy(f32[4,2,512,512]{3,2,0,1:T(8,128)} %fusion.6) | data formatting | bytes 16777216 | tf_op jit(solution)/shard_map/cgnk,cmk->gcnm/transpose | solution.py:62
  136.8 0.5 copy-done
  137.3 0.7 gather_fusion.1
  138.0 0.1 fusion.45
  138.3 24.1 %all-gather = f32[32,1,256]{2,1,0:T(1,128)S(1)} all-gather(f32[1,1,256]{2,1,0:T(1,128)S(1)} %bitcast.93), channel_id=1, replica_groups=mesh['row'=4,'col'=32] {'col'}, dimensions={0}, use_global_device_ids=true | all-gather | bytes 33792 | tf_op jit(solution)/shard_map/all_gather | solution.py:32
  162.4 0.1 fusion.44
  162.6 1.0 slice_add_fusion.1
  163.7 0.1 copy.29
  163.8 1.0 fusion.21
  164.8 11.7 %cholesky.49 = f32[128,128]{1,0:T(8,128)S(1)} custom-call(f32[128,128]{1,0:T(8,128)S(1)} %cholesky.115), custom_call_target="Cholesky" | custom-call | tf_op jit(solution)/shard_map/jit(cholesky)/cholesky | solution.py:76
  176.5 0.1 copy.30
  176.7 9.8 %custom-call.14 = f32[1,128,128]{1,2,0:T(8,128)S(1)} custom-call(f32[1,128,128]{2,1,0:T(8,128)S(1)} %get-tuple-element.42), custom_call_target="InvertDiagBlocksLowerTriangular" | custom-call | tf_op jit(solution)/shard_map/jit(cholesky)/cholesky | solution.py:76
  186.5 0.2 fusion.28
  186.8 0.3 convolution_subtract_fusion.2
  187.1 11.7 %cholesky.103 = f32[128,128]{1,0:T(8,128)S(1)} custom-call(f32[128,128]{1,0:T(8,128)S(1)} %convolution_subtract_fusion.2), custom_call_target="Cholesky" | custom-call | tf_op jit(solution)/shard_map/jit(cholesky)/cholesky | solution.py:76
  198.8 0.1 copy.32
  198.9 0.6 compare_reduce_fusion.1
  199.5 0.6 compare_reduce_fusion.2
  201.5 4.2 %while.1 = (s32[]{:T(128)}, f32[256,256]{0,1:T(8,128)S(1)}, s32[2,2]{1,0:T(2,128)S(1)}, f32[2,128,128]{2,1,0:T(8,128)S(1)}, s32[]{:T(128)}) while((s32[]{:T(128)}, f32[256,256]{0,1:T(8,128)S(1)}, s32[2,2]{1,0:T(2,128)S(1)}, f32[2,128,128]{2,1,0:T(8,128)S(1)}, s32[]{:T(128)}) %tuple.27), condition=%wide.while_cond, body=%wide.while_body.sunk | while | flops 2 | bytes 393321 | solution.py:77
  201.7 0.6 fusion.71
  202.3 1.3 dynamic-slice.7
  203.8 0.6 fusion.71
  204.3 1.3 dynamic-slice.7
  205.6 0.1 copy.47
  205.8 19.7 %custom-call.15 = f32[2,128,128]{1,2,0:T(8,128)S(1)} custom-call(f32[2,128,128]{2,1,0:T(8,128)S(1)} %get-tuple-element.12), custom_call_target="InvertDiagBlocksLowerTriangular" | custom-call | tf_op jit(solution)/shard_map/triangular_solve | solution.py:77
  225.4 0.1 copy.33
  225.6 0.3 fusion.23
  225.9 0.3 convolution_subtract_fusion.1
  226.2 0.3 fusion.26
  226.5 0.4 fusion.20
  226.9 12.5 %reduce-scatter.2.cloned.1.call-done = f32[1024,512]{1,0:T(8,128)} async-done(((f32[4096,512]{1,0:T(8,128)}), f32[1024,512]{1,0:T(8,128)}) %reduce-scatter.2.cloned.1.call-update) | async-done | bytes 2097168 | tf_op jit(solution)/shard_map/reduce_scatter | solution.py:65
  239.4 5.9 %gather_fusion.3 = f32[32,128,512]{2,1,0:T(8,128)} fusion(f32[2,4,128,512]{3,2,1,0:T(8,128)} %bitcast.83, s32[32]{0:T(128)S(1)} %reshape.254), kind=kCustom, calls=%fused_computation.3 | custom fusion | bytes 16777472 | tf_op jit(solution)/shard_map/jit(take_along_axis)/gather | solution.py:11
  245.3 6.1 %select_reduce_fusion = f32[16,128,512]{2,1,0:T(8,128)S(1)} fusion(f32[2,16,128,512]{3,2,1,0:T(8,128)} %bitcast.82, pred[2,16]{1,0:T(4,128)(4,1)S(1)} %compare_and_fusion.1, pred[2,16]{1,0:T(4,128)(4,1)S(1)} %fusion.44), kind=kLoop, calls=%fused_computation.9 | loop fusion | flops 5242880 | bytes 12582976 | tf_op jit(solution)/shard_map/reduce_sum | solution.py:92
  251.4 1.9 bitcast_select_fusion.1
  253.3 3.9 %fusion.12 = f32[2048,256]{1,0:T(8,128)} fusion(f32[2048,256]{1,0:T(8,128)S(1)} %get-tuple-element.43, f32[2048,256]{1,0:T(8,128)S(1)} %get-tuple-element.44, f32[256,256]{1,0:T(8,128)S(1)} %fusion.20, f32[2048,512]{1,0:T(8,128)S(1)} %bitcast.88, f32[256]{0:T(256)S(1)} %copy-done.3, s32[256]{0:T(256)S(1)} %iota_add_fusion, s32[2048]{0:T(1024)S(1)} %fusion.39, ...), kind=kOutput, calls=%fused_computation.17 | convolution fusion | flops 1613758464 | bytes 8663041 | tf_op jit(solution)/shard_map/dot_general | solution.py:104
  (54 shorter events, 1.6 us)
Async XLA Ops:
  6.5 78.3 %all-gather.3.cloned.1.call-start = ((), (), s32[]{:S(2)}) async-start(), calls=%async_computation.1 | async-start | bytes 17301504 | tf_op jit(solution)/shard_map/all_gather | solution.py:29
  7.3 155.3 %all-reduce.3.cloned.1.call-start = ((), (), s32[]{:S(2)}) async-start(), calls=%async_computation.2 | async-start | bytes 1048576 | tf_op jit(solution)/shard_map/psum | solution.py:59
  109.2 2.0 copy-start.1
  113.2 126.2 %reduce-scatter.2.cloned.1.call-start = ((), (), s32[]{:S(2)}) async-start(), calls=%async_computation.3 | async-start | bytes 10485760 | tf_op jit(solution)/shard_map/reduce_scatter | solution.py:65
  136.6 0.7 copy-start
  136.6 1.7 copy-start.3
  162.6 63.9 %copy-start.2 = (f32[256,512]{0,1:T(8,128)S(1)}, f32[256,512]{0,1:T(8,128)}, u32[]{:S(2)}) copy-start(f32[256,512]{0,1:T(8,128)} %all-reduce.3.cloned.1.call-done) | copy-start | bytes 1572868
Sparse Core Ops, SparseCore 0:
  9.6 75.1 all-gather.2
  113.4 42.4 all-reduce.2
  158.4 80.9 reduce-scatter.1

commit v3 on v2

--- a/solution.py
+++ b/solution.py
@@ -26,10 +26,14 @@
     tiles_block = block_size // TILE
     loc_tiles = loc_rows // TILE
 
-    gathered = lax.all_gather(child_factors, "col", axis=1, tiled=True)
-    k_loc = gathered.shape[2]
-    tiles4 = gathered.reshape(n_child, tiles_child, TILE, k_loc)
-    full_diag = lax.all_gather(root_diag, "col", axis=0, tiled=True)
+    diag_hi = lax.reduce_precision(root_diag, exponent_bits=8, mantissa_bits=7)
+    diag_rest = root_diag - diag_hi
+    diag_mid = lax.reduce_precision(diag_rest, exponent_bits=8, mantissa_bits=7)
+    diag_lo = diag_rest - diag_mid
+    diag_parts = jnp.stack([diag_hi, diag_mid, diag_lo]).astype(jnp.bfloat16).reshape(-1, TILE)
+    rows_here = child_factors.shape[1]
+    diag_block = jnp.zeros((rows_here, TILE), jnp.bfloat16)
+    diag_block = lax.dynamic_update_slice(diag_block, diag_parts, (0, 0))
 
     owner = (child_tiles * TILE // block_size) % row_count
     position = jnp.arange(tiles_child, dtype=jnp.int32)
@@ -39,35 +43,58 @@
         jnp.where(rank[:, :, None] == position[None, None, :], position[None, :, None], 0),
         axis=1,
     ).astype(jnp.int32)
-    grouped = pick_tiles(tiles4, order)
-
     own_tiles = col_index * tiles_block + jnp.arange(tiles_block, dtype=jnp.int32)
     pivot_tiles = jnp.arange(NPAN * tiles_block, dtype=jnp.int32)
     wanted = jnp.concatenate([own_tiles, pivot_tiles])
     match = child_tiles[:, :, None] == wanted[None, None, :]
     where_at = jnp.sum(jnp.where(match, position[None, :, None], 0), axis=1).astype(jnp.int32)
     present = jnp.any(match, axis=1)
-    col_rows = pick_tiles(tiles4, where_at)
-    col_rows = jnp.where(present[:, :, None, None], col_rows, jnp.zeros_like(col_rows))
     n_cols = wanted.shape[0] * TILE
-    col_rows = col_rows.reshape(n_child, n_cols, k_loc)
-    pivot_rows = col_rows[:, tiles_block * TILE :]
 
-    extra = jnp.einsum(
-        "cnk,cmk->nm", pivot_rows, col_rows, preferred_element_type=jnp.float32
-    )
-    pivot_part = lax.psum(extra, "row")
-
-    grouped = grouped.reshape(n_child, row_count, per_group * TILE, k_loc)
-    main = jnp.einsum(
-        "cgnk,cmk->gcnm", grouped, col_rows, preferred_element_type=jnp.float32
-    )
-    mine = lax.psum_scatter(
-        main.reshape(row_count * n_child * per_group * TILE, n_cols),
-        "row",
-        scatter_dimension=0,
-        tiled=True,
-    ).reshape(n_child, per_group * TILE, n_cols)
+    mine_parts = []
+    extra = None
+    carry = None
+    for child in range(n_child):
+        factors = child_factors[child]
+        k_loc = factors.shape[1]
+        last = child == n_child - 1
+        if carry is not None:
+            factors = factors + carry
+        if last:
+            factors = jnp.concatenate([factors, diag_block], axis=1)
+        gathered = lax.all_gather(factors, "col", axis=0, tiled=True)
+        if last:
+            diag_all = gathered[:, k_loc:].reshape(col_count, rows_here, TILE)
+            diag_all = diag_all[:, : diag_parts.shape[0]].reshape(col_count, 3, block_size)
+            diag_all = diag_all.astype(jnp.float32)
+            full_diag = ((diag_all[:, 0] + diag_all[:, 1]) + diag_all[:, 2]).reshape(-1)
+            gathered = gathered[:, :k_loc]
+        tiles3 = gathered.reshape(tiles_child, TILE, k_loc)
+        carry = (gathered[:1] * 0).astype(factors.dtype)
+        col_rows = jnp.take(tiles3, where_at[child], axis=0)
+        col_rows = jnp.where(present[child][:, None, None], col_rows, jnp.zeros_like(col_rows))
+        col_rows = col_rows.reshape(n_cols, k_loc)
+        pivot_rows = col_rows[tiles_block * TILE :]
+        term = jnp.einsum("nk,mk->nm", pivot_rows, col_rows, preferred_element_type=jnp.float32)
+        extra = term if extra is None else extra + term
+        if last:
+            pivot_part = extra
+            for shift in range(1, row_count):
+                pairs = [(i, (i + shift) % row_count) for i in range(row_count)]
+                pivot_part = pivot_part + lax.ppermute(extra, "row", pairs)
+            tiles3 = tiles3 + (pivot_part[:1, :1] * 0).astype(tiles3.dtype)[None]
+        grouped = jnp.take(tiles3, order[child], axis=0)
+        grouped = grouped.reshape(row_count, per_group * TILE, k_loc)
+        main = jnp.einsum("gnk,mk->gnm", grouped, col_rows, preferred_element_type=jnp.float32)
+        mine_parts.append(
+            lax.psum_scatter(
+                main.reshape(row_count * per_group * TILE, n_cols),
+                "row",
+                scatter_dimension=0,
+                tiled=True,
+            )
+        )
+    mine = jnp.stack(mine_parts)
 
     own_w = tiles_block * TILE
     lead_rows = NPAN * block_size

time: 265 us -> 323 us (1.22)
  waiting for transfers between devices: 87.5 us -> 132 us
  blocking collectives: 24.1 us -> 0 us
  other arithmetic: 68.2 us -> 92.2 us
  local copies, waits for them, and re-layouts: 43.6 us -> 52.6 us
  starting transfers between devices: 0.08 us -> 4.6 us
    ppermute x0 -> x3, waiting for transfers between devices: none -> 44 us  [shards(): pivot_part = pivot_part + lax.ppermute(extra, 'row', pairs)]
    gather x0 -> x4, local copies, waits for them, and re-layouts: none -> 27.4 us  [the longest x2 16.6 us: shards(): grouped = jnp.take(tiles3, order[child], axis=0)]
    all_gather x1 -> x0, blocking collectives: 24.1 us -> none  [shards(): full_diag = lax.all_gather(root_diag, 'col', axis=0, tiled=True)]
    gather x6 -> x2, local copies, waits for them, and re-layouts: 27.9 us -> 4.4 us  [pick_tiles(): return jnp.take_along_axis(tiles4, index[:, :, None, None], axis=1)]
    select_n x1 -> x3, other arithmetic: 2.57 us -> 18 us  [the longest x2 15.1 us: shards(): grouped = jnp.take(tiles3, order[child], axis=0)]
    all_gather x1 -> x2, waiting for transfers between devices: 74.3 us -> 87.4 us  [shards(): gathered = lax.all_gather(factors, 'col', axis=0, tiled=True)]
    reduce_scatter x1 -> x2, waiting for transfers between devices: 12.5 us -> 0.04 us  [shards(): lax.psum_scatter(main.reshape(row_count * per_group * TILE, n_cols), 'row...]
    slice x1 -> x8, local copies, waits for them, and re-layouts: 0.01 us -> 12.1 us  [the longest x1 8.27 us: shards(): gathered = gathered[:, :k_loc]]
  transfers between devices with their start and end apart: 3 -> 7, of which waited for: 2 -> 5; matrix products, arithmetic and copies ran while one was open for 34% -> 38% of each run, Pallas kernels for 0% -> 0%
where the time goes in v3:
time: 323 us; the launch traced here: 321 us
  waiting for transfers between devices  132 us (41%)
  other arithmetic  92.2 us (29%)
  local copies, waits for them, and re-layouts  52.6 us (16%)
  matrix products  24.8 us (8%)
  between operations  15.6 us (5%)
  starting transfers between devices  4.6 us (1%)
    all_gather x2, waiting for transfers between devices, shards(): gathered = lax.all_gather(factors, 'col', axis=0, tiled=True)  87.4 us
    ppermute x3, waiting for transfers between devices, shards(): pivot_part = pivot_part + lax.ppermute(extra, 'row', pairs)  44 us
    another operation x7, other arithmetic, shards(): lead = jnp.tril(jnp.linalg.cholesky(front00))  34.7 us
    another operation x3, other arithmetic, shards(): lax.linalg.triangular_solve(lead, jnp.eye(lead_rows, dtype=jnp.float32),...  19.9 us
    gather x2, local copies, waits for them, and re-layouts, shards(): grouped = jnp.take(tiles3, order[child], axis=0)  16.6 us
    dot_general x2, matrix products, shards(): jnp.einsum('gnk,mk->gnm', grouped, col_rows, preferred_element_type=jnp.f...  15.7 us
    select_n x2, other arithmetic, shards(): grouped = jnp.take(tiles3, order[child], axis=0)  15.1 us
    gather x2, local copies, waits for them, and re-layouts, shards(): col_rows = jnp.take(tiles3, where_at[child], axis=0)  10.8 us
  transfers between devices with their start and end apart: 7, of which 5 were waited for; matrix products, arithmetic and copies ran while one was open for 38% of the time, Pallas kernels for 0%

profile of v3, /device:TPU:0, one launch (start us, length us, event | category | flops | bytes accessed | tf_op | source)
XLA Modules:
  0.0 321.4 jit_solution(12916577157628009202)
XLA Ops:
  6.5 1.7 slice.121
  8.3 0.7 reduce-precision_convert_fusion.1
  9.0 56.0 %all-gather.6.cloned.1.call-done = bf16[1,2048,2048]{2,1,0:T(8,128)(2,1)} async-done(((bf16[1,64,2048]{2,1,0:T(8,128)(2,1)}), bf16[1,2048,2048]{2,1,0:T(8,128)(2,1)}) %all-gather.6.cloned.1.call-update) | async-done | bytes 8388624 | tf_op jit(solution)/shard_map/all_gather | solution.py:65
  65.0 0.8 fusion.29
  65.8 1.0 bitcast_add_fusion.1
  66.8 0.7 fusion.5
  68.4 5.4 %gather_fusion.2 = bf16[4,128,2048]{2,1,0:T(8,128)(2,1)} fusion(bf16[16,128,2048]{2,1,0:T(8,128)(2,1)} %bitcast.87, s32[1024]{0:T(1024)S(1)} %pad_clamp_fusion.3), kind=kCustom, calls=%fused_computation.clone | custom fusion | bytes 4194320 | tf_op jit(solution)/shard_map/jit(_take)/gather | solution.py:74
  73.9 8.3 %gather_fusion.4 = bf16[16,128,2048]{2,1,0:T(8,128)(2,1)} fusion(bf16[16,128,2048]{2,1,0:T(8,128)(2,1)} %bitcast.88, s32[1024]{0:T(1024)S(1)} %pad_clamp_fusion.1), kind=kCustom, calls=%fused_computation.1.clone | custom fusion | bytes 16777280 | tf_op jit(solution)/shard_map/jit(_take)/gather | solution.py:86
  82.2 7.6 %broadcast_select_fusion.1 = bf16[16,128,2048]{2,1,0:T(8,128)(2,1)} fusion(bf16[16,128,2048]{2,1,0:T(8,128)(2,1)} %gather_fusion.4, pred[16]{0:T(512)(128)(4,1)S(1)} %get-tuple-element.37), kind=kLoop, calls=%fused_computation.10 | loop fusion | flops 4194304 | bytes 16777232 | tf_op jit(solution)/shard_map/jit(_take)/select_n | solution.py:86
  89.8 31.5 %all-gather.4.cloned.1.call-done = bf16[2048,2176]{1,0:T(8,128)(2,1)} async-done(((bf16[64,2176]{1,0:T(8,128)(2,1)}), bf16[2048,2176]{1,0:T(8,128)(2,1)}) %all-gather.4.cloned.1.call-update) | async-done | bytes 8912912 | tf_op jit(solution)/shard_map/all_gather | solution.py:65
  121.3 8.3 %slice.171 = bf16[2048,2048]{1,0:T(8,128)(2,1)} slice(bf16[2048,2176]{1,0:T(8,128)(2,1)} %all-gather.4.cloned.1.call-done), slice={[0:2048], [0:2048]} | slice | bytes 16777216 | tf_op jit(solution)/shard_map/slice | solution.py:71
  129.5 5.4 %gather_fusion.3 = bf16[4,128,2048]{2,1,0:T(8,128)(2,1)} fusion(bf16[16,128,2048]{2,1,0:T(8,128)(2,1)} %bitcast.82, s32[1024]{0:T(1024)S(1)} %pad_clamp_fusion.2), kind=kCustom, calls=%fused_computation.2.clone | custom fusion | bytes 4194320 | tf_op jit(solution)/shard_map/jit(_take)/gather | solution.py:74
  134.9 2.9 select_select_fusion
  137.8 1.3 copy-done.2
  139.1 1.2 copy-done.1
  140.3 6.1 %fusion.46 = f32[2048,512]{1,0:T(8,128)} fusion(bf16[2048,2048]{1,0:T(8,128)(2,1)S(1)} %bitcast.92, bf16[512,2048]{1,0:T(8,128)(2,1)S(1)} %bitcast.94), kind=kOutput, calls=%fused_computation.150 | convolution fusion | flops 4294967296 | bytes 14680064 | tf_op jit(solution)/shard_map/gnk,mk->gnm/dot_general | solution.py:88
  146.5 1.4 slice.169
  148.4 0.7 fusion.45
  149.2 0.7 convolution_add_fusion
  149.9 2.8 collective-permute-start.2
  152.7 0.8 collective-permute-start.1
  153.5 0.9 collective-permute-start
  154.4 23.7 %collective-permute-done.2 = f32[256,512]{0,1:T(8,128)S(1)} collective-permute-done((f32[256,512]{0,1:T(8,128)S(1)}, f32[256,512]{0,1:T(8,128)S(1)}, u32[]{:S(2)}, u32[]{:S(2)}) %collective-permute-start.2) | collective-permute-done | bytes 524320 | tf_op jit(solution)/shard_map/ppermute | solution.py:84
  178.1 1.7 collective-permute-done.1
  179.9 18.6 %collective-permute-done = f32[256,512]{0,1:T(8,128)S(1)} collective-permute-done((f32[256,512]{0,1:T(8,128)S(1)}, f32[256,512]{0,1:T(8,128)S(1)}, u32[]{:S(2)}, u32[]{:S(2)}) %collective-permute-start) | collective-permute-done | bytes 524320 | tf_op jit(solution)/shard_map/ppermute | solution.py:84
  198.6 0.5 slice.182
  199.8 7.3 %broadcast_add_fusion = bf16[16,128,2048]{2,1,0:T(8,128)(2,1)} fusion(bf16[16,128,2048]{2,1,0:T(8,128)(2,1)} %bitcast.83, bf16[]{:T(256)} %bitcast.22), kind=kLoop, calls=%fused_computation.11 | loop fusion | flops 4194304 | bytes 16777218 | tf_op jit(solution)/shard_map/add | solution.py:85
  207.0 8.3 %gather_fusion.5 = bf16[16,128,2048]{2,1,0:T(8,128)(2,1)} fusion(bf16[16,128,2048]{2,1,0:T(8,128)(2,1)} %broadcast_add_fusion, s32[1024]{0:T(1024)S(1)} %pad_clamp_fusion), kind=kCustom, calls=%fused_computation.3.clone | custom fusion | bytes 16777280 | tf_op jit(solution)/shard_map/jit(_take)/gather | solution.py:86
  215.3 7.5 %broadcast_select_fusion = bf16[16,128,2048]{2,1,0:T(8,128)(2,1)} fusion(bf16[16,128,2048]{2,1,0:T(8,128)(2,1)} %gather_fusion.5, pred[16]{0:T(512)(128)(4,1)S(1)} %get-tuple-element.52), kind=kLoop, calls=%fused_computation.9 | loop fusion | flops 4194304 | bytes 16777232 | tf_op jit(solution)/shard_map/jit(_take)/select_n | solution.py:86
  222.8 9.6 %fusion.47 = f32[2048,512]{1,0:T(8,128)} fusion(bf16[2048,2048]{1,0:T(8,128)(2,1)} %bitcast.93, bf16[512,2048]{1,0:T(8,128)(2,1)S(1)} %bitcast.90), kind=kOutput, calls=%fused_computation.151 | convolution fusion | flops 4294967296 | bytes 14680064 | tf_op jit(solution)/shard_map/gnk,mk->gnm/dot_general | solution.py:88
  232.6 0.7 gather_fusion
  234.2 11.7 %cholesky.49 = f32[128,128]{1,0:T(8,128)S(1)} custom-call(f32[128,128]{1,0:T(8,128)S(1)} %cholesky.115), custom_call_target="Cholesky" | custom-call | tf_op jit(solution)/shard_map/jit(cholesky)/cholesky | solution.py:103
  246.1 9.8 %custom-call.14 = f32[1,128,128]{1,2,0:T(8,128)S(1)} custom-call(f32[1,128,128]{2,1,0:T(8,128)S(1)} %get-tuple-element.51), custom_call_target="InvertDiagBlocksLowerTriangular" | custom-call | tf_op jit(solution)/shard_map/jit(cholesky)/cholesky | solution.py:103
  256.5 11.7 %cholesky.103 = f32[128,128]{1,0:T(8,128)S(1)} custom-call(f32[128,128]{1,0:T(8,128)S(1)} %convolution_subtract_fusion.2), custom_call_target="Cholesky" | custom-call | tf_op jit(solution)/shard_map/jit(cholesky)/cholesky | solution.py:103
  268.3 0.6 compare_reduce_fusion.2
  269.0 0.7 compare_reduce_fusion.1
  271.4 4.3 %while.1 = (s32[]{:T(128)}, f32[256,256]{0,1:T(8,128)S(1)}, s32[2,2]{1,0:T(2,128)S(1)}, f32[2,128,128]{2,1,0:T(8,128)S(1)}, s32[]{:T(128)}) while((s32[]{:T(128)}, f32[256,256]{0,1:T(8,128)S(1)}, s32[2,2]{1,0:T(2,128)S(1)}, f32[2,128,128]{2,1,0:T(8,128)S(1)}, s32[]{:T(128)}) %tuple.41), condition=%wide.while_cond, body=%wide.while_body.sunk | while | flops 2 | bytes 393329 | solution.py:104
  271.4 0.6 fusion.63
  272.0 1.4 dynamic-slice.7
  273.5 0.6 fusion.63
  274.1 1.4 dynamic-slice.7
  275.7 19.9 %custom-call.15 = f32[2,128,128]{1,2,0:T(8,128)S(1)} custom-call(f32[2,128,128]{2,1,0:T(8,128)S(1)} %get-tuple-element.14), custom_call_target="InvertDiagBlocksLowerTriangular" | custom-call | tf_op jit(solution)/shard_map/triangular_solve | solution.py:104
  296.5 0.4 fusion.6
  297.0 1.8 pad_maximum_fusion
  298.8 4.3 %gather_fusion.1 = f32[32,128,512]{2,1,0:T(8,128)} fusion(f32[2,4,128,512]{3,2,1,0:T(8,128)S(1)} %pad_maximum_fusion, s32[32]{0:T(128)S(1)} %reshape.268), kind=kCustom, calls=%fused_computation.5 | custom fusion | bytes 16777472 | tf_op jit(solution)/shard_map/jit(take_along_axis)/gather | solution.py:11
  303.1 5.9 %select_reduce_fusion = f32[16,128,512]{2,1,0:T(8,128)S(1)} fusion(f32[2,16,128,512]{3,2,1,0:T(8,128)} %bitcast.84, pred[2,16]{1,0:T(4,128)(4,1)S(1)} %compare_and_fusion.4, pred[2,16]{1,0:T(4,128)(4,1)S(1)} %fusion.31), kind=kLoop, calls=%fused_computation.8 | loop fusion | flops 5242880 | bytes 12582976 | tf_op jit(solution)/shard_map/reduce_sum | solution.py:119
  309.1 2.0 bitcast_select_fusion
  311.1 3.8 %fusion.1 = f32[2048,256]{1,0:T(8,128)} fusion(f32[2048,256]{1,0:T(8,128)S(1)} %get-tuple-element.61, f32[2048,256]{1,0:T(8,128)S(1)} %get-tuple-element.62, f32[256,256]{1,0:T(8,128)S(1)} %fusion.6, f32[2048,512]{1,0:T(8,128)S(1)} %bitcast.86, f32[256]{0:T(256)S(1)} %copy-done.4, s32[256]{0:T(256)S(1)} %iota_add_fusion, s32[2048]{0:T(1024)S(1)} %fusion.25, ...), kind=kOutput, calls=%fused_computation.14 | convolution fusion | flops 1613758464 | bytes 8663041 | tf_op jit(solution)/shard_map/dot_general | solution.py:131
  (87 shorter events, 4.9 us)
Async XLA Ops:
  6.5 61.1 %copy-start = (s32[2,16]{1,0:T(2,128)S(1)}, s32[2,16]{1,0:T(2,128)}, u32[]{:S(2)}) copy-start(s32[2,16]{1,0:T(2,128)} %param.8) | copy-start | bytes 388
  6.5 58.5 %all-gather.6.cloned.1.call-start = ((), (), s32[]{:S(2)}) async-start(), calls=%async_computation.5 | async-start | bytes 8650752 | tf_op jit(solution)/shard_map/all_gather | solution.py:65
  8.2 113.0 %all-gather.4.cloned.1.call-start = ((), (), s32[]{:S(2)}) async-start(), calls=%async_computation.2 | async-start | bytes 9191424 | tf_op jit(solution)/shard_map/all_gather | solution.py:65
  67.5 229.4 %reduce-scatter.3.cloned.1.call-start = ((), (), s32[]{:S(2)}) async-start(), calls=%async_computation.3 | async-start | bytes 5242880 | tf_op jit(solution)/shard_map/reduce_scatter | solution.py:90
  134.9 5.4 %copy-start.1 = (bf16[16,128,2048]{2,1,0:T(8,128)(2,1)S(1)}, bf16[16,128,2048]{2,1,0:T(8,128)(2,1)}, u32[]{:S(2)}) copy-start(bf16[16,128,2048]{2,1,0:T(8,128)(2,1)} %broadcast_select_fusion.1) | copy-start | bytes 25165828
  137.8 1.3 copy-start.2
  146.5 150.5 %reduce-scatter.5.cloned.1.call-start = ((), (), s32[]{:S(2)}) async-start(), calls=%async_computation.4 | async-start | bytes 5242880 | tf_op jit(solution)/shard_map/reduce_scatter | solution.py:90
  146.5 1.9 copy-start.3
  149.9 28.2 %collective-permute-start.2 = (f32[256,512]{0,1:T(8,128)S(1)}, f32[256,512]{0,1:T(8,128)S(1)}, u32[]{:S(2)}, u32[]{:S(2)}) collective-permute-start(f32[256,512]{0,1:T(8,128)S(1)} %convolution_add_fusion), channel_id=1, source_target_pairs={{0,96},{32,0},{64,32},{96,64},{1,97},{33,1},{65,33},{97,65},{2,98}... | collective-permute-start | bytes 1572872 | tf_op jit(solution)/shard_map/ppermute | solution.py:84
  152.7 27.2 %collective-permute-start.1 = (f32[256,512]{0,1:T(8,128)S(1)}, f32[256,512]{0,1:T(8,128)S(1)}, u32[]{:S(2)}, u32[]{:S(2)}) collective-permute-start(f32[256,512]{0,1:T(8,128)S(1)} %convolution_add_fusion), channel_id=1, source_target_pairs={{0,64},{32,96},{64,0},{96,32},{1,65},{33,97},{65,1},{97,33},{2,66}... | collective-permute-start | bytes 1572872 | tf_op jit(solution)/shard_map/ppermute | solution.py:84
  153.5 44.9 %collective-permute-start = (f32[256,512]{0,1:T(8,128)S(1)}, f32[256,512]{0,1:T(8,128)S(1)}, u32[]{:S(2)}, u32[]{:S(2)}) collective-permute-start(f32[256,512]{0,1:T(8,128)S(1)} %convolution_add_fusion), channel_id=1, source_target_pairs={{0,32},{32,64},{64,96},{96,0},{1,33},{33,65},{65,97},{97,1},{2,34}... | collective-permute-start | bytes 1572872 | tf_op jit(solution)/shard_map/ppermute | solution.py:84
  232.4 1.4 slice-start
  309.1 2.0 copy-start.4
Sparse Core Ops, SparseCore 0:
  9.6 55.3 all-gather.5
  67.6 53.5 all-gather.3
  146.6 67.7 reduce-scatter.2
  232.5 45.8 reduce-scatter.4

commit v4 on v2

--- a/solution.py
+++ b/solution.py
@@ -30,6 +30,7 @@
     k_loc = gathered.shape[2]
     tiles4 = gathered.reshape(n_child, tiles_child, TILE, k_loc)
     full_diag = lax.all_gather(root_diag, "col", axis=0, tiled=True)
+    diag_edge = (full_diag[0] * 0).astype(jnp.int32)
 
     owner = (child_tiles * TILE // block_size) % row_count
     position = jnp.arange(tiles_child, dtype=jnp.int32)
@@ -46,6 +47,7 @@
     wanted = jnp.concatenate([own_tiles, pivot_tiles])
     match = child_tiles[:, :, None] == wanted[None, None, :]
     where_at = jnp.sum(jnp.where(match, position[None, :, None], 0), axis=1).astype(jnp.int32)
+    where_at = where_at + diag_edge
     present = jnp.any(match, axis=1)
     col_rows = pick_tiles(tiles4, where_at)
     col_rows = jnp.where(present[:, :, None, None], col_rows, jnp.zeros_like(col_rows))
@@ -56,12 +58,17 @@
     extra = jnp.einsum(
         "cnk,cmk->nm", pivot_rows, col_rows, preferred_element_type=jnp.float32
     )
-    pivot_part = lax.psum(extra, "row")
+    pivot_part = extra
+    for shift in range(1, row_count):
+        pairs = [(i, (i + shift) % row_count) for i in range(row_count)]
+        pivot_part = pivot_part + lax.ppermute(extra, "row", pairs)
+    grouped = grouped + (extra[:1, :1] * 0).astype(grouped.dtype)[None, None]
 
     grouped = grouped.reshape(n_child, row_count, per_group * TILE, k_loc)
     main = jnp.einsum(
         "cgnk,cmk->gcnm", grouped, col_rows, preferred_element_type=jnp.float32
     )
+    main = main + (pivot_part[:1, :1] * 0)[None, None]
     mine = lax.psum_scatter(
         main.reshape(row_count * n_child * per_group * TILE, n_cols),
         "row",

time: 265 us -> 256 us (0.966)
  waiting for transfers between devices: 87.5 us -> 72.3 us
  starting transfers between devices: 0.08 us -> 4.44 us
    all_gather x1, waiting for transfers between devices: 74.3 us -> 47.6 us  [shards(): gathered = lax.all_gather(child_factors, 'col', axis=1, tiled=True)]
    ppermute x0 -> x3, waiting for transfers between devices: none -> 10.3 us  [shards(): pivot_part = pivot_part + lax.ppermute(extra, 'row', pairs)]
    transpose x1 -> x0, local copies, waits for them, and re-layouts: 7.58 us -> none  [shards(): jnp.einsum('cgnk,cmk->gcnm', grouped, col_rows, preferred_element_type=jn...]
    add x0 -> x1, local copies, waits for them, and re-layouts: none -> 7.58 us  [shards(): main = main + (pivot_part[:1, :1] * 0)[None, None]]
    ppermute x0 -> x3, starting transfers between devices: none -> 4.4 us  [shards(): pivot_part = pivot_part + lax.ppermute(extra, 'row', pairs)]
  transfers between devices with their start and end apart: 3 -> 5, of which waited for: 2 -> 4; matrix products, arithmetic and copies ran while one was open for 34% -> 31% of each run, Pallas kernels for 0% -> 0%
where the time goes in v4:
time: 256 us; the launch traced here: 255 us
  waiting for transfers between devices  72.3 us (28%)
  other arithmetic  66.6 us (26%)
  local copies, waits for them, and re-layouts  43.8 us (17%)
  blocking collectives  25.9 us (10%)
  matrix products  24.6 us (10%)
  between operations  16.9 us (7%)
  starting transfers between devices  4.44 us (2%)
    all_gather x1, waiting for transfers between devices, shards(): gathered = lax.all_gather(child_factors, 'col', axis=1, tiled=True)  47.6 us
    another operation x7, other arithmetic, shards(): lead = jnp.tril(jnp.linalg.cholesky(front00))  34.6 us
    gather x6, local copies, waits for them, and re-layouts, pick_tiles(): return jnp.take_along_axis(tiles4, index[:, :, None, None], axis=1)  27.8 us
    all_gather x1, blocking collectives, shards(): full_diag = lax.all_gather(root_diag, 'col', axis=0, tiled=True)  25.9 us
    another operation x3, other arithmetic, shards(): lax.linalg.triangular_solve(lead, jnp.eye(lead_rows, dtype=jnp.float32),...  19.9 us
    dot_general x1, matrix products, shards(): jnp.einsum('cgnk,cmk->gcnm', grouped, col_rows, preferred_element_type=jn...  15.7 us
    reduce_scatter x1, waiting for transfers between devices, shards(): lax.psum_scatter(main.reshape(row_count * n_child * per_group * TILE, n_c...  13.7 us
    ppermute x3, waiting for transfers between devices, shards(): pivot_part = pivot_part + lax.ppermute(extra, 'row', pairs)  10.3 us
  transfers between devices with their start and end apart: 5, of which 4 were waited for; matrix products, arithmetic and copies ran while one was open for 31% of the time, Pallas kernels for 0%

profile of v4, /device:TPU:0, one launch (start us, length us, event | category | flops | bytes accessed | tf_op | source)
XLA Modules:
  0.0 254.5 jit_solution(12506935510409732141)
XLA Ops:
  6.5 0.7 all-gather.3.cloned.1.call-update
  7.3 25.9 %all-gather = f32[32,1,256]{2,1,0:T(1,128)S(1)} all-gather(f32[1,1,256]{2,1,0:T(1,128)} %bitcast.103), channel_id=1, replica_groups=mesh['row'=4,'col'=32] {'col'}, dimensions={0}, use_global_device_ids=true | all-gather | bytes 33792 | tf_op jit(solution)/shard_map/all_gather | solution.py:32
  33.2 0.5 slice.99
  34.4 0.9 fusion.40
  35.4 0.9 compare_reduce_fusion
  36.3 0.7 fusion.44
  37.0 0.2 convert_reduce_fusion
  37.3 47.6 %all-gather.3.cloned.1.call-done = bf16[2,2048,2048]{2,1,0:T(8,128)(2,1)} async-done(((bf16[2,64,2048]{2,1,0:T(8,128)(2,1)}), bf16[2,2048,2048]{2,1,0:T(8,128)(2,1)}) %all-gather.3.cloned.1.call-update) | async-done | bytes 16777232 | tf_op jit(solution)/shard_map/all_gather | solution.py:29
  84.9 8.5 %gather_fusion = bf16[8,128,2048]{2,1,0:T(8,128)(2,1)} fusion(bf16[2,16,128,2048]{3,2,1,0:T(8,128)(2,1)} %bitcast.94, s32[8]{0:T(128)S(1)} %reshape.246), kind=kCustom, calls=%fused_computation | custom fusion | bytes 8388672 | tf_op jit(solution)/shard_map/jit(take_along_axis)/gather | solution.py:11
  93.4 2.6 %fusion.7 = bf16[2,512,2048]{2,1,0:T(8,128)(2,1)S(1)} fusion(pred[2,512]{1,0:T(4,128)(4,1)S(1)} %get-tuple-element.45, pred[2,512]{1,0:T(4,128)(4,1)S(1)} %get-tuple-element.46, bf16[2,512,2048]{2,1,0:T(8,128)(2,1)} %bitcast.99), kind=kLoop, calls=%fused_computation.16 | loop fusion | flops 4194304 | bytes 8390656 | tf_op jit(solution)/shard_map/jit(_where)/select_n | solution.py:53
  96.0 1.3 fusion.14
  97.3 0.7 copy-done.1
  98.1 2.7 %collective-permute-start.2 = (f32[256,512]{0,1:T(8,128)S(1)}, f32[256,512]{0,1:T(8,128)S(1)}, u32[]{:S(2)}, u32[]{:S(2)}) collective-permute-start(f32[256,512]{0,1:T(8,128)S(1)} %fusion.14), channel_id=1, source_target_pairs={{0,96},{32,0},{64,32},{96,64},{1,97},{33,1},{65,33},{97,65},{2,98}... | collective-permute-start | bytes 1572872 | tf_op jit(solution)/shard_map/ppermute | solution.py:64
  100.7 0.8 collective-permute-start.1
  101.6 0.9 collective-permute-start
  102.7 0.5 slice.103
  103.3 13.1 %gather_fusion.2 = bf16[32,128,2048]{2,1,0:T(8,128)(2,1)} fusion(bf16[2,16,128,2048]{3,2,1,0:T(8,128)(2,1)} %bitcast.95, s32[32]{0:T(128)S(1)} %reshape.258), kind=kCustom, calls=%fused_computation.2 | custom fusion | bytes 33554688 | tf_op jit(solution)/shard_map/jit(take_along_axis)/gather | solution.py:11
  117.0 6.6 %collective-permute-done.2 = f32[256,512]{0,1:T(8,128)S(1)} collective-permute-done((f32[256,512]{0,1:T(8,128)S(1)}, f32[256,512]{0,1:T(8,128)S(1)}, u32[]{:S(2)}, u32[]{:S(2)}) %collective-permute-start.2) | collective-permute-done | bytes 524320 | tf_op jit(solution)/shard_map/ppermute | solution.py:64
  123.6 3.7 %collective-permute-done = f32[256,512]{0,1:T(8,128)S(1)} collective-permute-done((f32[256,512]{0,1:T(8,128)S(1)}, f32[256,512]{0,1:T(8,128)S(1)}, u32[]{:S(2)}, u32[]{:S(2)}) %collective-permute-start) | collective-permute-done | bytes 524320 | tf_op jit(solution)/shard_map/ppermute | solution.py:64
  127.3 0.1 add_add_fusion
  127.4 0.5 slice.104
  128.6 15.7 %add_bitcast_fusion = f32[4,2,512,512]{3,2,0,1:T(8,128)} fusion(f32[]{:T(128)} %bitcast.23, bf16[2,4,512,2048]{3,2,1,0:T(8,128)(2,1)} %bitcast.98, pred[2,4,512]{2,1,0:T(4,128)(4,1)S(1)} %broadcast_in_dim.187, bf16[]{:T(256)} %bitcast.22, bf16[2,512,2048]{2,1,0:T(8,128)(2,1)} %copy-done.1), kind=kOutput, calls=%fused_computation.11 | convolution fusion | flops 8633974784 | bytes 29364230 | tf_op jit(solution)/shard_map/cgnk,cmk->gcnm/dot_general | solution.py:68
  144.3 7.6 %copy.50 = f32[4,2,512,512]{3,2,1,0:T(8,128)} copy(f32[4,2,512,512]{3,2,0,1:T(8,128)} %add_bitcast_fusion) | data formatting | bytes 16777216 | tf_op jit(solution)/shard_map/add | solution.py:71
  152.1 0.4 copy-done
  152.6 0.7 gather_fusion.1
  153.8 0.1 copy.44
  154.0 11.7 %cholesky.49 = f32[128,128]{1,0:T(8,128)S(1)} custom-call(f32[128,128]{1,0:T(8,128)S(1)} %cholesky.115), custom_call_target="Cholesky" | custom-call | tf_op jit(solution)/shard_map/jit(cholesky)/cholesky | solution.py:83
  165.9 9.8 %custom-call.14 = f32[1,128,128]{1,2,0:T(8,128)S(1)} custom-call(f32[1,128,128]{2,1,0:T(8,128)S(1)} %get-tuple-element.42), custom_call_target="InvertDiagBlocksLowerTriangular" | custom-call | tf_op jit(solution)/shard_map/jit(cholesky)/cholesky | solution.py:83
  175.7 0.2 fusion.25
  176.0 0.3 convolution_subtract_fusion.2
  176.3 11.7 %cholesky.103 = f32[128,128]{1,0:T(8,128)S(1)} custom-call(f32[128,128]{1,0:T(8,128)S(1)} %convolution_subtract_fusion.2), custom_call_target="Cholesky" | custom-call | tf_op jit(solution)/shard_map/jit(cholesky)/cholesky | solution.py:83
  188.1 0.6 compare_reduce_fusion.2
  188.8 0.6 compare_reduce_fusion.1
  190.9 4.0 %while.1 = (s32[]{:T(128)}, f32[256,256]{0,1:T(8,128)S(1)}, s32[2,2]{1,0:T(2,128)S(1)}, f32[2,128,128]{2,1,0:T(8,128)S(1)}, s32[]{:T(128)}) while((s32[]{:T(128)}, f32[256,256]{0,1:T(8,128)S(1)}, s32[2,2]{1,0:T(2,128)S(1)}, f32[2,128,128]{2,1,0:T(8,128)S(1)}, s32[]{:T(128)}) %tuple.27), condition=%wide.while_cond, body=%wide.while_body.sunk | while | flops 2 | bytes 393329 | solution.py:84
  190.9 0.6 fusion.72
  191.5 1.3 dynamic-slice.7
  192.9 0.6 fusion.72
  193.5 1.3 dynamic-slice.7
  194.9 19.9 %custom-call.15 = f32[2,128,128]{1,2,0:T(8,128)S(1)} custom-call(f32[2,128,128]{2,1,0:T(8,128)S(1)} %get-tuple-element.12), custom_call_target="InvertDiagBlocksLowerTriangular" | custom-call | tf_op jit(solution)/shard_map/triangular_solve | solution.py:84
  214.8 0.3 fusion.20
  215.1 0.3 convolution_subtract_fusion.1
  215.4 0.3 fusion.23
  215.7 0.4 fusion.17
  216.2 13.7 %reduce-scatter.2.cloned.1.call-done = f32[1024,512]{1,0:T(8,128)} async-done(((f32[4096,512]{1,0:T(8,128)}), f32[1024,512]{1,0:T(8,128)}) %reduce-scatter.2.cloned.1.call-update) | async-done | bytes 2097168 | tf_op jit(solution)/shard_map/reduce_scatter | solution.py:72
  229.9 5.9 %gather_fusion.3 = f32[32,128,512]{2,1,0:T(8,128)} fusion(f32[2,4,128,512]{3,2,1,0:T(8,128)} %bitcast.92, s32[32]{0:T(128)S(1)} %reshape.264), kind=kCustom, calls=%fused_computation.3 | custom fusion | bytes 16777472 | tf_op jit(solution)/shard_map/jit(take_along_axis)/gather | solution.py:11
  235.8 6.1 %select_reduce_fusion = f32[16,128,512]{2,1,0:T(8,128)S(1)} fusion(f32[2,16,128,512]{3,2,1,0:T(8,128)} %bitcast.91, pred[2,16]{1,0:T(4,128)(4,1)S(1)} %compare_and_fusion.1, pred[2,16]{1,0:T(4,128)(4,1)S(1)} %fusion.41), kind=kLoop, calls=%fused_computation.10 | loop fusion | flops 5242880 | bytes 12582976 | tf_op jit(solution)/shard_map/reduce_sum | solution.py:99
  241.9 1.9 bitcast_select_fusion.1
  243.8 3.9 %fusion.9 = f32[2048,256]{1,0:T(8,128)} fusion(f32[2048,256]{1,0:T(8,128)S(1)} %get-tuple-element.43, f32[2048,256]{1,0:T(8,128)S(1)} %get-tuple-element.44, f32[256,256]{1,0:T(8,128)S(1)} %fusion.17, f32[2048,512]{1,0:T(8,128)S(1)} %bitcast.97, f32[256]{0:T(256)S(1)} %copy-done.2, s32[256]{0:T(256)S(1)} %iota_add_fusion, s32[2048]{0:T(1024)S(1)} %fusion.36, ...), kind=kOutput, calls=%fused_computation.19 | convolution fusion | flops 1613758464 | bytes 8663041 | tf_op jit(solution)/shard_map/dot_general | solution.py:111
  (59 shorter events, 2.3 us)
Async XLA Ops:
  6.5 78.4 %all-gather.3.cloned.1.call-start = ((), (), s32[]{:S(2)}) async-start(), calls=%async_computation.1 | async-start | bytes 17301504 | tf_op jit(solution)/shard_map/all_gather | solution.py:29
  7.3 222.6 %reduce-scatter.2.cloned.1.call-start = ((), (), s32[]{:S(2)}) async-start(), calls=%async_computation.2 | async-start | bytes 10485760 | tf_op jit(solution)/shard_map/reduce_scatter | solution.py:72
  96.0 2.0 copy-start.1
  98.1 25.6 %collective-permute-start.2 = (f32[256,512]{0,1:T(8,128)S(1)}, f32[256,512]{0,1:T(8,128)S(1)}, u32[]{:S(2)}, u32[]{:S(2)}) collective-permute-start(f32[256,512]{0,1:T(8,128)S(1)} %fusion.14), channel_id=1, source_target_pairs={{0,96},{32,0},{64,32},{96,64},{1,97},{33,1},{65,33},{97,65},{2,98}... | collective-permute-start | bytes 1572872 | tf_op jit(solution)/shard_map/ppermute | solution.py:64
  100.7 22.9 %collective-permute-start.1 = (f32[256,512]{0,1:T(8,128)S(1)}, f32[256,512]{0,1:T(8,128)S(1)}, u32[]{:S(2)}, u32[]{:S(2)}) collective-permute-start(f32[256,512]{0,1:T(8,128)S(1)} %fusion.14), channel_id=1, source_target_pairs={{0,64},{32,96},{64,0},{96,32},{1,65},{33,97},{65,1},{97,33},{2,66}... | collective-permute-start | bytes 1572872 | tf_op jit(solution)/shard_map/ppermute | solution.py:64
  101.6 25.7 %collective-permute-start = (f32[256,512]{0,1:T(8,128)S(1)}, f32[256,512]{0,1:T(8,128)S(1)}, u32[]{:S(2)}, u32[]{:S(2)}) collective-permute-start(f32[256,512]{0,1:T(8,128)S(1)} %fusion.14), channel_id=1, source_target_pairs={{0,32},{32,64},{64,96},{96,0},{1,33},{33,65},{65,97},{97,1},{2,34}... | collective-permute-start | bytes 1572872 | tf_op jit(solution)/shard_map/ppermute | solution.py:64
  151.9 0.7 copy-start
  241.9 1.9 copy-start.2
Sparse Core Ops, SparseCore 0:
  9.6 75.2 all-gather.2
  152.1 77.7 reduce-scatter.1

commit v5 on v4

--- a/solution.py
+++ b/solution.py
@@ -40,7 +40,6 @@
         jnp.where(rank[:, :, None] == position[None, None, :], position[None, :, None], 0),
         axis=1,
     ).astype(jnp.int32)
-    grouped = pick_tiles(tiles4, order)
 
     own_tiles = col_index * tiles_block + jnp.arange(tiles_block, dtype=jnp.int32)
     pivot_tiles = jnp.arange(NPAN * tiles_block, dtype=jnp.int32)
@@ -62,13 +61,16 @@
     for shift in range(1, row_count):
         pairs = [(i, (i + shift) % row_count) for i in range(row_count)]
         pivot_part = pivot_part + lax.ppermute(extra, "row", pairs)
-    grouped = grouped + (extra[:1, :1] * 0).astype(grouped.dtype)[None, None]
-
-    grouped = grouped.reshape(n_child, row_count, per_group * TILE, k_loc)
+    main_rows = col_rows + (extra[:1, :1] * 0).astype(col_rows.dtype)[None]
     main = jnp.einsum(
-        "cgnk,cmk->gcnm", grouped, col_rows, preferred_element_type=jnp.float32
+        "cuk,cmk->cum", gathered, main_rows, preferred_element_type=jnp.float32
     )
-    main = main + (pivot_part[:1, :1] * 0)[None, None]
+    main = main.reshape(n_child * tiles_child, TILE, n_cols)
+    child_base = (jnp.arange(n_child, dtype=jnp.int32) * tiles_child)[:, None]
+    flat_order = (order + child_base).reshape(n_child, row_count, per_group)
+    flat_order = jnp.transpose(flat_order, (1, 0, 2)).reshape(-1)
+    flat_order = flat_order + (pivot_part[0, 0] * 0).astype(jnp.int32)
+    main = jnp.take(main, flat_order, axis=0)
     mine = lax.psum_scatter(
         main.reshape(row_count * n_child * per_group * TILE, n_cols),
         "row",

time: 256 us -> 248 us (0.969)
  waiting for transfers between devices: 72.3 us -> 61.6 us
  other arithmetic: 66.6 us -> 72.5 us
  local copies, waits for them, and re-layouts: 43.8 us -> 39.5 us
    gather x6 -> x4, local copies, waits for them, and re-layouts: 27.8 us -> 14.6 us  [pick_tiles(): return jnp.take_along_axis(tiles4, index[:, :, None, None], axis=1)]
    ppermute x3, waiting for transfers between devices: 10.3 us -> 0.01 us  [shards(): pivot_part = pivot_part + lax.ppermute(extra, 'row', pairs)]
    dot_general x0 -> x1, local copies, waits for them, and re-layouts: none -> 8.67 us  [shards(): jnp.einsum('cuk,cmk->cum', gathered, main_rows, preferred_element_type=jn...]
    gather x0 -> x1, local copies, waits for them, and re-layouts: none -> 7.68 us  [shards(): main = jnp.take(main, flat_order, axis=0)]
    add x1 -> x3, local copies, waits for them, and re-layouts: 7.58 us -> 0.18 us  [shards(): flat_order = flat_order + (pivot_part[0, 0] * 0).astype(jnp.int32)]
    select_n x0 -> x2, other arithmetic: none -> 5.82 us  [shards(): main = jnp.take(main, flat_order, axis=0)]
  transfers between devices with their start and end apart: 5 -> 5, of which waited for: 4 -> 2; matrix products, arithmetic and copies ran while one was open for 31% -> 37% of each run, Pallas kernels for 0% -> 0%
where the time goes in v5:
time: 248 us; the launch traced here: 247 us
  other arithmetic  72.5 us (29%)
  waiting for transfers between devices  61.6 us (25%)
  local copies, waits for them, and re-layouts  39.5 us (16%)
  blocking collectives  25.9 us (10%)
  matrix products  24.5 us (10%)
  between operations  16.9 us (7%)
  starting transfers between devices  5.65 us (2%)
    all_gather x1, waiting for transfers between devices, shards(): gathered = lax.all_gather(child_factors, 'col', axis=1, tiled=True)  47.4 us
    another operation x7, other arithmetic, shards(): lead = jnp.tril(jnp.linalg.cholesky(front00))  34.6 us
    all_gather x1, blocking collectives, shards(): full_diag = lax.all_gather(root_diag, 'col', axis=0, tiled=True)  25.9 us
    another operation x3, other arithmetic, shards(): lax.linalg.triangular_solve(lead, jnp.eye(lead_rows, dtype=jnp.float32),...  19.9 us
    dot_general x1, matrix products, shards(): jnp.einsum('cuk,cmk->cum', gathered, main_rows, preferred_element_type=jn...  15.7 us
    gather x4, local copies, waits for them, and re-layouts, pick_tiles(): return jnp.take_along_axis(tiles4, index[:, :, None, None], axis=1)  14.6 us
    reduce_scatter x1, waiting for transfers between devices, shards(): lax.psum_scatter(main.reshape(row_count * n_child * per_group * TILE, n_c...  13.5 us
    dot_general x1, local copies, waits for them, and re-layouts, shards(): jnp.einsum('cuk,cmk->cum', gathered, main_rows, preferred_element_type=jn...  8.67 us
  transfers between devices with their start and end apart: 5, of which 2 were waited for; matrix products, arithmetic and copies ran while one was open for 37% of the time, Pallas kernels for 0%

profile of v5, /device:TPU:0, one launch (start us, length us, event | category | flops | bytes accessed | tf_op | source)
XLA Modules:
  0.0 246.7 jit_solution(17345989594832469171)
XLA Ops:
  6.5 0.7 all-gather.3.cloned.1.call-update
  7.3 25.9 %all-gather = f32[32,1,256]{2,1,0:T(1,128)S(1)} all-gather(f32[1,1,256]{2,1,0:T(1,128)} %bitcast.98), channel_id=1, replica_groups=mesh['row'=4,'col'=32] {'col'}, dimensions={0}, use_global_device_ids=true | all-gather | bytes 33792 | tf_op jit(solution)/shard_map/all_gather | solution.py:32
  33.2 0.5 slice.99
  34.4 0.9 fusion.35
  35.4 0.7 fusion.39
  36.1 0.2 convert_reduce_fusion
  36.5 0.9 compare_reduce_fusion
  37.5 47.4 %all-gather.3.cloned.1.call-done = bf16[2,2048,2048]{2,1,0:T(8,128)(2,1)} async-done(((bf16[2,64,2048]{2,1,0:T(8,128)(2,1)}), bf16[2,2048,2048]{2,1,0:T(8,128)(2,1)}) %all-gather.3.cloned.1.call-update) | async-done | bytes 16777232 | tf_op jit(solution)/shard_map/all_gather | solution.py:29
  84.9 8.5 %gather_fusion.1 = bf16[8,128,2048]{2,1,0:T(8,128)(2,1)} fusion(bf16[2,16,128,2048]{3,2,1,0:T(8,128)(2,1)} %bitcast.94, s32[8]{0:T(128)S(1)} %reshape.271), kind=kCustom, calls=%fused_computation.1 | custom fusion | bytes 8388672 | tf_op jit(solution)/shard_map/jit(take_along_axis)/gather | solution.py:11
  93.4 2.6 %fusion = bf16[2,512,2048]{2,1,0:T(8,128)(2,1)S(1)} fusion(pred[2,512]{1,0:T(4,128)(4,1)S(1)} %get-tuple-element.45, pred[2,512]{1,0:T(4,128)(4,1)S(1)} %get-tuple-element.46, bf16[2,512,2048]{2,1,0:T(8,128)(2,1)} %bitcast.93), kind=kLoop, calls=%fused_computation.10 | loop fusion | flops 4194304 | bytes 8390656 | tf_op jit(solution)/shard_map/jit(_where)/select_n | solution.py:52
  96.0 1.3 fusion.9
  97.3 0.7 copy-done.1
  98.0 1.5 collective-permute-start
  99.5 2.7 %collective-permute-start.1 = (f32[256,512]{0,1:T(8,128)S(1)}, f32[256,512]{0,1:T(8,128)S(1)}, u32[]{:S(2)}, u32[]{:S(2)}) collective-permute-start(f32[256,512]{0,1:T(8,128)S(1)} %fusion.9), channel_id=1, source_target_pairs={{0,64},{32,96},{64,0},{96,32},{1,65},{33,97},{65,1},{97,33},{2,66}... | collective-permute-start | bytes 1572872 | tf_op jit(solution)/shard_map/ppermute | solution.py:63
  102.1 1.5 collective-permute-start.2
  103.6 0.5 slice.104
  104.8 15.7 %convolution_bitcast_fusion = f32[2,2048,512]{1,2,0:T(8,128)} fusion(bf16[2,2048,2048]{2,1,0:T(8,128)(2,1)} %all-gather.3.cloned.1.call-done, bf16[2,512,2048]{2,1,0:T(8,128)(2,1)} %copy-done.1, bf16[]{:T(256)} %bitcast.21), kind=kOutput, calls=%fused_computation.8 | convolution fusion | flops 8592031744 | bytes 29360130 | tf_op jit(solution)/shard_map/cuk,cmk->cum/dot_general | solution.py:65
  120.5 8.7 %copy.57 = f32[2,2048,512]{2,1,0:T(8,128)} copy(f32[2,2048,512]{1,2,0:T(8,128)} %convolution_bitcast_fusion) | data formatting | bytes 16777216 | tf_op jit(solution)/shard_map/cuk,cmk->cum/dot_general | solution.py:65
  129.1 0.1 add_add_fusion
  129.3 0.5 slice.103
  130.8 7.7 %gather_fusion = f32[32,128,512]{2,1,0:T(8,128)} fusion(f32[32,128,512]{2,1,0:T(8,128)} %bitcast.90, s32[1024]{0:T(1024)S(1)} %pad_clamp_fusion), kind=kCustom, calls=%fused_computation | custom fusion | bytes 16777344 | tf_op jit(solution)/shard_map/jit(_take)/gather | solution.py:73
  138.5 5.8 %bitcast_select_fusion = f32[4096,512]{1,0:T(8,128)} fusion(f32[32,128,512]{2,1,0:T(8,128)} %gather_fusion, pred[4096]{0:T(1024)(128)(4,1)S(1)} %broadcast_bitcast_fusion), kind=kLoop, calls=%fused_computation.6 | loop fusion | flops 2097152 | bytes 16781312 | tf_op jit(solution)/shard_map/jit(_take)/select_n | solution.py:73
  144.5 0.5 copy-done
  145.0 0.7 gather_fusion.2
  146.2 0.1 copy.50
  146.4 11.7 %cholesky.49 = f32[128,128]{1,0:T(8,128)S(1)} custom-call(f32[128,128]{1,0:T(8,128)S(1)} %cholesky.115), custom_call_target="Cholesky" | custom-call | tf_op jit(solution)/shard_map/jit(cholesky)/cholesky | solution.py:85
  158.3 9.8 %custom-call.14 = f32[1,128,128]{1,2,0:T(8,128)S(1)} custom-call(f32[1,128,128]{2,1,0:T(8,128)S(1)} %get-tuple-element.42), custom_call_target="InvertDiagBlocksLowerTriangular" | custom-call | tf_op jit(solution)/shard_map/jit(cholesky)/cholesky | solution.py:85
  168.1 0.2 fusion.20
  168.4 0.3 convolution_subtract_fusion.2
  168.7 11.7 %cholesky.103 = f32[128,128]{1,0:T(8,128)S(1)} custom-call(f32[128,128]{1,0:T(8,128)S(1)} %convolution_subtract_fusion.2), custom_call_target="Cholesky" | custom-call | tf_op jit(solution)/shard_map/jit(cholesky)/cholesky | solution.py:85
  180.5 0.6 compare_reduce_fusion.1
  181.1 0.6 compare_reduce_fusion.2
  183.1 4.0 %while.1 = (s32[]{:T(128)}, f32[256,256]{0,1:T(8,128)S(1)}, s32[2,2]{1,0:T(2,128)S(1)}, f32[2,128,128]{2,1,0:T(8,128)S(1)}, s32[]{:T(128)}) while((s32[]{:T(128)}, f32[256,256]{0,1:T(8,128)S(1)}, s32[2,2]{1,0:T(2,128)S(1)}, f32[2,128,128]{2,1,0:T(8,128)S(1)}, s32[]{:T(128)}) %tuple.27), condition=%wide.while_cond, body=%wide.while_body.sunk | while | flops 2 | bytes 393321 | solution.py:86
  183.2 0.6 fusion.61
  183.7 1.3 dynamic-slice.7
  185.2 0.6 fusion.61
  185.8 1.3 dynamic-slice.7
  187.2 19.9 %custom-call.15 = f32[2,128,128]{1,2,0:T(8,128)S(1)} custom-call(f32[2,128,128]{2,1,0:T(8,128)S(1)} %get-tuple-element.12), custom_call_target="InvertDiagBlocksLowerTriangular" | custom-call | tf_op jit(solution)/shard_map/triangular_solve | solution.py:86
  207.1 0.1 copy.54
  207.2 0.3 fusion.15
  207.5 0.3 convolution_subtract_fusion.1
  207.8 0.3 fusion.18
  208.1 0.4 fusion.12
  208.6 13.5 %reduce-scatter.2.cloned.1.call-done = f32[1024,512]{1,0:T(8,128)} async-done(((f32[4096,512]{1,0:T(8,128)}), f32[1024,512]{1,0:T(8,128)}) %reduce-scatter.2.cloned.1.call-update) | async-done | bytes 2097168 | tf_op jit(solution)/shard_map/reduce_scatter | solution.py:74
  222.1 5.9 %gather_fusion.3 = f32[32,128,512]{2,1,0:T(8,128)} fusion(f32[2,4,128,512]{3,2,1,0:T(8,128)} %bitcast.89, s32[32]{0:T(128)S(1)} %reshape.283), kind=kCustom, calls=%fused_computation.3 | custom fusion | bytes 16777472 | tf_op jit(solution)/shard_map/jit(take_along_axis)/gather | solution.py:11
  227.9 6.1 %select_reduce_fusion = f32[16,128,512]{2,1,0:T(8,128)S(1)} fusion(f32[2,16,128,512]{3,2,1,0:T(8,128)} %bitcast.88, pred[2,16]{1,0:T(4,128)(4,1)S(1)} %compare_and_fusion.1, pred[2,16]{1,0:T(4,128)(4,1)S(1)} %fusion.36), kind=kLoop, calls=%fused_computation.7 | loop fusion | flops 5242880 | bytes 12582976 | tf_op jit(solution)/shard_map/reduce_sum | solution.py:101
  234.0 1.9 bitcast_select_fusion.2
  236.0 3.9 %fusion.3 = f32[2048,256]{1,0:T(8,128)} fusion(f32[2048,256]{1,0:T(8,128)S(1)} %get-tuple-element.43, f32[2048,256]{1,0:T(8,128)S(1)} %get-tuple-element.44, f32[256,256]{1,0:T(8,128)S(1)} %fusion.12, f32[2048,512]{1,0:T(8,128)S(1)} %bitcast.92, f32[256]{0:T(256)S(1)} %copy-done.2, s32[256]{0:T(256)S(1)} %iota_add_fusion, s32[2048]{0:T(1024)S(1)} %fusion.31, ...), kind=kOutput, calls=%fused_computation.14 | convolution fusion | flops 1613758464 | bytes 8663041 | tf_op jit(solution)/shard_map/dot_general | solution.py:113
  (65 shorter events, 2.4 us)
Async XLA Ops:
  6.5 78.4 %all-gather.3.cloned.1.call-start = ((), (), s32[]{:S(2)}) async-start(), calls=%async_computation.1 | async-start | bytes 17301504 | tf_op jit(solution)/shard_map/all_gather | solution.py:29
  7.3 214.8 %reduce-scatter.2.cloned.1.call-start = ((), (), s32[]{:S(2)}) async-start(), calls=%async_computation.2 | async-start | bytes 10485760 | tf_op jit(solution)/shard_map/reduce_scatter | solution.py:74
  96.0 2.0 copy-start.1
  98.0 31.1 %collective-permute-start = (f32[256,512]{0,1:T(8,128)S(1)}, f32[256,512]{0,1:T(8,128)S(1)}, u32[]{:S(2)}, u32[]{:S(2)}) collective-permute-start(f32[256,512]{0,1:T(8,128)S(1)} %fusion.9), channel_id=1, source_target_pairs={{0,32},{32,64},{64,96},{96,0},{1,33},{33,65},{65,97},{97,1},{2,34}... | collective-permute-start | bytes 1572872 | tf_op jit(solution)/shard_map/ppermute | solution.py:63
  99.5 29.7 %collective-permute-start.1 = (f32[256,512]{0,1:T(8,128)S(1)}, f32[256,512]{0,1:T(8,128)S(1)}, u32[]{:S(2)}, u32[]{:S(2)}) collective-permute-start(f32[256,512]{0,1:T(8,128)S(1)} %fusion.9), channel_id=1, source_target_pairs={{0,64},{32,96},{64,0},{96,32},{1,65},{33,97},{65,1},{97,33},{2,66}... | collective-permute-start | bytes 1572872 | tf_op jit(solution)/shard_map/ppermute | solution.py:63
  102.1 27.0 %collective-permute-start.2 = (f32[256,512]{0,1:T(8,128)S(1)}, f32[256,512]{0,1:T(8,128)S(1)}, u32[]{:S(2)}, u32[]{:S(2)}) collective-permute-start(f32[256,512]{0,1:T(8,128)S(1)} %fusion.9), channel_id=1, source_target_pairs={{0,96},{32,0},{64,32},{96,64},{1,97},{33,1},{65,33},{97,65},{2,98}... | collective-permute-start | bytes 1572872 | tf_op jit(solution)/shard_map/ppermute | solution.py:63
  144.3 0.7 copy-start
  234.0 1.9 copy-start.2
Sparse Core Ops, SparseCore 0:
  9.6 75.2 all-gather.2
  144.5 77.5 reduce-scatter.1

commit v6 on v5

--- a/solution.py
+++ b/solution.py
@@ -8,7 +8,7 @@
 
 
 def pick_tiles(tiles4, index):
-    return jnp.take_along_axis(tiles4, index[:, :, None, None], axis=1)
+    return jnp.take_along_axis(tiles4, index[:, :, None, None], axis=1, mode="clip")
 
 
 def shards(child_factors, child_tiles, root_diag):
@@ -63,14 +63,14 @@
         pivot_part = pivot_part + lax.ppermute(extra, "row", pairs)
     main_rows = col_rows + (extra[:1, :1] * 0).astype(col_rows.dtype)[None]
     main = jnp.einsum(
-        "cuk,cmk->cum", gathered, main_rows, preferred_element_type=jnp.float32
+        "cutk,cmk->cutm", tiles4, main_rows, preferred_element_type=jnp.float32
     )
     main = main.reshape(n_child * tiles_child, TILE, n_cols)
     child_base = (jnp.arange(n_child, dtype=jnp.int32) * tiles_child)[:, None]
     flat_order = (order + child_base).reshape(n_child, row_count, per_group)
     flat_order = jnp.transpose(flat_order, (1, 0, 2)).reshape(-1)
     flat_order = flat_order + (pivot_part[0, 0] * 0).astype(jnp.int32)
-    main = jnp.take(main, flat_order, axis=0)
+    main = jnp.take(main, flat_order, axis=0, mode="clip")
     mine = lax.psum_scatter(
         main.reshape(row_count * n_child * per_group * TILE, n_cols),
         "row",

time: 248 us -> 240 us (0.968)
  other arithmetic: 72.5 us -> 66.5 us
  matrix products: 24.5 us -> 19.9 us
  waiting for transfers between devices: 61.6 us -> 65.1 us
    reshape x0 -> x1, local copies, waits for them, and re-layouts: none -> 8.99 us  [shards(): main = main.reshape(n_child * tiles_child, TILE, n_cols)]
    dot_general x1 -> x0, local copies, waits for them, and re-layouts: 8.67 us -> none  [shards(): jnp.einsum('cuk,cmk->cum', gathered, main_rows, preferred_element_type=jn...]
    select_n x2 -> x0, other arithmetic: 5.82 us -> none  [shards(): main = jnp.take(main, flat_order, axis=0)]
    dot_general x1, matrix products: 15.7 us -> 11.1 us  [shards(): jnp.einsum('cutk,cmk->cutm', tiles4, main_rows, preferred_element_type=jn...]
    reduce_scatter x1, waiting for transfers between devices: 13.5 us -> 16.2 us  [shards(): lax.psum_scatter(main.reshape(row_count * n_child * per_group * TILE, n_c...]
    another operation x7 -> x6, other arithmetic: 34.6 us -> 34 us  [shards(): lead = jnp.tril(jnp.linalg.cholesky(front00))]
  transfers between devices with their start and end apart: 5 -> 5, of which waited for: 2 -> 3; matrix products, arithmetic and copies ran while one was open for 37% -> 36% of each run, Pallas kernels for 0% -> 0%
where the time goes in v6:
time: 240 us; the launch traced here: 239 us
  other arithmetic  66.5 us (28%)
  waiting for transfers between devices  65.1 us (27%)
  local copies, waits for them, and re-layouts  39 us (16%)
  blocking collectives  25.9 us (11%)
  matrix products  19.9 us (8%)
  between operations  16.9 us (7%)
  starting transfers between devices  5.72 us (2%)
    all_gather x1, waiting for transfers between devices, shards(): gathered = lax.all_gather(child_factors, 'col', axis=1, tiled=True)  47.5 us
    another operation x6, other arithmetic, shards(): lead = jnp.tril(jnp.linalg.cholesky(front00))  34 us
    all_gather x1, blocking collectives, shards(): full_diag = lax.all_gather(root_diag, 'col', axis=0, tiled=True)  25.9 us
    another operation x3, other arithmetic, shards(): lax.linalg.triangular_solve(lead, jnp.eye(lead_rows, dtype=jnp.float32),...  19.9 us
    reduce_scatter x1, waiting for transfers between devices, shards(): lax.psum_scatter(main.reshape(row_count * n_child * per_group * TILE, n_c...  16.2 us
    gather x4, local copies, waits for them, and re-layouts, pick_tiles(): jnp.take_along_axis(tiles4, index[:, :, None, None], axis=1, mode='clip')  14.6 us
    dot_general x1, matrix products, shards(): jnp.einsum('cutk,cmk->cutm', tiles4, main_rows, preferred_element_type=jn...  11.1 us
    reshape x1, local copies, waits for them, and re-layouts, shards(): main = main.reshape(n_child * tiles_child, TILE, n_cols)  8.99 us
  transfers between devices with their start and end apart: 5, of which 3 were waited for; matrix products, arithmetic and copies ran while one was open for 36% of the time, Pallas kernels for 0%

profile of v6, /device:TPU:0, one launch (start us, length us, event | category | flops | bytes accessed | tf_op | source)
XLA Modules:
  0.0 238.9 jit_solution(6653991229276031303)
XLA Ops:
  6.5 0.7 all-gather.3.cloned.1.call-update
  7.3 25.9 %all-gather = f32[32,1,256]{2,1,0:T(1,128)S(1)} all-gather(f32[1,1,256]{2,1,0:T(1,128)} %bitcast.96), channel_id=1, replica_groups=mesh['row'=4,'col'=32] {'col'}, dimensions={0}, use_global_device_ids=true | all-gather | bytes 33792 | tf_op jit(solution)/shard_map/all_gather | solution.py:32
  33.2 0.5 slice.99
  34.4 0.9 fusion.36
  35.4 0.9 compare_reduce_fusion
  36.3 0.7 fusion.40
  37.0 0.2 convert_reduce_fusion
  37.4 47.5 %all-gather.3.cloned.1.call-done = bf16[2,2048,2048]{2,1,0:T(8,128)(2,1)} async-done(((bf16[2,64,2048]{2,1,0:T(8,128)(2,1)}), bf16[2,2048,2048]{2,1,0:T(8,128)(2,1)}) %all-gather.3.cloned.1.call-update) | async-done | bytes 16777232 | tf_op jit(solution)/shard_map/all_gather | solution.py:29
  84.9 8.5 %gather_fusion.1 = bf16[8,128,2048]{2,1,0:T(8,128)(2,1)} fusion(bf16[2,16,128,2048]{3,2,1,0:T(8,128)(2,1)} %bitcast.90, s32[8]{0:T(128)S(1)} %reshape.240), kind=kCustom, calls=%fused_computation.1 | custom fusion | bytes 8388672 | tf_op jit(solution)/shard_map/jit(take_along_axis)/gather | solution.py:11
  93.4 2.7 %bitcast_select_fusion = bf16[2,512,2048]{2,1,0:T(8,128)(2,1)S(1)} fusion(pred[2,512]{1,0:T(4,128)(4,1)S(1)} %bitcast.95, bf16[2,512,2048]{2,1,0:T(8,128)(2,1)} %bitcast.88), kind=kLoop, calls=%fused_computation.9 | loop fusion | flops 2097152 | bytes 8389632 | tf_op jit(solution)/shard_map/jit(_where)/select_n | solution.py:52
  96.1 1.3 fusion.10
  97.4 1.5 collective-permute-start
  99.0 2.7 %collective-permute-start.1 = (f32[256,512]{0,1:T(8,128)S(1)}, f32[256,512]{0,1:T(8,128)S(1)}, u32[]{:S(2)}, u32[]{:S(2)}) collective-permute-start(f32[256,512]{0,1:T(8,128)S(1)} %fusion.10), channel_id=1, source_target_pairs={{0,64},{32,96},{64,0},{96,32},{1,65},{33,97},{65,1},{97,33},{2,66}... | collective-permute-start | bytes 1572872 | tf_op jit(solution)/shard_map/ppermute | solution.py:63
  101.7 1.5 collective-permute-start.2
  103.1 0.5 slice.103
  104.3 11.1 %fusion = f32[2,512,16,128]{3,1,2,0:T(8,128)} fusion(bf16[2,16,128,2048]{3,2,1,0:T(8,128)(2,1)S(1)} %bitcast.91, bf16[2,512,2048]{2,1,0:T(8,128)(2,1)S(1)} %bitcast_select_fusion, bf16[]{:T(256)} %bitcast.18), kind=kOutput, calls=%fused_computation.7 | convolution fusion | flops 8598323200 | bytes 29360130 | tf_op jit(solution)/shard_map/cutk,cmk->cutm/dot_general | solution.py:65
  115.4 9.0 %copy.67 = f32[32,128,512]{2,1,0:T(8,128)} copy(f32[32,128,512]{1,2,0:T(8,128)} %bitcast.89) | data formatting | bytes 16777216 | tf_op jit(solution)/shard_map/reshape | solution.py:68
  124.4 0.6 collective-permute-done.1
  124.9 1.2 add_add_fusion
  126.1 0.5 slice.104
  127.5 7.7 %gather_fusion = f32[32,128,512]{2,1,0:T(8,128)} fusion(f32[32,128,512]{2,1,0:T(8,128)} %copy.67, s32[1024]{0:T(1024)S(1)} %pad_clamp_fusion), kind=kCustom, calls=%fused_computation | custom fusion | bytes 16777344 | tf_op jit(solution)/shard_map/jit(_take)/gather | solution.py:73
  135.4 0.5 copy-done
  135.8 0.7 gather_fusion.2
  136.6 0.1 fusion.38
  137.1 0.1 copy.60
  137.3 11.7 %cholesky.49 = f32[128,128]{1,0:T(8,128)S(1)} custom-call(f32[128,128]{1,0:T(8,128)S(1)} %cholesky.115), custom_call_target="Cholesky" | custom-call | tf_op jit(solution)/shard_map/jit(cholesky)/cholesky | solution.py:85
  149.0 0.1 copy.61
  149.1 9.8 %custom-call.14 = f32[1,128,128]{1,2,0:T(8,128)S(1)} custom-call(f32[1,128,128]{2,1,0:T(8,128)S(1)} %get-tuple-element.46), custom_call_target="InvertDiagBlocksLowerTriangular" | custom-call | tf_op jit(solution)/shard_map/jit(cholesky)/cholesky | solution.py:85
  158.9 0.2 fusion.21
  159.2 0.3 convolution_subtract_fusion.2
  159.5 11.7 %cholesky.103 = f32[128,128]{1,0:T(8,128)S(1)} custom-call(f32[128,128]{1,0:T(8,128)S(1)} %convolution_subtract_fusion.2), custom_call_target="Cholesky" | custom-call | tf_op jit(solution)/shard_map/jit(cholesky)/cholesky | solution.py:85
  171.4 0.6 compare_reduce_fusion.1
  173.4 4.0 %while.1 = (s32[]{:T(128)}, f32[256,256]{0,1:T(8,128)S(1)}, s32[2,2]{1,0:T(2,128)S(1)}, f32[2,128,128]{2,1,0:T(8,128)S(1)}, s32[]{:T(128)}) while((s32[]{:T(128)}, f32[256,256]{0,1:T(8,128)S(1)}, s32[2,2]{1,0:T(2,128)S(1)}, f32[2,128,128]{2,1,0:T(8,128)S(1)}, s32[]{:T(128)}) %tuple.28), condition=%wide.while_cond, body=%wide.while_body.sunk | while | flops 2 | bytes 393321 | solution.py:86
  173.4 0.6 fusion.61
  174.0 1.3 dynamic-slice.7
  175.4 0.6 fusion.61
  176.0 1.3 dynamic-slice.7
  177.4 19.9 %custom-call.15 = f32[2,128,128]{1,2,0:T(8,128)S(1)} custom-call(f32[2,128,128]{2,1,0:T(8,128)S(1)} %get-tuple-element.12), custom_call_target="InvertDiagBlocksLowerTriangular" | custom-call | tf_op jit(solution)/shard_map/triangular_solve | solution.py:86
  197.3 0.1 copy.64
  197.5 0.3 fusion.16
  197.7 0.3 convolution_subtract_fusion.1
  198.1 0.3 fusion.19
  198.4 0.4 fusion.13
  198.8 16.2 %reduce-scatter.2.cloned.1.call-done = f32[1024,512]{1,0:T(8,128)} async-done(((f32[4096,512]{1,0:T(8,128)}), f32[1024,512]{1,0:T(8,128)}) %reduce-scatter.2.cloned.1.call-update) | async-done | bytes 2097168 | tf_op jit(solution)/shard_map/reduce_scatter | solution.py:74
  215.0 5.9 %gather_fusion.3 = f32[32,128,512]{2,1,0:T(8,128)} fusion(f32[2,4,128,512]{3,2,1,0:T(8,128)} %bitcast.84, s32[32]{0:T(128)S(1)} %reshape.252), kind=kCustom, calls=%fused_computation.3 | custom fusion | bytes 16777472 | tf_op jit(solution)/shard_map/jit(take_along_axis)/gather | solution.py:11
  220.9 5.3 %select_reduce_fusion = f32[16,128,512]{2,1,0:T(8,128)S(1)} fusion(f32[2,16,128,512]{3,2,1,0:T(8,128)} %bitcast.83, pred[2,16]{1,0:T(4,128)(4,1)S(1)} %fusion.37), kind=kLoop, calls=%fused_computation.6 | loop fusion | flops 3145728 | bytes 12582944 | tf_op jit(solution)/shard_map/reduce_sum | solution.py:101
  226.3 1.9 bitcast_select_fusion.1
  228.2 3.9 %fusion.4 = f32[2048,256]{1,0:T(8,128)} fusion(f32[2048,256]{1,0:T(8,128)S(1)} %get-tuple-element.47, f32[2048,256]{1,0:T(8,128)S(1)} %get-tuple-element.48, f32[256,256]{1,0:T(8,128)S(1)} %fusion.13, f32[2048,512]{1,0:T(8,128)S(1)} %bitcast.87, f32[256]{0:T(256)S(1)} %copy-done.2, s32[256]{0:T(256)S(1)} %iota_add_fusion, s32[2048]{0:T(1024)S(1)} %fusion.32, ...), kind=kOutput, calls=%fused_computation.13 | convolution fusion | flops 1613758464 | bytes 8663041 | tf_op jit(solution)/shard_map/dot_general | solution.py:113
  (56 shorter events, 2.0 us)
Async XLA Ops:
  6.5 78.4 %all-gather.3.cloned.1.call-start = ((), (), s32[]{:S(2)}) async-start(), calls=%async_computation.1 | async-start | bytes 17301504 | tf_op jit(solution)/shard_map/all_gather | solution.py:29
  7.3 207.8 %reduce-scatter.2.cloned.1.call-start = ((), (), s32[]{:S(2)}) async-start(), calls=%async_computation.2 | async-start | bytes 10485760 | tf_op jit(solution)/shard_map/reduce_scatter | solution.py:74
  93.4 10.8 %copy-start.1 = (bf16[2,2048,2048]{2,1,0:T(8,128)(2,1)S(1)}, bf16[2,2048,2048]{2,1,0:T(8,128)(2,1)}, u32[]{:S(2)}) copy-start(bf16[2,2048,2048]{2,1,0:T(8,128)(2,1)} %all-gather.3.cloned.1.call-done) | copy-start | bytes 50331652
  97.4 26.9 %collective-permute-start = (f32[256,512]{0,1:T(8,128)S(1)}, f32[256,512]{0,1:T(8,128)S(1)}, u32[]{:S(2)}, u32[]{:S(2)}) collective-permute-start(f32[256,512]{0,1:T(8,128)S(1)} %fusion.10), channel_id=1, source_target_pairs={{0,32},{32,64},{64,96},{96,0},{1,33},{33,65},{65,97},{97,1},{2,34}... | collective-permute-start | bytes 1572872 | tf_op jit(solution)/shard_map/ppermute | solution.py:63
  99.0 26.0 %collective-permute-start.1 = (f32[256,512]{0,1:T(8,128)S(1)}, f32[256,512]{0,1:T(8,128)S(1)}, u32[]{:S(2)}, u32[]{:S(2)}) collective-permute-start(f32[256,512]{0,1:T(8,128)S(1)} %fusion.10), channel_id=1, source_target_pairs={{0,64},{32,96},{64,0},{96,32},{1,65},{33,97},{65,1},{97,33},{2,66}... | collective-permute-start | bytes 1572872 | tf_op jit(solution)/shard_map/ppermute | solution.py:63
  101.7 23.3 %collective-permute-start.2 = (f32[256,512]{0,1:T(8,128)S(1)}, f32[256,512]{0,1:T(8,128)}, u32[]{:S(2)}, u32[]{:S(2)}) collective-permute-start(f32[256,512]{0,1:T(8,128)S(1)} %fusion.10), channel_id=1, source_target_pairs={{0,96},{32,0},{64,32},{96,64},{1,97},{33,1},{65,33},{97,65},{2,98}... | collective-permute-start | bytes 1572872 | tf_op jit(solution)/shard_map/ppermute | solution.py:63
  135.2 0.7 copy-start
  226.3 1.9 copy-start.2
Sparse Core Ops, SparseCore 0:
  9.6 75.2 all-gather.2
  135.3 79.6 reduce-scatter.1

commit v7 on v6

--- a/solution.py
+++ b/solution.py
@@ -48,7 +48,17 @@
     where_at = jnp.sum(jnp.where(match, position[None, :, None], 0), axis=1).astype(jnp.int32)
     where_at = where_at + diag_edge
     present = jnp.any(match, axis=1)
-    col_rows = pick_tiles(tiles4, where_at)
+    col_rows = jnp.stack(
+        [
+            jnp.stack(
+                [
+                    lax.dynamic_index_in_dim(tiles4[child], where_at[child, slot], 0, keepdims=False)
+                    for slot in range(where_at.shape[1])
+                ]
+            )
+            for child in range(n_child)
+        ]
+    )
     col_rows = jnp.where(present[:, :, None, None], col_rows, jnp.zeros_like(col_rows))
     n_cols = wanted.shape[0] * TILE
     col_rows = col_rows.reshape(n_child, n_cols, k_loc)

time: 240 us -> 238 us (level)
  waiting for transfers between devices: 65.1 us -> 48.4 us
  between operations: 16.9 us -> 31.9 us
    all_gather x1, waiting for transfers between devices: 47.5 us -> 30.2 us  [shards(): gathered = lax.all_gather(child_factors, 'col', axis=1, tiled=True)]
    gather x4 -> x2, local copies, waits for them, and re-layouts: 14.6 us -> 5.98 us  [pick_tiles(): jnp.take_along_axis(tiles4, index[:, :, None, None], axis=1, mode='clip')]
    slice x0 -> x2, local copies, waits for them, and re-layouts: none -> 7.43 us  [the longest x1 6.74 us: shards(): tiles4[child]]
    another operation x6 -> x7, other arithmetic: 34 us -> 34.6 us  [shards(): lead = jnp.tril(jnp.linalg.cholesky(front00))]
  transfers between devices with their start and end apart: 5 -> 5, of which waited for: 3 -> 3; matrix products, arithmetic and copies ran while one was open for 36% -> 37% of each run, Pallas kernels for 0% -> 0%
where the time goes in v7:
time: 238 us; the launch traced here: 236 us
  other arithmetic  65.5 us (28%)
  waiting for transfers between devices  48.4 us (20%)
  local copies, waits for them, and re-layouts  38.7 us (16%)
  between operations  31.9 us (13%)
  blocking collectives  26.1 us (11%)
  matrix products  19.9 us (8%)
  starting transfers between devices  5.72 us (2%)
    another operation x7, other arithmetic, shards(): lead = jnp.tril(jnp.linalg.cholesky(front00))  34.6 us
    all_gather x1, waiting for transfers between devices, shards(): gathered = lax.all_gather(child_factors, 'col', axis=1, tiled=True)  30.2 us
    all_gather x1, blocking collectives, shards(): full_diag = lax.all_gather(root_diag, 'col', axis=0, tiled=True)  26.1 us
    another operation x3, other arithmetic, shards(): lax.linalg.triangular_solve(lead, jnp.eye(lead_rows, dtype=jnp.float32),...  19.9 us
    reduce_scatter x1, waiting for transfers between devices, shards(): lax.psum_scatter(main.reshape(row_count * n_child * per_group * TILE, n_c...  17 us
    dot_general x1, matrix products, shards(): jnp.einsum('cutk,cmk->cutm', tiles4, main_rows, preferred_element_type=jn...  11.1 us
    reshape x1, local copies, waits for them, and re-layouts, shards(): main = main.reshape(n_child * tiles_child, TILE, n_cols)  8.99 us
    gather x1, local copies, waits for them, and re-layouts, shards(): main = jnp.take(main, flat_order, axis=0, mode='clip')  7.69 us
  transfers between devices with their start and end apart: 5, of which 3 were waited for; matrix products, arithmetic and copies ran while one was open for 37% of the time, Pallas kernels for 0%

profile of v7, /device:TPU:0, one launch (start us, length us, event | category | flops | bytes accessed | tf_op | source)
XLA Modules:
  0.0 236.3 jit_solution(547844790708496788)
XLA Ops:
  6.5 0.7 all-gather.3.cloned.1.call-update
  7.3 0.7 fusion.40
  8.0 0.2 convert_reduce_fusion
  8.5 1.3 gather_fusion.1
  9.9 26.1 %all-gather = f32[32,1,256]{2,1,0:T(1,128)S(1)} all-gather(f32[1,1,256]{2,1,0:T(1,128)} %bitcast.105), channel_id=1, replica_groups=mesh['row'=4,'col'=32] {'col'}, dimensions={0}, use_global_device_ids=true | all-gather | bytes 33792 | tf_op jit(solution)/shard_map/all_gather | solution.py:32
  36.0 0.5 slice.146
  37.2 0.9 fusion.36
  38.1 0.7 fusion.50
  48.8 0.9 compare_reduce_fusion
  54.8 30.2 %all-gather.3.cloned.1.call-done = bf16[2,2048,2048]{2,1,0:T(8,128)(2,1)} async-done(((bf16[2,64,2048]{2,1,0:T(8,128)(2,1)}), bf16[2,2048,2048]{2,1,0:T(8,128)(2,1)}) %all-gather.3.cloned.1.call-update) | async-done | bytes 16777232 | tf_op jit(solution)/shard_map/all_gather | solution.py:29
  84.9 6.7 %fusion.49 = (bf16[1,2048,2048]{2,1,0:T(8,128)(2,1)S(1)}, bf16[1,2048,2048]{2,1,0:T(8,128)(2,1)S(1)}) fusion(bf16[2,2048,2048]{2,1,0:T(8,128)(2,1)} %all-gather.3.cloned.1.call-done), kind=kLoop, calls=%fused_computation.132 | loop fusion | bytes 33554432 | tf_op jit(solution)/shard_map/slice | solution.py:55
  91.7 0.2 constant_dynamic-slice_fusion.9
  91.9 0.3 pad_maximum_fusion
  92.4 0.3 pad_maximum_fusion.1
  92.6 0.6 maximum_select_fusion
  93.3 1.3 fusion.10
  94.6 1.5 collective-permute-start
  96.1 2.7 %collective-permute-start.1 = (f32[256,512]{0,1:T(8,128)S(1)}, f32[256,512]{0,1:T(8,128)S(1)}, u32[]{:S(2)}, u32[]{:S(2)}) collective-permute-start(f32[256,512]{0,1:T(8,128)S(1)} %fusion.10), channel_id=1, source_target_pairs={{0,64},{32,96},{64,0},{96,32},{1,65},{33,97},{65,1},{97,33},{2,66}... | collective-permute-start | bytes 1572872 | tf_op jit(solution)/shard_map/ppermute | solution.py:73
  98.8 1.5 collective-permute-start.2
  100.3 0.6 slice.151
  101.6 11.1 %fusion = f32[2,512,16,128]{3,1,2,0:T(8,128)} fusion(bf16[2,16,128,2048]{3,2,1,0:T(8,128)(2,1)S(1)} %bitcast.95, bf16[2,512,2048]{2,1,0:T(8,128)(2,1)S(1)} %maximum_select_fusion, bf16[]{:T(256)} %bitcast.27), kind=kOutput, calls=%fused_computation.7 | convolution fusion | flops 8598323200 | bytes 29360130 | tf_op jit(solution)/shard_map/cutk,cmk->cutm/dot_general | solution.py:75
  112.7 9.0 %copy.67 = f32[32,128,512]{2,1,0:T(8,128)} copy(f32[32,128,512]{1,2,0:T(8,128)} %bitcast.100) | data formatting | bytes 16777216 | tf_op jit(solution)/shard_map/reshape | solution.py:78
  121.7 0.4 collective-permute-done.1
  122.1 1.2 add_add_fusion
  123.3 0.6 slice.152
  124.7 7.7 %gather_fusion = f32[32,128,512]{2,1,0:T(8,128)} fusion(f32[32,128,512]{2,1,0:T(8,128)} %copy.67, s32[1024]{0:T(1024)S(1)} %pad_clamp_fusion), kind=kCustom, calls=%fused_computation | custom fusion | bytes 16777344 | tf_op jit(solution)/shard_map/jit(_take)/gather | solution.py:83
  133.0 11.7 %cholesky.49 = f32[128,128]{1,0:T(8,128)S(1)} custom-call(f32[128,128]{1,0:T(8,128)S(1)} %cholesky.115), custom_call_target="Cholesky" | custom-call | tf_op jit(solution)/shard_map/jit(cholesky)/cholesky | solution.py:95
  144.8 9.8 %custom-call.14 = f32[1,128,128]{1,2,0:T(8,128)S(1)} custom-call(f32[1,128,128]{2,1,0:T(8,128)S(1)} %get-tuple-element.56), custom_call_target="InvertDiagBlocksLowerTriangular" | custom-call | tf_op jit(solution)/shard_map/jit(cholesky)/cholesky | solution.py:95
  154.6 0.2 fusion.21
  154.9 0.3 convolution_subtract_fusion.2
  155.2 11.7 %cholesky.103 = f32[128,128]{1,0:T(8,128)S(1)} custom-call(f32[128,128]{1,0:T(8,128)S(1)} %convolution_subtract_fusion.2), custom_call_target="Cholesky" | custom-call | tf_op jit(solution)/shard_map/jit(cholesky)/cholesky | solution.py:95
  167.1 0.6 compare_reduce_fusion.1
  167.7 0.7 compare_reduce_fusion.2
  169.8 4.2 %while.1 = (s32[]{:T(128)}, f32[256,256]{0,1:T(8,128)S(1)}, s32[2,2]{1,0:T(2,128)S(1)}, f32[2,128,128]{2,1,0:T(8,128)S(1)}, s32[]{:T(128)}) while((s32[]{:T(128)}, f32[256,256]{0,1:T(8,128)S(1)}, s32[2,2]{1,0:T(2,128)S(1)}, f32[2,128,128]{2,1,0:T(8,128)S(1)}, s32[]{:T(128)}) %tuple.42), condition=%wide.while_cond, body=%wide.while_body.sunk | while | flops 2 | bytes 393321 | solution.py:96
  169.8 0.6 fusion.60
  170.4 1.3 dynamic-slice.7
  171.9 0.6 fusion.60
  172.5 1.3 dynamic-slice.7
  174.0 19.9 %custom-call.15 = f32[2,128,128]{1,2,0:T(8,128)S(1)} custom-call(f32[2,128,128]{2,1,0:T(8,128)S(1)} %get-tuple-element.12), custom_call_target="InvertDiagBlocksLowerTriangular" | custom-call | tf_op jit(solution)/shard_map/triangular_solve | solution.py:96
  194.0 0.3 fusion.16
  194.3 0.3 convolution_subtract_fusion.1
  194.6 0.3 fusion.19
  194.9 0.4 fusion.13
  195.4 17.0 %reduce-scatter.2.cloned.1.call-done = f32[1024,512]{1,0:T(8,128)} async-done(((f32[4096,512]{1,0:T(8,128)}), f32[1024,512]{1,0:T(8,128)}) %reduce-scatter.2.cloned.1.call-update) | async-done | bytes 2097168 | tf_op jit(solution)/shard_map/reduce_scatter | solution.py:84
  212.4 5.9 %gather_fusion.2 = f32[32,128,512]{2,1,0:T(8,128)} fusion(f32[2,4,128,512]{3,2,1,0:T(8,128)} %bitcast.89, s32[32]{0:T(128)S(1)} %reshape.229), kind=kCustom, calls=%fused_computation.2 | custom fusion | bytes 16777472 | tf_op jit(solution)/shard_map/jit(take_along_axis)/gather | solution.py:11
  218.3 5.3 %select_reduce_fusion = f32[16,128,512]{2,1,0:T(8,128)S(1)} fusion(f32[2,16,128,512]{3,2,1,0:T(8,128)} %bitcast.88, pred[2,16]{1,0:T(4,128)(4,1)S(1)} %fusion.37), kind=kLoop, calls=%fused_computation.5 | loop fusion | flops 3145728 | bytes 12582944 | tf_op jit(solution)/shard_map/reduce_sum | solution.py:111
  223.7 1.9 bitcast_select_fusion
  225.6 3.9 %fusion.4 = f32[2048,256]{1,0:T(8,128)} fusion(f32[2048,256]{1,0:T(8,128)S(1)} %get-tuple-element.65, f32[2048,256]{1,0:T(8,128)S(1)} %get-tuple-element.66, f32[256,256]{1,0:T(8,128)S(1)} %fusion.13, f32[2048,512]{1,0:T(8,128)S(1)} %bitcast.92, f32[256]{0:T(256)S(1)} %copy-done, s32[256]{0:T(256)S(1)} %iota_add_fusion, s32[2048]{0:T(1024)S(1)} %fusion.32, ...), kind=kOutput, calls=%fused_computation.12 | convolution fusion | flops 1613758464 | bytes 8663041 | tf_op jit(solution)/shard_map/dot_general | solution.py:123
  (65 shorter events, 2.4 us)
Async XLA Ops:
  6.5 78.4 %all-gather.3.cloned.1.call-start = ((), (), s32[]{:S(2)}) async-start(), calls=%async_computation.1 | async-start | bytes 17301504 | tf_op jit(solution)/shard_map/all_gather | solution.py:29
  7.3 205.1 %reduce-scatter.2.cloned.1.call-start = ((), (), s32[]{:S(2)}) async-start(), calls=%async_computation.2 | async-start | bytes 10485760 | tf_op jit(solution)/shard_map/reduce_scatter | solution.py:84
  91.7 9.9 %slice-start = ((s8[16777216]{0:T(1024)(128)(4,1)}), s8[4194304]{0:T(1024)(128)(4,1)S(1)}, s32[]{:S(2)}) async-start(s8[16777216]{0:T(1024)(128)(4,1)} %bitcast.93), calls=%async_computation.3 | async-start | bytes 8388608
  92.2 9.4 %slice-start.1 = ((s8[16777216]{0:T(1024)(128)(4,1)}), s8[4194304]{0:T(1024)(128)(4,1)S(1)}, s32[]{:S(2)}) async-start(s8[16777216]{0:T(1024)(128)(4,1)} %bitcast.93), calls=%async_computation.4 | async-start | bytes 8388608
  92.6 8.9 %slice-start.2 = ((s8[16777216]{0:T(1024)(128)(4,1)}), s8[4194304]{0:T(1024)(128)(4,1)S(1)}, s32[]{:S(2)}) async-start(s8[16777216]{0:T(1024)(128)(4,1)} %bitcast.93), calls=%async_computation.5 | async-start | bytes 8388608
  93.3 8.3 %slice-start.3 = ((s8[16777216]{0:T(1024)(128)(4,1)}), s8[4194304]{0:T(1024)(128)(4,1)S(1)}, s32[]{:S(2)}) async-start(s8[16777216]{0:T(1024)(128)(4,1)} %bitcast.93), calls=%async_computation.6 | async-start | bytes 8388608
  94.6 27.1 %collective-permute-start = (f32[256,512]{0,1:T(8,128)S(1)}, f32[256,512]{0,1:T(8,128)S(1)}, u32[]{:S(2)}, u32[]{:S(2)}) collective-permute-start(f32[256,512]{0,1:T(8,128)S(1)} %fusion.10), channel_id=1, source_target_pairs={{0,32},{32,64},{64,96},{96,0},{1,33},{33,65},{65,97},{97,1},{2,34}... | collective-permute-start | bytes 1572872 | tf_op jit(solution)/shard_map/ppermute | solution.py:73
  96.1 26.0 %collective-permute-start.1 = (f32[256,512]{0,1:T(8,128)S(1)}, f32[256,512]{0,1:T(8,128)S(1)}, u32[]{:S(2)}, u32[]{:S(2)}) collective-permute-start(f32[256,512]{0,1:T(8,128)S(1)} %fusion.10), channel_id=1, source_target_pairs={{0,64},{32,96},{64,0},{96,32},{1,65},{33,97},{65,1},{97,33},{2,66}... | collective-permute-start | bytes 1572872 | tf_op jit(solution)/shard_map/ppermute | solution.py:73
  98.8 23.3 %collective-permute-start.2 = (f32[256,512]{0,1:T(8,128)S(1)}, f32[256,512]{0,1:T(8,128)}, u32[]{:S(2)}, u32[]{:S(2)}) collective-permute-start(f32[256,512]{0,1:T(8,128)S(1)} %fusion.10), channel_id=1, source_target_pairs={{0,96},{32,0},{64,32},{96,64},{1,97},{33,1},{65,33},{97,65},{2,98}... | collective-permute-start | bytes 1572872 | tf_op jit(solution)/shard_map/ppermute | solution.py:73
  223.7 1.9 copy-start
Sparse Core Ops, SparseCore 0:
  9.6 75.2 all-gather.2
  132.6 79.7 reduce-scatter.1

commit v8 on v7

--- a/solution.py
+++ b/solution.py
@@ -101,14 +101,16 @@
     my_tiles = lax.dynamic_slice_in_dim(order, row_index * per_group, per_group, axis=1)
     my_root = jnp.take_along_axis(child_tiles, my_tiles, axis=1)
     my_local = (my_root * TILE // block_size) // row_count * tiles_block + my_root % tiles_block
-    loc_index = jnp.arange(loc_tiles, dtype=jnp.int32)
-    hit = my_local[:, None, :] == loc_index[None, :, None]
-    src = jnp.sum(jnp.where(hit, jnp.arange(per_group, dtype=jnp.int32)[None, None, :], 0), axis=2)
-    got = jnp.any(hit, axis=2)
     mine4 = mine.reshape(n_child, per_group, TILE, n_cols)
-    placed = pick_tiles(mine4, src.astype(jnp.int32))
-    placed = jnp.where(got[:, :, None, None], placed, jnp.zeros_like(placed))
-    front_loc = jnp.sum(placed, axis=0).reshape(loc_rows, n_cols)
+    front_loc = jnp.zeros((loc_tiles, TILE, n_cols), jnp.float32)
+    for child in range(n_child):
+        for slot in range(per_group):
+            at = my_local[child, slot]
+            here = lax.dynamic_index_in_dim(front_loc, at, 0, keepdims=True)
+            front_loc = lax.dynamic_update_index_in_dim(
+                front_loc, here + mine4[child, slot][None], at, 0
+            )
+    front_loc = front_loc.reshape(loc_rows, n_cols)
 
     local_rows = jnp.arange(loc_rows, dtype=jnp.int32)
     row_block = row_index + local_rows // block_size * row_count

time: 238 us -> 229 us (0.962)
  between operations: 31.9 us -> 46.7 us
  waiting for transfers between devices: 48.4 us -> 34.4 us
  other arithmetic: 65.5 us -> 59.8 us
  local copies, waits for them, and re-layouts: 38.7 us -> 34.5 us
    reduce_scatter x1, waiting for transfers between devices: 17 us -> 1.16 us  [shards(): lax.psum_scatter(main.reshape(row_count * n_child * per_group * TILE, n_c...]
    gather x2 -> x0, local copies, waits for them, and re-layouts: 5.98 us -> none  [pick_tiles(): jnp.take_along_axis(tiles4, index[:, :, None, None], axis=1, mode='clip')]
    reduce_sum x1 -> x0, other arithmetic: 5.35 us -> none  [shards(): front_loc = jnp.sum(placed, axis=0).reshape(loc_rows, n_cols)]
    another operation x7 -> x6, other arithmetic: 34.6 us -> 34 us  [shards(): lead = jnp.tril(jnp.linalg.cholesky(front00))]
  transfers between devices with their start and end apart: 5 -> 5, of which waited for: 3 -> 3; matrix products, arithmetic and copies ran while one was open for 37% -> 38% of each run, Pallas kernels for 0% -> 0%
where the time goes in v8:
time: 229 us; the launch traced here: 227 us
  other arithmetic  59.8 us (26%)
  between operations  46.7 us (20%)
  local copies, waits for them, and re-layouts  34.5 us (15%)
  waiting for transfers between devices  34.4 us (15%)
  blocking collectives  25.9 us (11%)
  matrix products  19.9 us (9%)
  starting transfers between devices  5.71 us (2%)
    another operation x6, other arithmetic, shards(): lead = jnp.tril(jnp.linalg.cholesky(front00))  34 us
    all_gather x1, waiting for transfers between devices, shards(): gathered = lax.all_gather(child_factors, 'col', axis=1, tiled=True)  32 us
    all_gather x1, blocking collectives, shards(): full_diag = lax.all_gather(root_diag, 'col', axis=0, tiled=True)  25.9 us
    another operation x3, other arithmetic, shards(): lax.linalg.triangular_solve(lead, jnp.eye(lead_rows, dtype=jnp.float32),...  19.9 us
    dot_general x1, matrix products, shards(): jnp.einsum('cutk,cmk->cutm', tiles4, main_rows, preferred_element_type=jn...  11.1 us
    reshape x1, local copies, waits for them, and re-layouts, shards(): main = main.reshape(n_child * tiles_child, TILE, n_cols)  9.01 us
    gather x1, local copies, waits for them, and re-layouts, shards(): main = jnp.take(main, flat_order, axis=0, mode='clip')  7.69 us
    slice x1, local copies, waits for them, and re-layouts, shards(): tiles4[child]  6.74 us
  transfers between devices with their start and end apart: 5, of which 3 were waited for; matrix products, arithmetic and copies ran while one was open for 38% of the time, Pallas kernels for 0%

profile of v8, /device:TPU:0, one launch (start us, length us, event | category | flops | bytes accessed | tf_op | source)
XLA Modules:
  0.0 226.9 jit_solution(4259736658362102404)
XLA Ops:
  6.5 0.7 all-gather.3.cloned.1.call-update
  7.3 25.9 %all-gather = f32[32,1,256]{2,1,0:T(1,128)S(1)} all-gather(f32[1,1,256]{2,1,0:T(1,128)} %bitcast.160), channel_id=1, replica_groups=mesh['row'=4,'col'=32] {'col'}, dimensions={0}, use_global_device_ids=true | all-gather | bytes 33792 | tf_op jit(solution)/shard_map/all_gather | solution.py:32
  33.2 0.5 slice.208
  34.4 0.9 fusion.51
  35.3 0.7 fusion.62
  46.0 0.9 compare_reduce_fusion
  46.9 0.7 fusion.54
  53.0 32.0 %all-gather.3.cloned.1.call-done = bf16[2,2048,2048]{2,1,0:T(8,128)(2,1)} async-done(((bf16[2,64,2048]{2,1,0:T(8,128)(2,1)}), bf16[2,2048,2048]{2,1,0:T(8,128)(2,1)}) %all-gather.3.cloned.1.call-update) | async-done | bytes 16777232 | tf_op jit(solution)/shard_map/all_gather | solution.py:29
  85.0 6.7 %fusion.60 = (bf16[1,2048,2048]{2,1,0:T(8,128)(2,1)S(1)}, bf16[1,2048,2048]{2,1,0:T(8,128)(2,1)S(1)}) fusion(bf16[2,2048,2048]{2,1,0:T(8,128)(2,1)} %all-gather.3.cloned.1.call-done), kind=kLoop, calls=%fused_computation.146 | loop fusion | bytes 33554432 | tf_op jit(solution)/shard_map/slice | solution.py:55
  91.7 0.2 constant_dynamic-slice_fusion.9
  91.9 0.3 pad_maximum_fusion
  92.4 0.3 pad_maximum_fusion.1
  92.7 0.6 maximum_select_fusion
  93.3 1.3 fusion.10
  94.6 1.5 collective-permute-start
  96.1 2.7 %collective-permute-start.1 = (f32[256,512]{0,1:T(8,128)S(1)}, f32[256,512]{0,1:T(8,128)S(1)}, u32[]{:S(2)}, u32[]{:S(2)}) collective-permute-start(f32[256,512]{0,1:T(8,128)S(1)} %fusion.10), channel_id=1, source_target_pairs={{0,64},{32,96},{64,0},{96,32},{1,65},{33,97},{65,1},{97,33},{2,66}... | collective-permute-start | bytes 1572872 | tf_op jit(solution)/shard_map/ppermute | solution.py:73
  98.8 1.5 collective-permute-start.2
  100.3 0.5 slice.213
  101.5 11.1 %fusion = f32[2,512,16,128]{3,1,2,0:T(8,128)} fusion(bf16[2,16,128,2048]{3,2,1,0:T(8,128)(2,1)S(1)} %bitcast.142, bf16[2,512,2048]{2,1,0:T(8,128)(2,1)S(1)} %maximum_select_fusion, bf16[]{:T(256)} %bitcast.26), kind=kOutput, calls=%fused_computation.5 | convolution fusion | flops 8598323200 | bytes 29360130 | tf_op jit(solution)/shard_map/cutk,cmk->cutm/dot_general | solution.py:75
  112.6 9.0 %copy.67 = f32[32,128,512]{2,1,0:T(8,128)} copy(f32[32,128,512]{1,2,0:T(8,128)} %bitcast.147) | data formatting | bytes 16777216 | tf_op jit(solution)/shard_map/reshape | solution.py:78
  121.6 0.5 collective-permute-done.1
  122.1 1.2 add_add_fusion
  123.3 0.5 slice.214
  124.6 7.7 %gather_fusion = f32[32,128,512]{2,1,0:T(8,128)} fusion(f32[32,128,512]{2,1,0:T(8,128)} %copy.67, s32[1024]{0:T(1024)S(1)} %pad_clamp_fusion), kind=kCustom, calls=%fused_computation | custom fusion | bytes 16777344 | tf_op jit(solution)/shard_map/jit(_take)/gather | solution.py:83
  132.5 0.5 copy-done
  133.0 0.7 gather_fusion.1
  133.8 0.7 fusion.61
  149.5 11.7 %cholesky.49 = f32[128,128]{1,0:T(8,128)S(1)} custom-call(f32[128,128]{1,0:T(8,128)S(1)} %cholesky.115), custom_call_target="Cholesky" | custom-call | tf_op jit(solution)/shard_map/jit(cholesky)/cholesky | solution.py:95
  161.3 9.8 %custom-call.14 = f32[1,128,128]{1,2,0:T(8,128)S(1)} custom-call(f32[1,128,128]{2,1,0:T(8,128)S(1)} %get-tuple-element.56), custom_call_target="InvertDiagBlocksLowerTriangular" | custom-call | tf_op jit(solution)/shard_map/jit(cholesky)/cholesky | solution.py:95
  171.1 0.2 fusion.36
  171.4 0.3 convolution_subtract_fusion.2
  171.7 11.7 %cholesky.103 = f32[128,128]{1,0:T(8,128)S(1)} custom-call(f32[128,128]{1,0:T(8,128)S(1)} %convolution_subtract_fusion.2), custom_call_target="Cholesky" | custom-call | tf_op jit(solution)/shard_map/jit(cholesky)/cholesky | solution.py:95
  183.6 0.6 compare_reduce_fusion.1
  185.6 4.0 %while.1 = (s32[]{:T(128)}, f32[256,256]{0,1:T(8,128)S(1)}, s32[2,2]{1,0:T(2,128)S(1)}, f32[2,128,128]{2,1,0:T(8,128)S(1)}, s32[]{:T(128)}) while((s32[]{:T(128)}, f32[256,256]{0,1:T(8,128)S(1)}, s32[2,2]{1,0:T(2,128)S(1)}, f32[2,128,128]{2,1,0:T(8,128)S(1)}, s32[]{:T(128)}) %tuple.49), condition=%wide.while_cond, body=%wide.while_body.sunk | while | flops 2 | bytes 393321 | solution.py:96
  185.6 0.6 fusion.72
  186.2 1.3 dynamic-slice.7
  187.6 0.6 fusion.72
  188.2 1.3 dynamic-slice.7
  189.7 19.9 %custom-call.15 = f32[2,128,128]{1,2,0:T(8,128)S(1)} custom-call(f32[2,128,128]{2,1,0:T(8,128)S(1)} %get-tuple-element.12), custom_call_target="InvertDiagBlocksLowerTriangular" | custom-call | tf_op jit(solution)/shard_map/triangular_solve | solution.py:96
  209.7 0.3 fusion.31
  210.0 0.3 convolution_subtract_fusion.1
  210.3 0.3 fusion.34
  210.6 0.4 fusion.13
  211.0 1.2 reduce-scatter.2.cloned.1.call-done
  212.2 0.5 broadcast_in_dim.119
  212.7 1.1 copy-done.1
  214.3 1.9 bitcast_select_fusion
  216.2 3.8 %fusion.4 = f32[2048,256]{1,0:T(8,128)} fusion(f32[2048,256]{1,0:T(8,128)S(1)} %get-tuple-element.73, f32[2048,256]{1,0:T(8,128)S(1)} %get-tuple-element.74, f32[256,256]{1,0:T(8,128)S(1)} %fusion.13, f32[2048,512]{1,0:T(8,128)S(1)} %bitcast.139, f32[256]{0:T(256)S(1)} %copy-done.2, s32[256]{0:T(256)S(1)} %iota_add_fusion, s32[2048]{0:T(1024)S(1)} %fusion.47, ...), kind=kOutput, calls=%fused_computation.10 | convolution fusion | flops 1613758464 | bytes 8663041 | tf_op jit(solution)/shard_map/dot_general | solution.py:125
  (73 shorter events, 2.8 us)
Async XLA Ops:
  6.5 78.4 %all-gather.3.cloned.1.call-start = ((), (), s32[]{:S(2)}) async-start(), calls=%async_computation.1 | async-start | bytes 17301504 | tf_op jit(solution)/shard_map/all_gather | solution.py:29
  7.3 204.9 %reduce-scatter.2.cloned.1.call-start = ((), (), s32[]{:S(2)}) async-start(), calls=%async_computation.2 | async-start | bytes 10485760 | tf_op jit(solution)/shard_map/reduce_scatter | solution.py:84
  91.7 9.7 %slice-start = ((s8[16777216]{0:T(1024)(128)(4,1)}), s8[4194304]{0:T(1024)(128)(4,1)S(1)}, s32[]{:S(2)}) async-start(s8[16777216]{0:T(1024)(128)(4,1)} %bitcast.140), calls=%async_computation.3 | async-start | bytes 8388608
  92.2 9.2 %slice-start.1 = ((s8[16777216]{0:T(1024)(128)(4,1)}), s8[4194304]{0:T(1024)(128)(4,1)S(1)}, s32[]{:S(2)}) async-start(s8[16777216]{0:T(1024)(128)(4,1)} %bitcast.140), calls=%async_computation.4 | async-start | bytes 8388608
  92.7 8.8 %slice-start.2 = ((s8[16777216]{0:T(1024)(128)(4,1)}), s8[4194304]{0:T(1024)(128)(4,1)S(1)}, s32[]{:S(2)}) async-start(s8[16777216]{0:T(1024)(128)(4,1)} %bitcast.140), calls=%async_computation.5 | async-start | bytes 8388608
  93.3 8.2 %slice-start.3 = ((s8[16777216]{0:T(1024)(128)(4,1)}), s8[4194304]{0:T(1024)(128)(4,1)S(1)}, s32[]{:S(2)}) async-start(s8[16777216]{0:T(1024)(128)(4,1)} %bitcast.140), calls=%async_computation.6 | async-start | bytes 8388608
  94.6 27.0 %collective-permute-start = (f32[256,512]{0,1:T(8,128)S(1)}, f32[256,512]{0,1:T(8,128)S(1)}, u32[]{:S(2)}, u32[]{:S(2)}) collective-permute-start(f32[256,512]{0,1:T(8,128)S(1)} %fusion.10), channel_id=1, source_target_pairs={{0,32},{32,64},{64,96},{96,0},{1,33},{33,65},{65,97},{97,1},{2,34}... | collective-permute-start | bytes 1572872 | tf_op jit(solution)/shard_map/ppermute | solution.py:73
  96.1 26.0 %collective-permute-start.1 = (f32[256,512]{0,1:T(8,128)S(1)}, f32[256,512]{0,1:T(8,128)S(1)}, u32[]{:S(2)}, u32[]{:S(2)}) collective-permute-start(f32[256,512]{0,1:T(8,128)S(1)} %fusion.10), channel_id=1, source_target_pairs={{0,64},{32,96},{64,0},{96,32},{1,65},{33,97},{65,1},{97,33},{2,66}... | collective-permute-start | bytes 1572872 | tf_op jit(solution)/shard_map/ppermute | solution.py:73
  98.8 23.3 %collective-permute-start.2 = (f32[256,512]{0,1:T(8,128)S(1)}, f32[256,512]{0,1:T(8,128)}, u32[]{:S(2)}, u32[]{:S(2)}) collective-permute-start(f32[256,512]{0,1:T(8,128)S(1)} %fusion.10), channel_id=1, source_target_pairs={{0,96},{32,0},{64,32},{96,64},{1,97},{33,1},{65,33},{97,65},{2,98}... | collective-permute-start | bytes 1572872 | tf_op jit(solution)/shard_map/ppermute | solution.py:73
  132.3 0.7 copy-start
  212.2 1.6 copy-start.1
  214.1 2.1 copy-start.2
Sparse Core Ops, SparseCore 0:
  9.6 75.2 all-gather.2
  132.5 79.6 reduce-scatter.1

commit v9 on v8

--- a/solution.py
+++ b/solution.py
@@ -73,20 +73,21 @@
         pivot_part = pivot_part + lax.ppermute(extra, "row", pairs)
     main_rows = col_rows + (extra[:1, :1] * 0).astype(col_rows.dtype)[None]
     main = jnp.einsum(
-        "cutk,cmk->cutm", tiles4, main_rows, preferred_element_type=jnp.float32
+        "cutk,cmk->cumt", tiles4, main_rows, preferred_element_type=jnp.float32
     )
-    main = main.reshape(n_child * tiles_child, TILE, n_cols)
+    main = main.reshape(n_child * tiles_child, n_cols, TILE)
     child_base = (jnp.arange(n_child, dtype=jnp.int32) * tiles_child)[:, None]
     flat_order = (order + child_base).reshape(n_child, row_count, per_group)
     flat_order = jnp.transpose(flat_order, (1, 0, 2)).reshape(-1)
     flat_order = flat_order + (pivot_part[0, 0] * 0).astype(jnp.int32)
     main = jnp.take(main, flat_order, axis=0, mode="clip")
     mine = lax.psum_scatter(
-        main.reshape(row_count * n_child * per_group * TILE, n_cols),
+        main.reshape(row_count * n_child * per_group * n_cols, TILE),
         "row",
         scatter_dimension=0,
         tiled=True,
-    ).reshape(n_child, per_group * TILE, n_cols)
+    ).reshape(n_child, per_group, n_cols, TILE)
+    mine = jnp.transpose(mine, (0, 1, 3, 2))
 
     own_w = tiles_block * TILE
     lead_rows = NPAN * block_size
@@ -101,7 +102,7 @@
     my_tiles = lax.dynamic_slice_in_dim(order, row_index * per_group, per_group, axis=1)
     my_root = jnp.take_along_axis(child_tiles, my_tiles, axis=1)
     my_local = (my_root * TILE // block_size) // row_count * tiles_block + my_root % tiles_block
-    mine4 = mine.reshape(n_child, per_group, TILE, n_cols)
+    mine4 = mine
     front_loc = jnp.zeros((loc_tiles, TILE, n_cols), jnp.float32)
     for child in range(n_child):
         for slot in range(per_group):

time: 229 us -> 248 us (1.083)
  other arithmetic: 59.8 us -> 71.1 us
  waiting for transfers between devices: 34.4 us -> 43.4 us
    dynamic_update_slice x7, other arithmetic: 0.39 us -> 11.7 us  [shards(): lax.dynamic_update_index_in_dim(front_loc, here + mine4[child, slot][None...]
    ppermute x3, waiting for transfers between devices: 0.53 us -> 9.55 us  [shards(): pivot_part = pivot_part + lax.ppermute(extra, 'row', pairs)]
    reshape x1 -> x0, local copies, waits for them, and re-layouts: 9.01 us -> none  [shards(): main = main.reshape(n_child * tiles_child, TILE, n_cols)]
    dynamic_update_slice x1 -> x2, local copies, waits for them, and re-layouts: 0.02 us -> 6.09 us  [shards(): lax.dynamic_update_index_in_dim(front_loc, here + mine4[child, slot][None...]
  transfers between devices with their start and end apart: 5 -> 5, of which waited for: 3 -> 3; matrix products, arithmetic and copies ran while one was open for 38% -> 32% of each run, Pallas kernels for 0% -> 0%
where the time goes in v9:
time: 248 us; the launch traced here: 247 us
  other arithmetic  71.1 us (29%)
  between operations  46.7 us (19%)
  waiting for transfers between devices  43.4 us (18%)
  local copies, waits for them, and re-layouts  32.3 us (13%)
  blocking collectives  25.9 us (10%)
  matrix products  21.5 us (9%)
  starting transfers between devices  5.7 us (2%)
    another operation x6, other arithmetic, shards(): lead = jnp.tril(jnp.linalg.cholesky(front00))  34 us
    all_gather x1, waiting for transfers between devices, shards(): gathered = lax.all_gather(child_factors, 'col', axis=1, tiled=True)  31.9 us
    all_gather x1, blocking collectives, shards(): full_diag = lax.all_gather(root_diag, 'col', axis=0, tiled=True)  25.9 us
    another operation x3, other arithmetic, shards(): lax.linalg.triangular_solve(lead, jnp.eye(lead_rows, dtype=jnp.float32),...  19.9 us
    dynamic_update_slice x7, other arithmetic, shards(): lax.dynamic_update_index_in_dim(front_loc, here + mine4[child, slot][None...  11.7 us
    dot_general x1, matrix products, shards(): jnp.einsum('cutk,cmk->cumt', tiles4, main_rows, preferred_element_type=jn...  11.1 us
    ppermute x3, waiting for transfers between devices, shards(): pivot_part = pivot_part + lax.ppermute(extra, 'row', pairs)  9.55 us
    gather x1, local copies, waits for them, and re-layouts, shards(): main = jnp.take(main, flat_order, axis=0, mode='clip')  7.7 us
  transfers between devices with their start and end apart: 5, of which 3 were waited for; matrix products, arithmetic and copies ran while one was open for 32% of the time, Pallas kernels for 0%

profile of v9, /device:TPU:0, one launch (start us, length us, event | category | flops | bytes accessed | tf_op | source)
XLA Modules:
  0.0 246.6 jit_solution(9589057995130155579)
XLA Ops:
  6.5 0.7 all-gather.3.cloned.1.call-update
  7.3 25.9 %all-gather = f32[32,1,256]{2,1,0:T(1,128)S(1)} all-gather(f32[1,1,256]{2,1,0:T(1,128)} %bitcast.162), channel_id=1, replica_groups=mesh['row'=4,'col'=32] {'col'}, dimensions={0}, use_global_device_ids=true | all-gather | bytes 33792 | tf_op jit(solution)/shard_map/all_gather | solution.py:32
  33.2 0.5 slice.208
  34.4 0.9 fusion.51
  35.3 0.7 fusion.62
  46.0 0.9 compare_reduce_fusion
  47.0 0.7 fusion.54
  53.1 31.9 %all-gather.3.cloned.1.call-done = bf16[2,2048,2048]{2,1,0:T(8,128)(2,1)} async-done(((bf16[2,64,2048]{2,1,0:T(8,128)(2,1)}), bf16[2,2048,2048]{2,1,0:T(8,128)(2,1)}) %all-gather.3.cloned.1.call-update) | async-done | bytes 16777232 | tf_op jit(solution)/shard_map/all_gather | solution.py:29
  85.0 6.7 %fusion.60 = (bf16[1,2048,2048]{2,1,0:T(8,128)(2,1)S(1)}, bf16[1,2048,2048]{2,1,0:T(8,128)(2,1)S(1)}) fusion(bf16[2,2048,2048]{2,1,0:T(8,128)(2,1)} %all-gather.3.cloned.1.call-done), kind=kLoop, calls=%fused_computation.146 | loop fusion | bytes 33554432 | tf_op jit(solution)/shard_map/slice | solution.py:55
  92.6 0.6 maximum_select_fusion
  93.2 1.3 fusion.10
  94.5 1.5 collective-permute-start
  96.1 2.7 %collective-permute-start.1 = (f32[256,512]{0,1:T(8,128)S(1)}, f32[256,512]{0,1:T(8,128)S(1)}, u32[]{:S(2)}, u32[]{:S(2)}) collective-permute-start(f32[256,512]{0,1:T(8,128)S(1)} %fusion.10), channel_id=1, source_target_pairs={{0,64},{32,96},{64,0},{96,32},{1,65},{33,97},{65,1},{97,33},{2,66}... | collective-permute-start | bytes 1572872 | tf_op jit(solution)/shard_map/ppermute | solution.py:73
  98.7 1.5 collective-permute-start.2
  100.2 0.5 slice.213
  101.4 11.1 %fusion = f32[2,512,16,128]{3,1,2,0:T(8,128)} fusion(bf16[2,16,128,2048]{3,2,1,0:T(8,128)(2,1)S(1)} %bitcast.144, bf16[2,512,2048]{2,1,0:T(8,128)(2,1)S(1)} %maximum_select_fusion, bf16[]{:T(256)} %bitcast.26), kind=kOutput, calls=%fused_computation.5 | convolution fusion | flops 8598323200 | bytes 29360130 | tf_op jit(solution)/shard_map/cutk,cmk->cumt/dot_general | solution.py:75
  112.5 9.5 %collective-permute-done.1 = f32[256,512]{0,1:T(8,128)S(1)} collective-permute-done((f32[256,512]{0,1:T(8,128)S(1)}, f32[256,512]{0,1:T(8,128)S(1)}, u32[]{:S(2)}, u32[]{:S(2)}) %collective-permute-start.1) | collective-permute-done | bytes 524320 | tf_op jit(solution)/shard_map/ppermute | solution.py:73
  122.0 1.2 add_add_fusion
  123.2 0.5 slice.214
  124.5 7.7 %gather_fusion = f32[32,512,128]{2,1,0:T(8,128)} fusion(f32[32,512,128]{2,1,0:T(8,128)} %bitcast.147, s32[1024]{0:T(1024)S(1)} %pad_clamp_fusion), kind=kCustom, calls=%fused_computation | custom fusion | bytes 16777344 | tf_op jit(solution)/shard_map/jit(_take)/gather | solution.py:83
  132.5 0.5 copy-done
  132.9 0.7 gather_fusion.1
  133.8 0.6 fusion.61
  149.3 11.7 %cholesky.49 = f32[128,128]{1,0:T(8,128)S(1)} custom-call(f32[128,128]{1,0:T(8,128)S(1)} %cholesky.115), custom_call_target="Cholesky" | custom-call | tf_op jit(solution)/shard_map/jit(cholesky)/cholesky | solution.py:96
  161.1 9.8 %custom-call.14 = f32[1,128,128]{1,2,0:T(8,128)S(1)} custom-call(f32[1,128,128]{2,1,0:T(8,128)S(1)} %get-tuple-element.52), custom_call_target="InvertDiagBlocksLowerTriangular" | custom-call | tf_op jit(solution)/shard_map/jit(cholesky)/cholesky | solution.py:96
  171.5 11.7 %cholesky.103 = f32[128,128]{1,0:T(8,128)S(1)} custom-call(f32[128,128]{1,0:T(8,128)S(1)} %convolution_subtract_fusion.2), custom_call_target="Cholesky" | custom-call | tf_op jit(solution)/shard_map/jit(cholesky)/cholesky | solution.py:96
  183.4 0.7 compare_reduce_fusion.1
  185.5 4.2 %while.1 = (s32[]{:T(128)}, f32[256,256]{0,1:T(8,128)S(1)}, s32[2,2]{1,0:T(2,128)S(1)}, f32[2,128,128]{2,1,0:T(8,128)S(1)}, s32[]{:T(128)}) while((s32[]{:T(128)}, f32[256,256]{0,1:T(8,128)S(1)}, s32[2,2]{1,0:T(2,128)S(1)}, f32[2,128,128]{2,1,0:T(8,128)S(1)}, s32[]{:T(128)}) %tuple.48), condition=%wide.while_cond, body=%wide.while_body.sunk | while | flops 2 | bytes 393321 | solution.py:97
  185.5 0.6 fusion.72
  186.1 1.4 dynamic-slice.7
  187.6 0.6 fusion.72
  188.2 1.4 dynamic-slice.7
  189.6 19.9 %custom-call.15 = f32[2,128,128]{1,2,0:T(8,128)S(1)} custom-call(f32[2,128,128]{2,1,0:T(8,128)S(1)} %get-tuple-element.12), custom_call_target="InvertDiagBlocksLowerTriangular" | custom-call | tf_op jit(solution)/shard_map/triangular_solve | solution.py:97
  210.3 0.3 fusion.34
  210.6 0.4 fusion.13
  211.0 1.2 reduce-scatter.2.cloned.1.call-done
  212.2 2.4 broadcast_in_dim.119
  214.6 0.7 fusion.28
  215.3 1.7 fusion.27
  217.0 1.7 fusion.25
  218.7 1.7 fusion.23
  220.3 1.7 fusion.21
  222.0 1.7 fusion.19
  223.7 1.7 fusion.17
  225.4 1.7 fusion.15
  227.0 5.4 %copy.54 = f32[16,128,512]{2,1,0:T(8,128)} copy(f32[16,128,512]{1,2,0:T(8,128)} %fusion.15) | data formatting | bytes 8388608 | tf_op jit(solution)/shard_map/jit(dynamic_update_index_in_dim)/dynamic_update_slice | solution.py:111
  232.4 3.5 %bitcast_select_fusion = (f32[2048,256]{1,0:T(8,128)S(1)}, f32[2048,256]{1,0:T(8,128)S(1)}) fusion(f32[256,256]{1,0:T(8,128)S(1)} %copy.51, pred[2048]{0:T(1024)(128)(4,1)S(1)} %fusion.50, f32[256,128]{0,1:T(8,128)S(1)} %fusion.34, f32[256,128]{0,1:T(8,128)S(1)} %fusion.31, f32[2048,512]{1,0:T(8,128)} %bitcast.140), kind=kOutput, calls=%fused_computation.18 | convolution fusion | flops 1611202560 | bytes 6817792 | tf_op jit(solution)/shard_map/dot_general | solution.py:124
  235.9 3.8 %fusion.4 = f32[2048,256]{1,0:T(8,128)} fusion(f32[2048,256]{1,0:T(8,128)S(1)} %get-tuple-element.69, f32[2048,256]{1,0:T(8,128)S(1)} %get-tuple-element.70, f32[256,256]{1,0:T(8,128)S(1)} %fusion.13, f32[2048,512]{1,0:T(8,128)S(1)} %bitcast.141, f32[256]{0:T(256)S(1)} %copy-done.3, s32[256]{0:T(256)S(1)} %iota_add_fusion, s32[2048]{0:T(1024)S(1)} %fusion.47, ...), kind=kOutput, calls=%fused_computation.10 | convolution fusion | flops 1613758464 | bytes 8663041 | tf_op jit(solution)/shard_map/dot_general | solution.py:126
  (75 shorter events, 4.1 us)
Async XLA Ops:
  6.5 78.4 %all-gather.3.cloned.1.call-start = ((), (), s32[]{:S(2)}) async-start(), calls=%async_computation.1 | async-start | bytes 17301504 | tf_op jit(solution)/shard_map/all_gather | solution.py:29
  7.3 205.0 %reduce-scatter.2.cloned.1.call-start = ((), (), s32[]{:S(2)}) async-start(), calls=%async_computation.2 | async-start | bytes 10485760 | tf_op jit(solution)/shard_map/reduce_scatter | solution.py:84
  91.7 9.6 %slice-start = ((s8[16777216]{0:T(1024)(128)(4,1)}), s8[4194304]{0:T(1024)(128)(4,1)S(1)}, s32[]{:S(2)}) async-start(s8[16777216]{0:T(1024)(128)(4,1)} %bitcast.142), calls=%async_computation.3 | async-start | bytes 8388608
  92.1 9.2 %slice-start.1 = ((s8[16777216]{0:T(1024)(128)(4,1)}), s8[4194304]{0:T(1024)(128)(4,1)S(1)}, s32[]{:S(2)}) async-start(s8[16777216]{0:T(1024)(128)(4,1)} %bitcast.142), calls=%async_computation.4 | async-start | bytes 8388608
  92.6 8.8 %slice-start.2 = ((s8[16777216]{0:T(1024)(128)(4,1)}), s8[4194304]{0:T(1024)(128)(4,1)S(1)}, s32[]{:S(2)}) async-start(s8[16777216]{0:T(1024)(128)(4,1)} %bitcast.142), calls=%async_computation.5 | async-start | bytes 8388608
  93.2 8.2 %slice-start.3 = ((s8[16777216]{0:T(1024)(128)(4,1)}), s8[4194304]{0:T(1024)(128)(4,1)S(1)}, s32[]{:S(2)}) async-start(s8[16777216]{0:T(1024)(128)(4,1)} %bitcast.142), calls=%async_computation.6 | async-start | bytes 8388608
  94.5 17.9 %collective-permute-start = (f32[256,512]{0,1:T(8,128)S(1)}, f32[256,512]{0,1:T(8,128)S(1)}, u32[]{:S(2)}, u32[]{:S(2)}) collective-permute-start(f32[256,512]{0,1:T(8,128)S(1)} %fusion.10), channel_id=1, source_target_pairs={{0,32},{32,64},{64,96},{96,0},{1,33},{33,65},{65,97},{97,1},{2,34}... | collective-permute-start | bytes 1572872 | tf_op jit(solution)/shard_map/ppermute | solution.py:73
  96.1 26.0 %collective-permute-start.1 = (f32[256,512]{0,1:T(8,128)S(1)}, f32[256,512]{0,1:T(8,128)S(1)}, u32[]{:S(2)}, u32[]{:S(2)}) collective-permute-start(f32[256,512]{0,1:T(8,128)S(1)} %fusion.10), channel_id=1, source_target_pairs={{0,64},{32,96},{64,0},{96,32},{1,65},{33,97},{65,1},{97,33},{2,66}... | collective-permute-start | bytes 1572872 | tf_op jit(solution)/shard_map/ppermute | solution.py:73
  98.7 23.3 %collective-permute-start.2 = (f32[256,512]{0,1:T(8,128)S(1)}, f32[256,512]{0,1:T(8,128)}, u32[]{:S(2)}, u32[]{:S(2)}) collective-permute-start(f32[256,512]{0,1:T(8,128)S(1)} %fusion.10), channel_id=1, source_target_pairs={{0,96},{32,0},{64,32},{96,64},{1,97},{33,1},{65,33},{97,65},{2,98}... | collective-permute-start | bytes 1572872 | tf_op jit(solution)/shard_map/ppermute | solution.py:73
  132.2 0.7 copy-start
  212.2 2.4 copy-start.2
  232.4 3.5 %copy-start.1 = (f32[16,128,512]{2,1,0:T(8,128)S(1)}, f32[16,128,512]{2,1,0:T(8,128)}, u32[]{:S(2)}) copy-start(f32[16,128,512]{2,1,0:T(8,128)} %copy.54) | copy-start | bytes 12582916
  232.4 3.5 %copy-start.3 = (f32[256]{0:T(256)S(1)}, f32[256]{0:T(256)}, u32[]{:S(2)}) copy-start(f32[256]{0:T(256)} %param.5) | copy-start | bytes 3076
Sparse Core Ops, SparseCore 0:
  9.6 75.2 all-gather.2
  132.4 79.7 reduce-scatter.1

commit v10 on v8

--- a/solution.py
+++ b/solution.py
@@ -26,7 +26,17 @@
     tiles_block = block_size // TILE
     loc_tiles = loc_rows // TILE
 
-    gathered = lax.all_gather(child_factors, "col", axis=1, tiled=True)
+    parity = [[c for c in range(col_count) if c % 2 == p] for p in range(2)]
+    half = lax.all_gather(child_factors, "col", axis=1, tiled=True, axis_index_groups=parity)
+    other = lax.ppermute(half, "col", [(c, c ^ 1) for c in range(col_count)])
+    core = col_index % 2
+    even = jnp.where(core == 0, half, other)
+    odd = jnp.where(core == 0, other, half)
+    n_rows_dev = child_factors.shape[1]
+    gathered = jnp.stack(
+        [even.reshape(2, -1, n_rows_dev, even.shape[2]), odd.reshape(2, -1, n_rows_dev, odd.shape[2])],
+        axis=2,
+    ).reshape(2, -1, even.shape[2])
     k_loc = gathered.shape[2]
     tiles4 = gathered.reshape(n_child, tiles_child, TILE, k_loc)
     full_diag = lax.all_gather(root_diag, "col", axis=0, tiled=True)

time: 229 us -> 270 us (1.18)
  waiting for transfers between devices: 34.4 us -> 76.4 us
  local copies, waits for them, and re-layouts: 34.5 us -> 18.9 us
  other arithmetic: 59.8 us -> 73.6 us
  matrix products: 19.9 us -> 23.4 us
    all_gather x1, waiting for transfers between devices: 32 us -> 75.6 us  [shards(): lax.all_gather(child_factors, 'col', axis=1, tiled=True, axis_index_group...]
    reshape x1 -> x0, local copies, waits for them, and re-layouts: 9.01 us -> none  [shards(): main = main.reshape(n_child * tiles_child, TILE, n_cols)]
    another operation x0 -> x2, other arithmetic: none -> 8.31 us  [shards(): jnp.stack([even.reshape(2, -1, n_rows_dev, even.shape[2]), odd.reshape(2,...]
    slice x1 -> x0, local copies, waits for them, and re-layouts: 6.74 us -> none  [shards(): tiles4[child]]
    select_n x0 -> x1, other arithmetic: none -> 6.49 us  [shards(): even = jnp.where(core == 0, half, other)]
    dot_general x1, matrix products: 11.1 us -> 14.5 us  [shards(): jnp.einsum('cutk,cmk->cutm', tiles4, main_rows, preferred_element_type=jn...]
  transfers between devices with their start and end apart: 5 -> 6, of which waited for: 3 -> 1; matrix products, arithmetic and copies ran while one was open for 38% -> 33% of each run, Pallas kernels for 0% -> 0%
where the time goes in v10:
time: 270 us; the launch traced here: 268 us
  waiting for transfers between devices  76.4 us (28%)
  other arithmetic  73.6 us (27%)
  between operations  46.5 us (17%)
  blocking collectives  23.9 us (9%)
  matrix products  23.4 us (9%)
  local copies, waits for them, and re-layouts  18.9 us (7%)
  starting transfers between devices  5.72 us (2%)
    all_gather x1, waiting for transfers between devices, shards(): lax.all_gather(child_factors, 'col', axis=1, tiled=True, axis_index_group...  75.6 us
    another operation x6, other arithmetic, shards(): lead = jnp.tril(jnp.linalg.cholesky(front00))  34 us
    all_gather x1, blocking collectives, shards(): full_diag = lax.all_gather(root_diag, 'col', axis=0, tiled=True)  23.9 us
    another operation x3, other arithmetic, shards(): lax.linalg.triangular_solve(lead, jnp.eye(lead_rows, dtype=jnp.float32),...  19.9 us
    dot_general x1, matrix products, shards(): jnp.einsum('cutk,cmk->cutm', tiles4, main_rows, preferred_element_type=jn...  14.5 us
    another operation x2, other arithmetic, shards(): jnp.stack([even.reshape(2, -1, n_rows_dev, even.shape[2]), odd.reshape(2,...  8.31 us
    gather x1, local copies, waits for them, and re-layouts, shards(): main = jnp.take(main, flat_order, axis=0, mode='clip')  7.69 us
    select_n x1, other arithmetic, shards(): even = jnp.where(core == 0, half, other)  6.49 us
  transfers between devices with their start and end apart: 6, of which 1 were waited for; matrix products, arithmetic and copies ran while one was open for 33% of the time, Pallas kernels for 0%

profile of v10, /device:TPU:0, one launch (start us, length us, event | category | flops | bytes accessed | tf_op | source)
XLA Modules:
  0.0 268.4 jit_solution(6637157467399233317)
XLA Ops:
  6.5 0.7 all-gather.3.cloned.1.call-update
  7.3 75.6 %all-gather.3.cloned.1.call-done = bf16[2,1024,2048]{2,1,0:T(8,128)(2,1)} async-done(((bf16[2,64,2048]{2,1,0:T(8,128)(2,1)}), bf16[2,1024,2048]{2,1,0:T(8,128)(2,1)}) %all-gather.3.cloned.1.call-update) | async-done | bytes 8388624 | tf_op jit(solution)/shard_map/all_gather | solution.py:30
  82.9 23.9 %all-gather = f32[32,1,256]{2,1,0:T(1,128)S(1)} all-gather(f32[1,1,256]{2,1,0:T(1,128)} %bitcast.166), channel_id=1, replica_groups=mesh['row'=4,'col'=32] {'col'}, dimensions={0}, use_global_device_ids=true | all-gather | bytes 33792 | tf_op jit(solution)/shard_map/all_gather | solution.py:42
  106.9 0.5 slice.209
  108.0 0.9 fusion.53
  108.9 0.7 fusion.63
  119.5 0.9 compare_reduce_fusion
  120.5 0.7 fusion.56
  121.2 0.2 convert_reduce_fusion
  126.6 6.5 %broadcast_select_fusion.1 = (bf16[2,1024,2048]{2,1,0:T(8,128)(2,1)S(1)}, bf16[2,1024,2048]{2,1,0:T(8,128)(2,1)S(1)}) fusion(bf16[2,1024,2048]{2,1,0:T(8,128)(2,1)} %all-gather.3.cloned.1.call-done, bf16[2,1024,2048]{2,1,0:T(8,128)(2,1)} %collective-permute-done, pred[]{:T(512)S(6)} %eq.66), kind=kLoop, calls=%fused_computation.12 | loop fusion | flops 8388608 | bytes 33554432 | tf_op jit(solution)/shard_map/jit(_where)/select_n | solution.py:33
  133.1 1.5 fusion
  134.6 0.2 constant_dynamic-slice_fusion.9
  134.7 0.3 pad_maximum_fusion.1
  135.0 0.2 constant_dynamic-slice_fusion.5
  135.2 0.3 pad_maximum_fusion.2
  135.5 0.6 maximum_select_fusion
  136.1 1.3 fusion.12
  137.4 1.5 collective-permute-start.1
  138.9 2.7 collective-permute-start.2
  141.6 1.5 collective-permute-start.3
  143.1 6.8 %pad_maximum_fusion = bf16[2,16,2,64,2048]{4,3,2,1,0:T(8,128)(2,1)} fusion(bf16[2,16,1,64,2048]{4,3,2,1,0:T(8,128)(2,1)S(1)} %bitcast.144, bf16[2,16,1,64,2048]{4,3,2,1,0:T(8,128)(2,1)S(1)} %bitcast.142), kind=kLoop, calls=%fused_computation.6 | loop fusion | flops 8388608 | bytes 33554432 | tf_op jit(solution)/shard_map/stack | solution.py:36
  149.9 0.5 slice.215
  150.9 14.5 %fusion.2 = f32[2,16,128,512]{3,2,1,0:T(8,128)} fusion(bf16[2,16,128,2048]{3,2,1,0:T(8,128)(2,1)} %bitcast.148, bf16[2,512,2048]{2,1,0:T(8,128)(2,1)S(1)} %maximum_select_fusion, bf16[]{:T(256)} %bitcast.31), kind=kOutput, calls=%fused_computation.14 | convolution fusion | flops 8592031744 | bytes 29360130 | tf_op jit(solution)/shard_map/cutk,cmk->cutm/dot_general | solution.py:85
  165.6 0.6 slice.216
  167.1 7.7 %gather_fusion = f32[32,128,512]{2,1,0:T(8,128)} fusion(f32[32,128,512]{2,1,0:T(8,128)} %bitcast.151, s32[1024]{0:T(1024)S(1)} %pad_clamp_fusion), kind=kCustom, calls=%fused_computation | custom fusion | bytes 16777344 | tf_op jit(solution)/shard_map/jit(_take)/gather | solution.py:93
  175.0 0.5 copy-done
  175.5 0.7 gather_fusion.1
  176.3 0.7 fusion.62
  191.9 11.7 %cholesky.49 = f32[128,128]{1,0:T(8,128)S(1)} custom-call(f32[128,128]{1,0:T(8,128)S(1)} %cholesky.115), custom_call_target="Cholesky" | custom-call | tf_op jit(solution)/shard_map/jit(cholesky)/cholesky | solution.py:105
  203.7 9.8 %custom-call.14 = f32[1,128,128]{1,2,0:T(8,128)S(1)} custom-call(f32[1,128,128]{2,1,0:T(8,128)S(1)} %get-tuple-element.54), custom_call_target="InvertDiagBlocksLowerTriangular" | custom-call | tf_op jit(solution)/shard_map/jit(cholesky)/cholesky | solution.py:105
  213.6 0.2 fusion.38
  213.9 0.3 convolution_subtract_fusion.2
  214.1 11.7 %cholesky.103 = f32[128,128]{1,0:T(8,128)S(1)} custom-call(f32[128,128]{1,0:T(8,128)S(1)} %convolution_subtract_fusion.2), custom_call_target="Cholesky" | custom-call | tf_op jit(solution)/shard_map/jit(cholesky)/cholesky | solution.py:105
  226.0 0.7 compare_reduce_fusion.1
  228.1 4.2 %while.1 = (s32[]{:T(128)}, f32[256,256]{0,1:T(8,128)S(1)}, s32[2,2]{1,0:T(2,128)S(1)}, f32[2,128,128]{2,1,0:T(8,128)S(1)}, s32[]{:T(128)}) while((s32[]{:T(128)}, f32[256,256]{0,1:T(8,128)S(1)}, s32[2,2]{1,0:T(2,128)S(1)}, f32[2,128,128]{2,1,0:T(8,128)S(1)}, s32[]{:T(128)}) %tuple.49), condition=%wide.while_cond, body=%wide.while_body.sunk | while | flops 2 | bytes 393321 | solution.py:106
  228.1 0.6 fusion.73
  228.8 1.3 dynamic-slice.7
  230.2 0.6 fusion.73
  230.9 1.3 dynamic-slice.7
  232.3 19.9 %custom-call.15 = f32[2,128,128]{1,2,0:T(8,128)S(1)} custom-call(f32[2,128,128]{2,1,0:T(8,128)S(1)} %get-tuple-element.12), custom_call_target="InvertDiagBlocksLowerTriangular" | custom-call | tf_op jit(solution)/shard_map/triangular_solve | solution.py:106
  252.3 0.3 fusion.33
  252.6 0.3 convolution_subtract_fusion.1
  252.9 0.3 fusion.36
  253.3 0.4 fusion.15
  253.7 0.5 broadcast_in_dim.119
  254.3 1.1 copy-done.1
  255.8 1.9 bitcast_select_fusion
  257.7 3.8 %fusion.6 = f32[2048,256]{1,0:T(8,128)} fusion(f32[2048,256]{1,0:T(8,128)S(1)} %get-tuple-element.71, f32[2048,256]{1,0:T(8,128)S(1)} %get-tuple-element.72, f32[256,256]{1,0:T(8,128)S(1)} %fusion.15, f32[2048,512]{1,0:T(8,128)S(1)} %bitcast.147, f32[256]{0:T(256)S(1)} %copy-done.2, s32[256]{0:T(256)S(1)} %iota_add_fusion, s32[2048]{0:T(1024)S(1)} %fusion.49, ...), kind=kOutput, calls=%fused_computation.19 | convolution fusion | flops 1613758464 | bytes 8663041 | tf_op jit(solution)/shard_map/dot_general | solution.py:135
  (67 shorter events, 2.6 us)
Async XLA Ops:
  6.5 76.4 %all-gather.3.cloned.1.call-start = ((), (), s32[]{:S(2)}) async-start(), calls=%async_computation.1 | async-start | bytes 8912896 | tf_op jit(solution)/shard_map/all_gather | solution.py:30
  7.3 246.5 %reduce-scatter.2.cloned.1.call-start = ((), (), s32[]{:S(2)}) async-start(), calls=%async_computation.2 | async-start | bytes 10485760 | tf_op jit(solution)/shard_map/reduce_scatter | solution.py:94
  82.9 43.6 %collective-permute-start = (bf16[2,1024,2048]{2,1,0:T(8,128)(2,1)}, bf16[2,1024,2048]{2,1,0:T(8,128)(2,1)}, u32[]{:S(2)}, u32[]{:S(2)}) collective-permute-start(bf16[2,1024,2048]{2,1,0:T(8,128)(2,1)} %all-gather.3.cloned.1.call-done), channel_id=1, source_target_pairs={{0,1},{1,0},{2,3},{3,2},{4,5},{5,4},{6,7},{7,6},{8,9},{9,8},{10,11... | collective-permute-start | bytes 25165832 | tf_op jit(solution)/shard_map/ppermute | solution.py:31
  137.4 28.1 %collective-permute-start.1 = (f32[256,512]{0,1:T(8,128)S(1)}, f32[256,512]{0,1:T(8,128)S(1)}, u32[]{:S(2)}, u32[]{:S(2)}) collective-permute-start(f32[256,512]{0,1:T(8,128)S(1)} %fusion.12), channel_id=1, source_target_pairs={{0,32},{32,64},{64,96},{96,0},{1,33},{33,65},{65,97},{97,1},{2,34}... | collective-permute-start | bytes 1572872 | tf_op jit(solution)/shard_map/ppermute | solution.py:83
  138.9 26.5 %collective-permute-start.2 = (f32[256,512]{0,1:T(8,128)S(1)}, f32[256,512]{0,1:T(8,128)S(1)}, u32[]{:S(2)}, u32[]{:S(2)}) collective-permute-start(f32[256,512]{0,1:T(8,128)S(1)} %fusion.12), channel_id=1, source_target_pairs={{0,64},{32,96},{64,0},{96,32},{1,65},{33,97},{65,1},{97,33},{2,66}... | collective-permute-start | bytes 1572872 | tf_op jit(solution)/shard_map/ppermute | solution.py:83
  141.6 23.9 %collective-permute-start.3 = (f32[256,512]{0,1:T(8,128)S(1)}, f32[256,512]{0,1:T(8,128)S(1)}, u32[]{:S(2)}, u32[]{:S(2)}) collective-permute-start(f32[256,512]{0,1:T(8,128)S(1)} %fusion.12), channel_id=1, source_target_pairs={{0,96},{32,0},{64,32},{96,64},{1,97},{33,1},{65,33},{97,65},{2,98}... | collective-permute-start | bytes 1572872 | tf_op jit(solution)/shard_map/ppermute | solution.py:83
  174.8 0.7 copy-start
  253.7 1.6 copy-start.1
  255.7 2.1 copy-start.2
Sparse Core Ops, SparseCore 0:
  9.5 73.4 all-gather.2
  174.9 78.0 reduce-scatter.1

commit v11 on v9

--- a/solution.py
+++ b/solution.py
@@ -79,7 +79,6 @@
     child_base = (jnp.arange(n_child, dtype=jnp.int32) * tiles_child)[:, None]
     flat_order = (order + child_base).reshape(n_child, row_count, per_group)
     flat_order = jnp.transpose(flat_order, (1, 0, 2)).reshape(-1)
-    flat_order = flat_order + (pivot_part[0, 0] * 0).astype(jnp.int32)
     main = jnp.take(main, flat_order, axis=0, mode="clip")
     mine = lax.psum_scatter(
         main.reshape(row_count * n_child * per_group * n_cols, TILE),
@@ -87,7 +86,7 @@
         scatter_dimension=0,
         tiled=True,
     ).reshape(n_child, per_group, n_cols, TILE)
-    mine = jnp.transpose(mine, (0, 1, 3, 2))
+    mine = lax.optimization_barrier(jnp.transpose(mine, (0, 1, 3, 2)))
 
     own_w = tiles_block * TILE
     lead_rows = NPAN * block_size

time: 248 us -> 282 us (1.14)
  waiting for transfers between devices: 43.4 us -> 77.4 us
    ppermute x3, waiting for transfers between devices: 9.55 us -> 44.7 us  [shards(): pivot_part = pivot_part + lax.ppermute(extra, 'row', pairs)]
  transfers between devices with their start and end apart: 5 -> 5, of which waited for: 3 -> 3; matrix products, arithmetic and copies ran while one was open for 32% -> 24% of each run, Pallas kernels for 0% -> 0%
where the time goes in v11:
time: 282 us; the launch traced here: 280 us
  waiting for transfers between devices  77.4 us (27%)
  other arithmetic  69.9 us (25%)
  between operations  46.6 us (17%)
  local copies, waits for them, and re-layouts  33.3 us (12%)
  blocking collectives  25.9 us (9%)
  matrix products  21.4 us (8%)
  starting transfers between devices  5.74 us (2%)
    ppermute x3, waiting for transfers between devices, shards(): pivot_part = pivot_part + lax.ppermute(extra, 'row', pairs)  44.7 us
    another operation x6, other arithmetic, shards(): lead = jnp.tril(jnp.linalg.cholesky(front00))  34 us
    all_gather x1, waiting for transfers between devices, shards(): gathered = lax.all_gather(child_factors, 'col', axis=1, tiled=True)  31.9 us
    all_gather x1, blocking collectives, shards(): full_diag = lax.all_gather(root_diag, 'col', axis=0, tiled=True)  25.9 us
    another operation x3, other arithmetic, shards(): lax.linalg.triangular_solve(lead, jnp.eye(lead_rows, dtype=jnp.float32),...  19.7 us
    dynamic_update_slice x7, other arithmetic, shards(): lax.dynamic_update_index_in_dim(front_loc, here + mine4[child, slot][None...  11.7 us
    dot_general x1, matrix products, shards(): jnp.einsum('cutk,cmk->cumt', tiles4, main_rows, preferred_element_type=jn...  11 us
    gather x1, local copies, waits for them, and re-layouts, shards(): main = jnp.take(main, flat_order, axis=0, mode='clip')  7.69 us
  transfers between devices with their start and end apart: 5, of which 3 were waited for; matrix products, arithmetic and copies ran while one was open for 24% of the time, Pallas kernels for 0%

profile of v11, /device:TPU:0, one launch (start us, length us, event | category | flops | bytes accessed | tf_op | source)
XLA Modules:
  0.0 280.5 jit_solution(18065556473409583886)
XLA Ops:
  6.5 0.7 all-gather.3.cloned.1.call-update
  7.3 25.9 %all-gather = f32[32,1,256]{2,1,0:T(1,128)S(1)} all-gather(f32[1,1,256]{2,1,0:T(1,128)} %bitcast.156), channel_id=1, replica_groups=mesh['row'=4,'col'=32] {'col'}, dimensions={0}, use_global_device_ids=true | all-gather | bytes 33792 | tf_op jit(solution)/shard_map/all_gather | solution.py:32
  33.2 0.5 slice.204
  34.4 0.9 fusion.51
  35.3 0.7 fusion.62
  45.9 0.9 compare_reduce_fusion
  46.9 0.7 fusion.54
  53.1 31.9 %all-gather.3.cloned.1.call-done = bf16[2,2048,2048]{2,1,0:T(8,128)(2,1)} async-done(((bf16[2,64,2048]{2,1,0:T(8,128)(2,1)}), bf16[2,2048,2048]{2,1,0:T(8,128)(2,1)}) %all-gather.3.cloned.1.call-update) | async-done | bytes 16777232 | tf_op jit(solution)/shard_map/all_gather | solution.py:29
  85.0 6.7 %fusion.60 = (bf16[1,2048,2048]{2,1,0:T(8,128)(2,1)S(1)}, bf16[1,2048,2048]{2,1,0:T(8,128)(2,1)S(1)}) fusion(bf16[2,2048,2048]{2,1,0:T(8,128)(2,1)} %all-gather.3.cloned.1.call-done), kind=kLoop, calls=%fused_computation.146 | loop fusion | bytes 33554432 | tf_op jit(solution)/shard_map/slice | solution.py:55
  92.6 0.6 maximum_select_fusion
  93.2 1.3 fusion.10
  94.5 0.5 slice.209
  96.5 1.3 slice-done.3
  97.8 11.0 %fusion = f32[2,512,16,128]{3,1,2,0:T(8,128)} fusion(bf16[2,16,128,2048]{3,2,1,0:T(8,128)(2,1)S(1)} %bitcast.138, bf16[2,512,2048]{2,1,0:T(8,128)(2,1)S(1)} %maximum_select_fusion, bf16[]{:T(256)} %bitcast.21), kind=kOutput, calls=%fused_computation.5 | convolution fusion | flops 8598323200 | bytes 29360130 | tf_op jit(solution)/shard_map/cutk,cmk->cumt/dot_general | solution.py:75
  108.9 7.7 %gather_fusion = f32[32,512,128]{2,1,0:T(8,128)} fusion(f32[32,512,128]{2,1,0:T(8,128)} %bitcast.141, s32[1024]{0:T(1024)S(1)} %pad_clamp_fusion), kind=kCustom, calls=%fused_computation | custom fusion | bytes 16777344 | tf_op jit(solution)/shard_map/jit(_take)/gather | solution.py:82
  116.8 0.5 copy-done
  117.2 0.7 gather_fusion.1
  118.1 0.6 fusion.61
  133.5 1.5 collective-permute-start
  135.0 2.7 collective-permute-start.1
  137.7 1.5 collective-permute-start.2
  139.2 21.3 %collective-permute-done = f32[256,512]{0,1:T(8,128)S(1)} collective-permute-done((f32[256,512]{0,1:T(8,128)S(1)}, f32[256,512]{0,1:T(8,128)S(1)}, u32[]{:S(2)}, u32[]{:S(2)}) %collective-permute-start) | collective-permute-done | bytes 524320 | tf_op jit(solution)/shard_map/ppermute | solution.py:73
  160.6 23.4 %collective-permute-done.1 = f32[256,512]{0,1:T(8,128)S(1)} collective-permute-done((f32[256,512]{0,1:T(8,128)S(1)}, f32[256,512]{0,1:T(8,128)S(1)}, u32[]{:S(2)}, u32[]{:S(2)}) %collective-permute-start.1) | collective-permute-done | bytes 524320 | tf_op jit(solution)/shard_map/ppermute | solution.py:73
  184.3 11.7 %cholesky.49 = f32[128,128]{1,0:T(8,128)S(1)} custom-call(f32[128,128]{1,0:T(8,128)S(1)} %cholesky.115), custom_call_target="Cholesky" | custom-call | tf_op jit(solution)/shard_map/jit(cholesky)/cholesky | solution.py:95
  196.2 9.8 %custom-call.14 = f32[1,128,128]{1,2,0:T(8,128)S(1)} custom-call(f32[1,128,128]{2,1,0:T(8,128)S(1)} %get-tuple-element.52), custom_call_target="InvertDiagBlocksLowerTriangular" | custom-call | tf_op jit(solution)/shard_map/jit(cholesky)/cholesky | solution.py:95
  206.6 11.7 %cholesky.103 = f32[128,128]{1,0:T(8,128)S(1)} custom-call(f32[128,128]{1,0:T(8,128)S(1)} %convolution_subtract_fusion.2), custom_call_target="Cholesky" | custom-call | tf_op jit(solution)/shard_map/jit(cholesky)/cholesky | solution.py:95
  218.4 0.7 compare_reduce_fusion.1
  220.5 4.3 %while.1 = (s32[]{:T(128)}, f32[256,256]{0,1:T(8,128)S(1)}, s32[2,2]{1,0:T(2,128)S(1)}, f32[2,128,128]{2,1,0:T(8,128)S(1)}, s32[]{:T(128)}) while((s32[]{:T(128)}, f32[256,256]{0,1:T(8,128)S(1)}, s32[2,2]{1,0:T(2,128)S(1)}, f32[2,128,128]{2,1,0:T(8,128)S(1)}, s32[]{:T(128)}) %tuple.48), condition=%wide.while_cond, body=%wide.while_body.sunk | while | flops 2 | bytes 393321 | solution.py:96
  220.7 0.6 fusion.72
  221.3 1.4 dynamic-slice.7
  222.8 0.6 fusion.72
  223.4 1.4 dynamic-slice.7
  224.9 19.7 %custom-call.15 = f32[2,128,128]{1,2,0:T(8,128)S(1)} custom-call(f32[2,128,128]{2,1,0:T(8,128)S(1)} %get-tuple-element.12), custom_call_target="InvertDiagBlocksLowerTriangular" | custom-call | tf_op jit(solution)/shard_map/triangular_solve | solution.py:96
  245.0 0.3 convolution_subtract_fusion.1
  245.3 0.3 fusion.34
  245.6 0.4 fusion.13
  246.1 2.4 broadcast_in_dim.121
  248.5 0.7 fusion.28
  249.2 1.7 fusion.27
  250.9 1.7 fusion.25
  252.5 1.7 fusion.23
  254.2 1.7 fusion.21
  255.9 1.7 fusion.19
  257.6 1.7 fusion.17
  259.2 1.7 fusion.15
  260.9 5.4 %copy.50 = f32[16,128,512]{2,1,0:T(8,128)} copy(f32[16,128,512]{1,2,0:T(8,128)} %fusion.15) | data formatting | bytes 8388608 | tf_op jit(solution)/shard_map/jit(dynamic_update_index_in_dim)/dynamic_update_slice | solution.py:110
  266.3 3.5 %bitcast_select_fusion = (f32[2048,256]{1,0:T(8,128)S(1)}, f32[2048,256]{1,0:T(8,128)S(1)}) fusion(f32[256,256]{1,0:T(8,128)S(1)} %copy.48, pred[2048]{0:T(1024)(128)(4,1)S(1)} %fusion.50, f32[256,128]{0,1:T(8,128)S(1)} %fusion.34, f32[256,128]{0,1:T(8,128)S(1)} %fusion.31, f32[2048,512]{1,0:T(8,128)} %bitcast.134), kind=kOutput, calls=%fused_computation.18 | convolution fusion | flops 1611202560 | bytes 6817792 | tf_op jit(solution)/shard_map/dot_general | solution.py:123
  269.8 3.8 %fusion.4 = f32[2048,256]{1,0:T(8,128)} fusion(f32[2048,256]{1,0:T(8,128)S(1)} %get-tuple-element.69, f32[2048,256]{1,0:T(8,128)S(1)} %get-tuple-element.70, f32[256,256]{1,0:T(8,128)S(1)} %fusion.13, f32[2048,512]{1,0:T(8,128)S(1)} %bitcast.135, f32[256]{0:T(256)S(1)} %copy-done.3, s32[256]{0:T(256)S(1)} %iota_add_fusion, s32[2048]{0:T(1024)S(1)} %fusion.47, ...), kind=kOutput, calls=%fused_computation.10 | convolution fusion | flops 1613758464 | bytes 8663041 | tf_op jit(solution)/shard_map/dot_general | solution.py:125
  (75 shorter events, 4.2 us)
Async XLA Ops:
  6.5 78.4 %all-gather.3.cloned.1.call-start = ((), (), s32[]{:S(2)}) async-start(), calls=%async_computation.1 | async-start | bytes 17301504 | tf_op jit(solution)/shard_map/all_gather | solution.py:29
  7.3 238.8 %reduce-scatter.2.cloned.1.call-start = ((), (), s32[]{:S(2)}) async-start(), calls=%async_computation.2 | async-start | bytes 10485760 | tf_op jit(solution)/shard_map/reduce_scatter | solution.py:83
  91.7 4.8 %slice-start = ((s8[16777216]{0:T(1024)(128)(4,1)}), s8[4194304]{0:T(1024)(128)(4,1)S(1)}, s32[]{:S(2)}) async-start(s8[16777216]{0:T(1024)(128)(4,1)} %bitcast.136), calls=%async_computation.3 | async-start | bytes 8388608
  91.9 4.6 %slice-start.1 = ((s8[16777216]{0:T(1024)(128)(4,1)}), s8[4194304]{0:T(1024)(128)(4,1)S(1)}, s32[]{:S(2)}) async-start(s8[16777216]{0:T(1024)(128)(4,1)} %bitcast.136), calls=%async_computation.4 | async-start | bytes 8388608
  92.3 4.2 %slice-start.2 = ((s8[16777216]{0:T(1024)(128)(4,1)}), s8[4194304]{0:T(1024)(128)(4,1)S(1)}, s32[]{:S(2)}) async-start(s8[16777216]{0:T(1024)(128)(4,1)} %bitcast.136), calls=%async_computation.5 | async-start | bytes 8388608
  92.6 5.2 %slice-start.3 = ((s8[16777216]{0:T(1024)(128)(4,1)}), s8[4194304]{0:T(1024)(128)(4,1)S(1)}, s32[]{:S(2)}) async-start(s8[16777216]{0:T(1024)(128)(4,1)} %bitcast.136), calls=%async_computation.6 | async-start | bytes 8388608
  116.5 0.7 copy-start
  133.5 27.1 %collective-permute-start = (f32[256,512]{0,1:T(8,128)S(1)}, f32[256,512]{0,1:T(8,128)S(1)}, u32[]{:S(2)}, u32[]{:S(2)}) collective-permute-start(f32[256,512]{0,1:T(8,128)S(1)} %copy.41), channel_id=1, source_target_pairs={{0,32},{32,64},{64,96},{96,0},{1,33},{33,65},{65,97},{97,1},{2,34}... | collective-permute-start | bytes 1572872 | tf_op jit(solution)/shard_map/ppermute | solution.py:73
  135.0 49.0 %collective-permute-start.1 = (f32[256,512]{0,1:T(8,128)S(1)}, f32[256,512]{0,1:T(8,128)S(1)}, u32[]{:S(2)}, u32[]{:S(2)}) collective-permute-start(f32[256,512]{0,1:T(8,128)S(1)} %copy.41), channel_id=1, source_target_pairs={{0,64},{32,96},{64,0},{96,32},{1,65},{33,97},{65,1},{97,33},{2,66}... | collective-permute-start | bytes 1572872 | tf_op jit(solution)/shard_map/ppermute | solution.py:73
  137.7 46.3 %collective-permute-start.2 = (f32[256,512]{0,1:T(8,128)S(1)}, f32[256,512]{0,1:T(8,128)S(1)}, u32[]{:S(2)}, u32[]{:S(2)}) collective-permute-start(f32[256,512]{0,1:T(8,128)S(1)} %copy.41), channel_id=1, source_target_pairs={{0,96},{32,0},{64,32},{96,64},{1,97},{33,1},{65,33},{97,65},{2,98}... | collective-permute-start | bytes 1572872 | tf_op jit(solution)/shard_map/ppermute | solution.py:73
  246.1 2.4 copy-start.2
  266.3 3.5 %copy-start.1 = (f32[16,128,512]{2,1,0:T(8,128)S(1)}, f32[16,128,512]{2,1,0:T(8,128)}, u32[]{:S(2)}) copy-start(f32[16,128,512]{2,1,0:T(8,128)} %copy.50) | copy-start | bytes 12582916
  266.3 3.5 %copy-start.3 = (f32[256]{0:T(256)S(1)}, f32[256]{0:T(256)}, u32[]{:S(2)}) copy-start(f32[256]{0:T(256)} %param.5) | copy-start | bytes 3076
Sparse Core Ops, SparseCore 0:
  9.6 75.2 all-gather.2
  116.7 102.4 reduce-scatter.1

commit v12 on v8

--- a/solution.py
+++ b/solution.py
@@ -52,7 +52,9 @@
         [
             jnp.stack(
                 [
-                    lax.dynamic_index_in_dim(tiles4[child], where_at[child, slot], 0, keepdims=False)
+                    lax.dynamic_slice(
+                        tiles4, (child, where_at[child, slot], 0, 0), (1, 1, TILE, k_loc)
+                    )[0, 0]
                     for slot in range(where_at.shape[1])
                 ]
             )

time: 229 us -> 225 us (0.983)
  local copies, waits for them, and re-layouts: 34.5 us -> 30.7 us
    slice x1 -> x0, local copies, waits for them, and re-layouts: 6.74 us -> none  [shards(): tiles4[child]]
    another operation x10 -> x11, local copies, waits for them, and re-layouts: 3.99 us -> 7.29 us
    another operation x6 -> x7, other arithmetic: 34 us -> 34.6 us  [shards(): lead = jnp.tril(jnp.linalg.cholesky(front00))]
  transfers between devices with their start and end apart: 5 -> 5, of which waited for: 3 -> 3; matrix products, arithmetic and copies ran while one was open for 38% -> 39% of each run, Pallas kernels for 0% -> 0%
where the time goes in v12:
time: 225 us; the launch traced here: 224 us
  other arithmetic  60.7 us (27%)
  between operations  46.9 us (21%)
  waiting for transfers between devices  33.9 us (15%)
  local copies, waits for them, and re-layouts  30.7 us (14%)
  blocking collectives  25.9 us (12%)
  matrix products  19.9 us (9%)
  starting transfers between devices  5.65 us (3%)
    another operation x7, other arithmetic, shards(): lead = jnp.tril(jnp.linalg.cholesky(front00))  34.6 us
    all_gather x1, waiting for transfers between devices, shards(): gathered = lax.all_gather(child_factors, 'col', axis=1, tiled=True)  31.9 us
    all_gather x1, blocking collectives, shards(): full_diag = lax.all_gather(root_diag, 'col', axis=0, tiled=True)  25.9 us
    another operation x3, other arithmetic, shards(): lax.linalg.triangular_solve(lead, jnp.eye(lead_rows, dtype=jnp.float32),...  19.9 us
    dot_general x1, matrix products, shards(): jnp.einsum('cutk,cmk->cutm', tiles4, main_rows, preferred_element_type=jn...  11.1 us
    reshape x1, local copies, waits for them, and re-layouts, shards(): main = main.reshape(n_child * tiles_child, TILE, n_cols)  9.01 us
    gather x1, local copies, waits for them, and re-layouts, shards(): main = jnp.take(main, flat_order, axis=0, mode='clip')  7.69 us
    ppermute x3, starting transfers between devices, shards(): pivot_part = pivot_part + lax.ppermute(extra, 'row', pairs)  5.61 us
  transfers between devices with their start and end apart: 5, of which 3 were waited for; matrix products, arithmetic and copies ran while one was open for 39% of the time, Pallas kernels for 0%

profile of v12, /device:TPU:0, one launch (start us, length us, event | category | flops | bytes accessed | tf_op | source)
XLA Modules:
  0.0 223.7 jit_solution(7653696373621212941)
XLA Ops:
  6.5 0.7 all-gather.3.cloned.1.call-update
  7.3 25.9 %all-gather = f32[32,1,256]{2,1,0:T(1,128)S(1)} all-gather(f32[1,1,256]{2,1,0:T(1,128)} %bitcast.173), channel_id=1, replica_groups=mesh['row'=4,'col'=32] {'col'}, dimensions={0}, use_global_device_ids=true | all-gather | bytes 33792 | tf_op jit(solution)/shard_map/all_gather | solution.py:32
  33.2 0.5 slice.191
  34.4 0.9 fusion.51
  35.3 0.7 fusion.61
  46.0 0.9 compare_reduce_fusion
  47.0 0.7 fusion.54
  47.7 0.2 convert_reduce_fusion
  53.0 31.9 %all-gather.3.cloned.1.call-done = bf16[2,2048,2048]{2,1,0:T(8,128)(2,1)} async-done(((bf16[2,64,2048]{2,1,0:T(8,128)(2,1)}), bf16[2,2048,2048]{2,1,0:T(8,128)(2,1)}) %all-gather.3.cloned.1.call-update) | async-done | bytes 16777232 | tf_op jit(solution)/shard_map/all_gather | solution.py:29
  84.9 3.2 %dynamic-slice_bitcast_fusion.7 = (bf16[1,128,2048]{2,1,0:T(8,128)(2,1)S(1)}, bf16[1,128,2048]{2,1,0:T(8,128)(2,1)S(1)}, bf16[1,128,2048]{2,1,0:T(8,128)(2,1)S(1...) fusion(bf16[2,16,128,2048]{3,2,1,0:T(8,128)(2,1)} %bitcast.165,, ...), kind=kLoop, calls=%fused_computation.31 | loop fusion | bytes 8388640 | tf_op jit(solution)/shard_map/stack;squeeze | solution.py:53
  88.2 0.6 pad_maximum_fusion
  88.7 0.6 maximum_select_fusion
  89.4 1.3 fusion.10
  90.7 0.5 slice.195
  91.2 1.5 collective-permute-start
  92.7 2.7 %collective-permute-start.1 = (f32[256,512]{0,1:T(8,128)S(1)}, f32[256,512]{0,1:T(8,128)}, u32[]{:S(2)}, u32[]{:S(2)}) collective-permute-start(f32[256,512]{0,1:T(8,128)S(1)} %fusion.10), channel_id=1, source_target_pairs={{0,64},{32,96},{64,0},{96,32},{1,65},{33,97},{65,1},{97,33},{2,66}... | collective-permute-start | bytes 1572872 | tf_op jit(solution)/shard_map/ppermute | solution.py:75
  95.3 1.5 collective-permute-start.2
  97.5 11.1 %fusion = f32[2,512,16,128]{3,1,2,0:T(8,128)} fusion(bf16[2,16,128,2048]{3,2,1,0:T(8,128)(2,1)S(1)} %bitcast.168, bf16[2,512,2048]{2,1,0:T(8,128)(2,1)S(1)} %maximum_select_fusion, bf16[]{:T(256)} %bitcast.33), kind=kOutput, calls=%fused_computation.5 | convolution fusion | flops 8598323200 | bytes 29360130 | tf_op jit(solution)/shard_map/cutk,cmk->cutm/dot_general | solution.py:77
  108.6 9.0 %copy.67 = f32[32,128,512]{2,1,0:T(8,128)} copy(f32[32,128,512]{1,2,0:T(8,128)} %bitcast.154) | data formatting | bytes 16777216 | tf_op jit(solution)/shard_map/reshape | solution.py:80
  117.6 1.0 collective-permute-done.1
  118.6 1.3 add_add_fusion
  119.9 0.5 slice.196
  121.3 7.7 %gather_fusion = f32[32,128,512]{2,1,0:T(8,128)} fusion(f32[32,128,512]{2,1,0:T(8,128)} %copy.67, s32[1024]{0:T(1024)S(1)} %pad_clamp_fusion), kind=kCustom, calls=%fused_computation | custom fusion | bytes 16777344 | tf_op jit(solution)/shard_map/jit(_take)/gather | solution.py:85
  129.2 0.5 copy-done
  129.6 0.7 gather_fusion.1
  130.5 0.7 fusion.60
  146.3 11.7 %cholesky.49 = f32[128,128]{1,0:T(8,128)S(1)} custom-call(f32[128,128]{1,0:T(8,128)S(1)} %cholesky.115), custom_call_target="Cholesky" | custom-call | tf_op jit(solution)/shard_map/jit(cholesky)/cholesky | solution.py:97
  158.2 9.8 %custom-call.14 = f32[1,128,128]{1,2,0:T(8,128)S(1)} custom-call(f32[1,128,128]{2,1,0:T(8,128)S(1)} %get-tuple-element.54), custom_call_target="InvertDiagBlocksLowerTriangular" | custom-call | tf_op jit(solution)/shard_map/jit(cholesky)/cholesky | solution.py:97
  168.0 0.2 fusion.36
  168.3 0.3 convolution_subtract_fusion.2
  168.6 11.7 %cholesky.103 = f32[128,128]{1,0:T(8,128)S(1)} custom-call(f32[128,128]{1,0:T(8,128)S(1)} %convolution_subtract_fusion.2), custom_call_target="Cholesky" | custom-call | tf_op jit(solution)/shard_map/jit(cholesky)/cholesky | solution.py:97
  180.4 0.7 compare_reduce_fusion.1
  181.1 0.6 compare_reduce_fusion.2
  183.2 4.1 %while.1 = (s32[]{:T(128)}, f32[256,256]{0,1:T(8,128)S(1)}, s32[2,2]{1,0:T(2,128)S(1)}, f32[2,128,128]{2,1,0:T(8,128)S(1)}, s32[]{:T(128)}) while((s32[]{:T(128)}, f32[256,256]{0,1:T(8,128)S(1)}, s32[2,2]{1,0:T(2,128)S(1)}, f32[2,128,128]{2,1,0:T(8,128)S(1)}, s32[]{:T(128)}) %tuple.49), condition=%wide.while_cond, body=%wide.while_body.sunk | while | flops 2 | bytes 393321 | solution.py:98
  183.2 0.6 fusion.71
  183.8 1.3 dynamic-slice.7
  185.3 0.6 fusion.71
  185.8 1.3 dynamic-slice.7
  187.3 19.9 %custom-call.15 = f32[2,128,128]{1,2,0:T(8,128)S(1)} custom-call(f32[2,128,128]{2,1,0:T(8,128)S(1)} %get-tuple-element.12), custom_call_target="InvertDiagBlocksLowerTriangular" | custom-call | tf_op jit(solution)/shard_map/triangular_solve | solution.py:98
  207.4 0.3 fusion.31
  207.6 0.3 convolution_subtract_fusion.1
  208.0 0.3 fusion.34
  208.3 0.4 fusion.13
  208.7 0.3 reduce-scatter.2.cloned.1.call-done
  209.0 0.5 broadcast_in_dim.119
  209.5 1.1 copy-done.1
  211.1 1.9 bitcast_select_fusion
  213.0 3.8 %fusion.4 = f32[2048,256]{1,0:T(8,128)} fusion(f32[2048,256]{1,0:T(8,128)S(1)} %get-tuple-element.71, f32[2048,256]{1,0:T(8,128)S(1)} %get-tuple-element.72, f32[256,256]{1,0:T(8,128)S(1)} %fusion.13, f32[2048,512]{1,0:T(8,128)S(1)} %bitcast.153, f32[256]{0:T(256)S(1)} %copy-done.2, s32[256]{0:T(256)S(1)} %iota_add_fusion, s32[2048]{0:T(1024)S(1)} %fusion.47, ...), kind=kOutput, calls=%fused_computation.10 | convolution fusion | flops 1613758464 | bytes 8663041 | tf_op jit(solution)/shard_map/dot_general | solution.py:127
  (71 shorter events, 2.5 us)
Async XLA Ops:
  6.5 78.4 %all-gather.3.cloned.1.call-start = ((), (), s32[]{:S(2)}) async-start(), calls=%async_computation.1 | async-start | bytes 17301504 | tf_op jit(solution)/shard_map/all_gather | solution.py:29
  7.3 201.7 %reduce-scatter.2.cloned.1.call-start = ((), (), s32[]{:S(2)}) async-start(), calls=%async_computation.2 | async-start | bytes 10485760 | tf_op jit(solution)/shard_map/reduce_scatter | solution.py:86
  84.9 12.5 %slice-start = ((s8[16777216]{0:T(1024)(128)(4,1)}), s8[4194304]{0:T(1024)(128)(4,1)S(1)}, s32[]{:S(2)}) async-start(s8[16777216]{0:T(1024)(128)(4,1)} %bitcast.166), calls=%async_computation.3 | async-start | bytes 8388608
  88.1 9.3 %slice-start.1 = ((s8[16777216]{0:T(1024)(128)(4,1)}), s8[4194304]{0:T(1024)(128)(4,1)S(1)}, s32[]{:S(2)}) async-start(s8[16777216]{0:T(1024)(128)(4,1)} %bitcast.166), calls=%async_computation.4 | async-start | bytes 8388608
  88.7 8.7 %slice-start.2 = ((s8[16777216]{0:T(1024)(128)(4,1)}), s8[4194304]{0:T(1024)(128)(4,1)S(1)}, s32[]{:S(2)}) async-start(s8[16777216]{0:T(1024)(128)(4,1)} %bitcast.166), calls=%async_computation.5 | async-start | bytes 8388608
  89.4 8.1 %slice-start.3 = ((s8[16777216]{0:T(1024)(128)(4,1)}), s8[4194304]{0:T(1024)(128)(4,1)S(1)}, s32[]{:S(2)}) async-start(s8[16777216]{0:T(1024)(128)(4,1)} %bitcast.166), calls=%async_computation.6 | async-start | bytes 8388608
  91.2 26.4 %collective-permute-start = (f32[256,512]{0,1:T(8,128)S(1)}, f32[256,512]{0,1:T(8,128)S(1)}, u32[]{:S(2)}, u32[]{:S(2)}) collective-permute-start(f32[256,512]{0,1:T(8,128)S(1)} %fusion.10), channel_id=1, source_target_pairs={{0,32},{32,64},{64,96},{96,0},{1,33},{33,65},{65,97},{97,1},{2,34}... | collective-permute-start | bytes 1572872 | tf_op jit(solution)/shard_map/ppermute | solution.py:75
  92.7 25.9 %collective-permute-start.1 = (f32[256,512]{0,1:T(8,128)S(1)}, f32[256,512]{0,1:T(8,128)}, u32[]{:S(2)}, u32[]{:S(2)}) collective-permute-start(f32[256,512]{0,1:T(8,128)S(1)} %fusion.10), channel_id=1, source_target_pairs={{0,64},{32,96},{64,0},{96,32},{1,65},{33,97},{65,1},{97,33},{2,66}... | collective-permute-start | bytes 1572872 | tf_op jit(solution)/shard_map/ppermute | solution.py:75
  95.3 23.2 %collective-permute-start.2 = (f32[256,512]{0,1:T(8,128)S(1)}, f32[256,512]{0,1:T(8,128)}, u32[]{:S(2)}, u32[]{:S(2)}) collective-permute-start(f32[256,512]{0,1:T(8,128)S(1)} %fusion.10), channel_id=1, source_target_pairs={{0,96},{32,0},{64,32},{96,64},{1,97},{33,1},{65,33},{97,65},{2,98}... | collective-permute-start | bytes 1572872 | tf_op jit(solution)/shard_map/ppermute | solution.py:75
  129.0 0.7 copy-start
  209.0 1.6 copy-start.1
  210.9 2.1 copy-start.2
Sparse Core Ops, SparseCore 0:
  9.6 75.2 all-gather.2
  129.1 79.8 reduce-scatter.1

commit v13 on v12

--- a/solution.py
+++ b/solution.py
@@ -46,7 +46,13 @@
     wanted = jnp.concatenate([own_tiles, pivot_tiles])
     match = child_tiles[:, :, None] == wanted[None, None, :]
     where_at = jnp.sum(jnp.where(match, position[None, :, None], 0), axis=1).astype(jnp.int32)
-    where_at = where_at + diag_edge
+    my_tiles = lax.dynamic_slice_in_dim(order, row_index * per_group, per_group, axis=1)
+    my_root = jnp.take_along_axis(child_tiles, my_tiles, axis=1)
+    my_local = (my_root * TILE // block_size) // row_count * tiles_block + my_root % tiles_block
+    n_slots = where_at.size
+    all_index = jnp.concatenate([where_at.reshape(-1), my_local.reshape(-1)]) + diag_edge
+    where_at = all_index[:n_slots].reshape(where_at.shape)
+    my_local = all_index[n_slots:].reshape(my_local.shape)
     present = jnp.any(match, axis=1)
     col_rows = jnp.stack(
         [
@@ -100,9 +106,6 @@
     )
     cols_panel = jnp.where(col_index == 0, front00, pivot_part[:, :own_w]).T
 
-    my_tiles = lax.dynamic_slice_in_dim(order, row_index * per_group, per_group, axis=1)
-    my_root = jnp.take_along_axis(child_tiles, my_tiles, axis=1)
-    my_local = (my_root * TILE // block_size) // row_count * tiles_block + my_root % tiles_block
     mine4 = mine.reshape(n_child, per_group, TILE, n_cols)
     front_loc = jnp.zeros((loc_tiles, TILE, n_cols), jnp.float32)
     for child in range(n_child):

time: 225 us -> 225 us (level)
    all_gather x1, waiting for transfers between devices: 31.9 us -> 29.6 us  [shards(): gathered = lax.all_gather(child_factors, 'col', axis=1, tiled=True)]
where the time goes in v13:
time: 225 us; the launch traced here: 223 us
  other arithmetic  60.5 us (27%)
  between operations  47.7 us (21%)
  waiting for transfers between devices  33.1 us (15%)
  local copies, waits for them, and re-layouts  30.2 us (13%)
  blocking collectives  26.1 us (12%)
  matrix products  19.9 us (9%)
  starting transfers between devices  5.66 us (3%)
    another operation x7, other arithmetic, shards(): lead = jnp.tril(jnp.linalg.cholesky(front00))  34.6 us
    all_gather x1, waiting for transfers between devices, shards(): gathered = lax.all_gather(child_factors, 'col', axis=1, tiled=True)  29.6 us
    all_gather x1, blocking collectives, shards(): full_diag = lax.all_gather(root_diag, 'col', axis=0, tiled=True)  26.1 us
    another operation x3, other arithmetic, shards(): lax.linalg.triangular_solve(lead, jnp.eye(lead_rows, dtype=jnp.float32),...  19.9 us
    dot_general x1, matrix products, shards(): jnp.einsum('cutk,cmk->cutm', tiles4, main_rows, preferred_element_type=jn...  11.1 us
    reshape x1, local copies, waits for them, and re-layouts, shards(): main = main.reshape(n_child * tiles_child, TILE, n_cols)  9 us
    gather x1, local copies, waits for them, and re-layouts, shards(): main = jnp.take(main, flat_order, axis=0, mode='clip')  7.69 us
    ppermute x3, starting transfers between devices, shards(): pivot_part = pivot_part + lax.ppermute(extra, 'row', pairs)  5.62 us
  transfers between devices with their start and end apart: 5, of which 3 were waited for; matrix products, arithmetic and copies ran while one was open for 39% of the time, Pallas kernels for 0%

profile of v13, /device:TPU:0, one launch (start us, length us, event | category | flops | bytes accessed | tf_op | source)
XLA Modules:
  0.0 223.2 jit_solution(9866385760944552934)
XLA Ops:
  6.5 0.7 all-gather.3.cloned.1.call-update
  7.3 0.7 fusion.54
  8.0 0.2 convert_reduce_fusion
  8.5 1.3 gather_fusion.1
  9.9 26.1 %all-gather = f32[32,1,256]{2,1,0:T(1,128)S(1)} all-gather(f32[1,1,256]{2,1,0:T(1,128)} %bitcast.173), channel_id=1, replica_groups=mesh['row'=4,'col'=32] {'col'}, dimensions={0}, use_global_device_ids=true | all-gather | bytes 33792 | tf_op jit(solution)/shard_map/all_gather | solution.py:32
  36.0 0.6 slice.211
  37.3 0.9 fusion.51
  38.3 0.7 fusion.60
  49.3 0.9 compare_reduce_fusion
  55.4 29.6 %all-gather.3.cloned.1.call-done = bf16[2,2048,2048]{2,1,0:T(8,128)(2,1)} async-done(((bf16[2,64,2048]{2,1,0:T(8,128)(2,1)}), bf16[2,2048,2048]{2,1,0:T(8,128)(2,1)}) %all-gather.3.cloned.1.call-update) | async-done | bytes 16777232 | tf_op jit(solution)/shard_map/all_gather | solution.py:29
  84.9 3.1 %dynamic-slice_bitcast_fusion.7 = (bf16[1,128,2048]{2,1,0:T(8,128)(2,1)S(1)}, bf16[1,128,2048]{2,1,0:T(8,128)(2,1)S(1)}, bf16[1,128,2048]{2,1,0:T(8,128)(2,1)S(1...) fusion(bf16[2,16,128,2048]{3,2,1,0:T(8,128)(2,1)} %bitcast.165,, ...), kind=kLoop, calls=%fused_computation.31 | loop fusion | bytes 8388640 | tf_op jit(solution)/shard_map/stack;squeeze | solution.py:59
  88.1 0.6 pad_maximum_fusion
  88.7 0.6 maximum_select_fusion
  89.3 1.3 fusion.10
  90.6 0.5 slice.215
  91.1 1.5 collective-permute-start
  92.6 2.7 %collective-permute-start.1 = (f32[256,512]{0,1:T(8,128)S(1)}, f32[256,512]{0,1:T(8,128)S(1)}, u32[]{:S(2)}, u32[]{:S(2)}) collective-permute-start(f32[256,512]{0,1:T(8,128)S(1)} %fusion.10), channel_id=1, source_target_pairs={{0,64},{32,96},{64,0},{96,32},{1,65},{33,97},{65,1},{97,33},{2,66}... | collective-permute-start | bytes 1572872 | tf_op jit(solution)/shard_map/ppermute | solution.py:81
  95.3 1.4 collective-permute-start.2
  97.4 11.1 %fusion = f32[2,512,16,128]{3,1,2,0:T(8,128)} fusion(bf16[2,16,128,2048]{3,2,1,0:T(8,128)(2,1)S(1)} %bitcast.168, bf16[2,512,2048]{2,1,0:T(8,128)(2,1)S(1)} %maximum_select_fusion, bf16[]{:T(256)} %bitcast.34), kind=kOutput, calls=%fused_computation.5 | convolution fusion | flops 8598323200 | bytes 29360130 | tf_op jit(solution)/shard_map/cutk,cmk->cutm/dot_general | solution.py:83
  108.4 9.0 %copy.67 = f32[32,128,512]{2,1,0:T(8,128)} copy(f32[32,128,512]{1,2,0:T(8,128)} %bitcast.154) | data formatting | bytes 16777216 | tf_op jit(solution)/shard_map/reshape | solution.py:86
  117.4 1.1 collective-permute-done.1
  118.6 1.2 add_add_fusion
  119.8 0.6 slice.216
  121.2 7.7 %gather_fusion = f32[32,128,512]{2,1,0:T(8,128)} fusion(f32[32,128,512]{2,1,0:T(8,128)} %copy.67, s32[1024]{0:T(1024)S(1)} %pad_clamp_fusion), kind=kCustom, calls=%fused_computation | custom fusion | bytes 16777344 | tf_op jit(solution)/shard_map/jit(_take)/gather | solution.py:91
  144.4 0.1 copy.60
  144.6 11.7 %cholesky.49 = f32[128,128]{1,0:T(8,128)S(1)} custom-call(f32[128,128]{1,0:T(8,128)S(1)} %cholesky.115), custom_call_target="Cholesky" | custom-call | tf_op jit(solution)/shard_map/jit(cholesky)/cholesky | solution.py:103
  156.5 9.8 %custom-call.14 = f32[1,128,128]{1,2,0:T(8,128)S(1)} custom-call(f32[1,128,128]{2,1,0:T(8,128)S(1)} %get-tuple-element.54), custom_call_target="InvertDiagBlocksLowerTriangular" | custom-call | tf_op jit(solution)/shard_map/jit(cholesky)/cholesky | solution.py:103
  166.3 0.2 fusion.36
  166.6 0.3 convolution_subtract_fusion.2
  166.9 11.7 %cholesky.103 = f32[128,128]{1,0:T(8,128)S(1)} custom-call(f32[128,128]{1,0:T(8,128)S(1)} %convolution_subtract_fusion.2), custom_call_target="Cholesky" | custom-call | tf_op jit(solution)/shard_map/jit(cholesky)/cholesky | solution.py:103
  178.7 0.7 compare_reduce_fusion.1
  179.4 0.6 compare_reduce_fusion.2
  181.4 4.0 %while.1 = (s32[]{:T(128)}, f32[256,256]{0,1:T(8,128)S(1)}, s32[2,2]{1,0:T(2,128)S(1)}, f32[2,128,128]{2,1,0:T(8,128)S(1)}, s32[]{:T(128)}) while((s32[]{:T(128)}, f32[256,256]{0,1:T(8,128)S(1)}, s32[2,2]{1,0:T(2,128)S(1)}, f32[2,128,128]{2,1,0:T(8,128)S(1)}, s32[]{:T(128)}) %tuple.50), condition=%wide.while_cond, body=%wide.while_body.sunk | while | flops 2 | bytes 393321 | solution.py:104
  181.5 0.6 fusion.70
  182.0 1.3 dynamic-slice.7
  183.5 0.6 fusion.70
  184.1 1.3 dynamic-slice.7
  185.5 19.9 %custom-call.15 = f32[2,128,128]{1,2,0:T(8,128)S(1)} custom-call(f32[2,128,128]{2,1,0:T(8,128)S(1)} %get-tuple-element.12), custom_call_target="InvertDiagBlocksLowerTriangular" | custom-call | tf_op jit(solution)/shard_map/triangular_solve | solution.py:104
  205.4 0.1 copy.64
  205.5 0.3 fusion.31
  205.8 0.3 convolution_subtract_fusion.1
  206.1 0.3 fusion.34
  206.5 0.4 fusion.13
  206.9 1.7 reduce-scatter.2.cloned.1.call-done
  208.5 0.5 broadcast_in_dim.121
  209.1 1.1 copy-done
  210.6 1.9 bitcast_select_fusion
  212.6 3.8 %fusion.4 = f32[2048,256]{1,0:T(8,128)} fusion(f32[2048,256]{1,0:T(8,128)S(1)} %get-tuple-element.71, f32[2048,256]{1,0:T(8,128)S(1)} %get-tuple-element.72, f32[256,256]{1,0:T(8,128)S(1)} %fusion.13, f32[2048,512]{1,0:T(8,128)S(1)} %bitcast.153, f32[256]{0:T(256)S(1)} %copy-done.1, s32[256]{0:T(256)S(1)} %iota_add_fusion, s32[2048]{0:T(1024)S(1)} %fusion.47, ...), kind=kOutput, calls=%fused_computation.10 | convolution fusion | flops 1613758464 | bytes 8663041 | tf_op jit(solution)/shard_map/dot_general | solution.py:130
  (68 shorter events, 2.2 us)
Async XLA Ops:
  6.5 78.4 %all-gather.3.cloned.1.call-start = ((), (), s32[]{:S(2)}) async-start(), calls=%async_computation.1 | async-start | bytes 17301504 | tf_op jit(solution)/shard_map/all_gather | solution.py:29
  7.3 201.3 %reduce-scatter.2.cloned.1.call-start = ((), (), s32[]{:S(2)}) async-start(), calls=%async_computation.2 | async-start | bytes 10485760 | tf_op jit(solution)/shard_map/reduce_scatter | solution.py:92
  84.9 12.4 %slice-start = ((s8[16777216]{0:T(1024)(128)(4,1)}), s8[4194304]{0:T(1024)(128)(4,1)S(1)}, s32[]{:S(2)}) async-start(s8[16777216]{0:T(1024)(128)(4,1)} %bitcast.166), calls=%async_computation.3 | async-start | bytes 8388608
  88.1 9.3 %slice-start.1 = ((s8[16777216]{0:T(1024)(128)(4,1)}), s8[4194304]{0:T(1024)(128)(4,1)S(1)}, s32[]{:S(2)}) async-start(s8[16777216]{0:T(1024)(128)(4,1)} %bitcast.166), calls=%async_computation.4 | async-start | bytes 8388608
  88.6 8.7 %slice-start.2 = ((s8[16777216]{0:T(1024)(128)(4,1)}), s8[4194304]{0:T(1024)(128)(4,1)S(1)}, s32[]{:S(2)}) async-start(s8[16777216]{0:T(1024)(128)(4,1)} %bitcast.166), calls=%async_computation.5 | async-start | bytes 8388608
  89.3 8.0 %slice-start.3 = ((s8[16777216]{0:T(1024)(128)(4,1)}), s8[4194304]{0:T(1024)(128)(4,1)S(1)}, s32[]{:S(2)}) async-start(s8[16777216]{0:T(1024)(128)(4,1)} %bitcast.166), calls=%async_computation.6 | async-start | bytes 8388608
  91.1 26.3 %collective-permute-start = (f32[256,512]{0,1:T(8,128)S(1)}, f32[256,512]{0,1:T(8,128)S(1)}, u32[]{:S(2)}, u32[]{:S(2)}) collective-permute-start(f32[256,512]{0,1:T(8,128)S(1)} %fusion.10), channel_id=1, source_target_pairs={{0,32},{32,64},{64,96},{96,0},{1,33},{33,65},{65,97},{97,1},{2,34}... | collective-permute-start | bytes 1572872 | tf_op jit(solution)/shard_map/ppermute | solution.py:81
  92.6 26.0 %collective-permute-start.1 = (f32[256,512]{0,1:T(8,128)S(1)}, f32[256,512]{0,1:T(8,128)S(1)}, u32[]{:S(2)}, u32[]{:S(2)}) collective-permute-start(f32[256,512]{0,1:T(8,128)S(1)} %fusion.10), channel_id=1, source_target_pairs={{0,64},{32,96},{64,0},{96,32},{1,65},{33,97},{65,1},{97,33},{2,66}... | collective-permute-start | bytes 1572872 | tf_op jit(solution)/shard_map/ppermute | solution.py:81
  95.3 23.3 %collective-permute-start.2 = (f32[256,512]{0,1:T(8,128)S(1)}, f32[256,512]{0,1:T(8,128)}, u32[]{:S(2)}, u32[]{:S(2)}) collective-permute-start(f32[256,512]{0,1:T(8,128)S(1)} %fusion.10), channel_id=1, source_target_pairs={{0,96},{32,0},{64,32},{96,64},{1,97},{33,1},{65,33},{97,65},{2,98}... | collective-permute-start | bytes 1572872 | tf_op jit(solution)/shard_map/ppermute | solution.py:81
  208.5 1.6 copy-start
  210.5 2.1 copy-start.1
Sparse Core Ops, SparseCore 0:
  9.6 75.2 all-gather.2
  129.0 79.4 reduce-scatter.1

commit v14 on v12

--- a/solution.py
+++ b/solution.py
@@ -104,14 +104,10 @@
     my_root = jnp.take_along_axis(child_tiles, my_tiles, axis=1)
     my_local = (my_root * TILE // block_size) // row_count * tiles_block + my_root % tiles_block
     mine4 = mine.reshape(n_child, per_group, TILE, n_cols)
-    front_loc = jnp.zeros((loc_tiles, TILE, n_cols), jnp.float32)
-    for child in range(n_child):
-        for slot in range(per_group):
-            at = my_local[child, slot]
-            here = lax.dynamic_index_in_dim(front_loc, at, 0, keepdims=True)
-            front_loc = lax.dynamic_update_index_in_dim(
-                front_loc, here + mine4[child, slot][None], at, 0
-            )
+    onto = (my_local[:, None, :] == jnp.arange(loc_tiles, dtype=jnp.int32)[None, :, None])
+    front_loc = jnp.einsum(
+        "cls,cstm->ltm", onto.astype(jnp.float32), mine4, precision=highest
+    )
     front_loc = front_loc.reshape(loc_rows, n_cols)
 
     local_rows = jnp.arange(loc_rows, dtype=jnp.int32)

time: 225 us -> 231 us (1.027)
  waiting for transfers between devices: 33.9 us -> 50.6 us
  between operations: 46.9 us -> 32.2 us
  matrix products: 19.9 us -> 25.6 us
    reduce_scatter x1, waiting for transfers between devices: 0.26 us -> 14.1 us  [shards(): lax.psum_scatter(main.reshape(row_count * n_child * per_group * TILE, n_c...]
    dot_general x0 -> x1, matrix products: none -> 5.68 us  [shards(): jnp.einsum('cls,cstm->ltm', onto.astype(jnp.float32), mine4, precision=hi...]
    ppermute x3, waiting for transfers between devices: 0.98 us -> 4.07 us  [shards(): pivot_part = pivot_part + lax.ppermute(extra, 'row', pairs)]
    dot_general x0 -> x1, local copies, waits for them, and re-layouts: none -> 2.43 us  [shards(): jnp.einsum('cls,cstm->ltm', onto.astype(jnp.float32), mine4, precision=hi...]
  transfers between devices with their start and end apart: 5 -> 5, of which waited for: 3 -> 4; matrix products, arithmetic and copies ran while one was open for 39% -> 38% of each run, Pallas kernels for 0% -> 0%
where the time goes in v14:
time: 231 us; the launch traced here: 229 us
  other arithmetic  60.1 us (26%)
  waiting for transfers between devices  50.6 us (22%)
  between operations  32.2 us (14%)
  local copies, waits for them, and re-layouts  30.6 us (13%)
  blocking collectives  25.9 us (11%)
  matrix products  25.6 us (11%)
  starting transfers between devices  4.44 us (2%)
    another operation x7, other arithmetic, shards(): lead = jnp.tril(jnp.linalg.cholesky(front00))  34.6 us
    all_gather x1, waiting for transfers between devices, shards(): gathered = lax.all_gather(child_factors, 'col', axis=1, tiled=True)  31.7 us
    all_gather x1, blocking collectives, shards(): full_diag = lax.all_gather(root_diag, 'col', axis=0, tiled=True)  25.9 us
    another operation x3, other arithmetic, shards(): lax.linalg.triangular_solve(lead, jnp.eye(lead_rows, dtype=jnp.float32),...  19.9 us
    reduce_scatter x1, waiting for transfers between devices, shards(): lax.psum_scatter(main.reshape(row_count * n_child * per_group * TILE, n_c...  14.1 us
    dot_general x1, matrix products, shards(): jnp.einsum('cutk,cmk->cutm', tiles4, main_rows, preferred_element_type=jn...  11.1 us
    reshape x1, local copies, waits for them, and re-layouts, shards(): main = main.reshape(n_child * tiles_child, TILE, n_cols)  9 us
    gather x1, local copies, waits for them, and re-layouts, shards(): main = jnp.take(main, flat_order, axis=0, mode='clip')  7.69 us
  transfers between devices with their start and end apart: 5, of which 4 were waited for; matrix products, arithmetic and copies ran while one was open for 38% of the time, Pallas kernels for 0%

profile of v14, /device:TPU:0, one launch (start us, length us, event | category | flops | bytes accessed | tf_op | source)
XLA Modules:
  0.0 229.3 jit_solution(17597846375876635109)
XLA Ops:
  6.5 0.7 all-gather.3.cloned.1.call-update
  7.3 25.9 %all-gather = f32[32,1,256]{2,1,0:T(1,128)S(1)} all-gather(f32[1,1,256]{2,1,0:T(1,128)} %bitcast.118), channel_id=1, replica_groups=mesh['row'=4,'col'=32] {'col'}, dimensions={0}, use_global_device_ids=true | all-gather | bytes 33792 | tf_op jit(solution)/shard_map/all_gather | solution.py:32
  33.2 0.5 slice.127
  34.4 0.9 fusion.37
  35.3 0.7 fusion.49
  46.1 0.9 compare_reduce_fusion
  47.1 0.7 fusion.43
  47.8 0.2 convert_reduce_fusion
  53.2 31.7 %all-gather.3.cloned.1.call-done = bf16[2,2048,2048]{2,1,0:T(8,128)(2,1)} async-done(((bf16[2,64,2048]{2,1,0:T(8,128)(2,1)}), bf16[2,2048,2048]{2,1,0:T(8,128)(2,1)}) %all-gather.3.cloned.1.call-update) | async-done | bytes 16777232 | tf_op jit(solution)/shard_map/all_gather | solution.py:29
  84.9 3.1 %dynamic-slice_bitcast_fusion.7 = (bf16[1,128,2048]{2,1,0:T(8,128)(2,1)S(1)}, bf16[1,128,2048]{2,1,0:T(8,128)(2,1)S(1)}, bf16[1,128,2048]{2,1,0:T(8,128)(2,1)S(1...) fusion(bf16[2,16,128,2048]{3,2,1,0:T(8,128)(2,1)} %bitcast.110,, ...), kind=kLoop, calls=%fused_computation.33 | loop fusion | bytes 8388640 | tf_op jit(solution)/shard_map/stack;squeeze | solution.py:53
  88.0 0.6 pad_maximum_fusion
  88.6 0.6 maximum_select_fusion
  89.3 1.3 fusion.11
  90.6 0.5 slice.131
  91.1 2.7 %collective-permute-start.2 = (f32[256,512]{0,1:T(8,128)S(1)}, f32[256,512]{0,1:T(8,128)S(1)}, u32[]{:S(2)}, u32[]{:S(2)}) collective-permute-start(f32[256,512]{0,1:T(8,128)S(1)} %fusion.11), channel_id=1, source_target_pairs={{0,96},{32,0},{64,32},{96,64},{1,97},{33,1},{65,33},{97,65},{2,98}... | collective-permute-start | bytes 1572872 | tf_op jit(solution)/shard_map/ppermute | solution.py:75
  93.8 0.8 collective-permute-start.1
  94.6 0.9 collective-permute-start
  96.2 11.1 %fusion = f32[2,512,16,128]{3,1,2,0:T(8,128)} fusion(bf16[2,16,128,2048]{3,2,1,0:T(8,128)(2,1)S(1)} %bitcast.113, bf16[2,512,2048]{2,1,0:T(8,128)(2,1)S(1)} %maximum_select_fusion, bf16[]{:T(256)} %bitcast.35), kind=kOutput, calls=%fused_computation.5 | convolution fusion | flops 8598323200 | bytes 29360130 | tf_op jit(solution)/shard_map/cutk,cmk->cutm/dot_general | solution.py:77
  107.3 9.0 %copy.73 = f32[32,128,512]{2,1,0:T(8,128)} copy(f32[32,128,512]{1,2,0:T(8,128)} %bitcast.106) | data formatting | bytes 16777216 | tf_op jit(solution)/shard_map/reshape | solution.py:80
  116.3 0.3 collective-permute-done.2
  116.6 3.8 %collective-permute-done = f32[256,512]{0,1:T(8,128)} collective-permute-done((f32[256,512]{0,1:T(8,128)S(1)}, f32[256,512]{0,1:T(8,128)}, u32[]{:S(2)}, u32[]{:S(2)}) %collective-permute-start) | collective-permute-done | bytes 524320 | tf_op jit(solution)/shard_map/ppermute | solution.py:75
  120.3 1.2 add_add_fusion
  121.5 0.5 slice.132
  122.9 7.7 %gather_fusion = f32[32,128,512]{2,1,0:T(8,128)} fusion(f32[32,128,512]{2,1,0:T(8,128)} %copy.73, s32[1024]{0:T(1024)S(1)} %pad_clamp_fusion), kind=kCustom, calls=%fused_computation | custom fusion | bytes 16777344 | tf_op jit(solution)/shard_map/jit(_take)/gather | solution.py:85
  130.8 0.4 copy-done
  131.2 0.7 gather_fusion.1
  132.4 11.7 %cholesky.49 = f32[128,128]{1,0:T(8,128)S(1)} custom-call(f32[128,128]{1,0:T(8,128)S(1)} %cholesky.115), custom_call_target="Cholesky" | custom-call | tf_op jit(solution)/shard_map/jit(cholesky)/cholesky | solution.py:97
  144.2 9.8 %custom-call.14 = f32[1,128,128]{1,2,0:T(8,128)S(1)} custom-call(f32[1,128,128]{2,1,0:T(8,128)S(1)} %get-tuple-element.54), custom_call_target="InvertDiagBlocksLowerTriangular" | custom-call | tf_op jit(solution)/shard_map/jit(cholesky)/cholesky | solution.py:97
  154.0 0.2 fusion.22
  154.3 0.3 convolution_subtract_fusion.2
  154.6 11.7 %cholesky.103 = f32[128,128]{1,0:T(8,128)S(1)} custom-call(f32[128,128]{1,0:T(8,128)S(1)} %convolution_subtract_fusion.2), custom_call_target="Cholesky" | custom-call | tf_op jit(solution)/shard_map/jit(cholesky)/cholesky | solution.py:97
  166.4 0.6 compare_reduce_fusion.2
  167.1 0.6 compare_reduce_fusion.1
  169.2 4.0 %while.1 = (s32[]{:T(128)}, f32[256,256]{0,1:T(8,128)S(1)}, s32[2,2]{1,0:T(2,128)S(1)}, f32[2,128,128]{2,1,0:T(8,128)S(1)}, s32[]{:T(128)}) while((s32[]{:T(128)}, f32[256,256]{0,1:T(8,128)S(1)}, s32[2,2]{1,0:T(2,128)S(1)}, f32[2,128,128]{2,1,0:T(8,128)S(1)}, s32[]{:T(128)}) %tuple.42), condition=%wide.while_cond, body=%wide.while_body.sunk | while | flops 2 | bytes 393329 | solution.py:98
  169.2 0.6 fusion.59
  169.8 1.3 dynamic-slice.7
  171.3 0.6 fusion.59
  171.8 1.3 dynamic-slice.7
  173.3 19.9 %custom-call.15 = f32[2,128,128]{1,2,0:T(8,128)S(1)} custom-call(f32[2,128,128]{2,1,0:T(8,128)S(1)} %get-tuple-element.12), custom_call_target="InvertDiagBlocksLowerTriangular" | custom-call | tf_op jit(solution)/shard_map/triangular_solve | solution.py:98
  193.2 0.3 fusion.17
  193.4 0.3 convolution_subtract_fusion.1
  193.8 0.3 fusion.20
  194.1 0.4 fusion.14
  194.5 14.1 %reduce-scatter.2.cloned.1.call-done = f32[1024,512]{1,0:T(8,128)} async-done(((f32[4096,512]{1,0:T(8,128)}), f32[1024,512]{1,0:T(8,128)}) %reduce-scatter.2.cloned.1.call-update) | async-done | bytes 2097168 | tf_op jit(solution)/shard_map/reduce_scatter | solution.py:86
  208.6 5.7 %convolution_bitcast_fusion = f32[16,128,512]{2,0,1:T(8,128)S(1)} fusion(f32[2,4,128,512]{3,2,1,0:T(8,128)} %bitcast.109, s32[2,4]{1,0:T(2,128)S(1)} %fusion.41), kind=kOutput, calls=%fused_computation.11 | convolution fusion | flops 100663424 | bytes 6291488 | tf_op jit(solution)/shard_map/cls,cstm->ltm/dot_general | solution.py:108
  214.3 2.4 %copy.75 = f32[16,128,512]{2,1,0:T(8,128)S(1)} copy(f32[16,128,512]{2,0,1:T(8,128)S(1)} %convolution_bitcast_fusion) | data formatting | bytes 8388608 | tf_op jit(solution)/shard_map/cls,cstm->ltm/dot_general | solution.py:108
  216.7 1.9 bitcast_select_fusion
  218.7 3.8 %fusion.4 = f32[2048,256]{1,0:T(8,128)} fusion(f32[2048,256]{1,0:T(8,128)S(1)} %get-tuple-element.63, f32[2048,256]{1,0:T(8,128)S(1)} %get-tuple-element.64, f32[256,256]{1,0:T(8,128)S(1)} %fusion.14, f32[2048,512]{1,0:T(8,128)S(1)} %bitcast.105, f32[256]{0:T(256)S(1)} %copy-done.1, s32[256]{0:T(256)S(1)} %iota_add_fusion, s32[2048]{0:T(1024)S(1)} %fusion.33, ...), kind=kOutput, calls=%fused_computation.10 | convolution fusion | flops 1613758464 | bytes 8663041 | tf_op jit(solution)/shard_map/dot_general | solution.py:123
  (61 shorter events, 2.1 us)
Async XLA Ops:
  6.5 78.4 %all-gather.3.cloned.1.call-start = ((), (), s32[]{:S(2)}) async-start(), calls=%async_computation.1 | async-start | bytes 17301504 | tf_op jit(solution)/shard_map/all_gather | solution.py:29
  7.3 201.3 %reduce-scatter.2.cloned.1.call-start = ((), (), s32[]{:S(2)}) async-start(), calls=%async_computation.2 | async-start | bytes 10485760 | tf_op jit(solution)/shard_map/reduce_scatter | solution.py:86
  84.9 11.2 %slice-start = ((s8[16777216]{0:T(1024)(128)(4,1)}), s8[4194304]{0:T(1024)(128)(4,1)S(1)}, s32[]{:S(2)}) async-start(s8[16777216]{0:T(1024)(128)(4,1)} %bitcast.111), calls=%async_computation.3 | async-start | bytes 8388608
  88.0 8.1 %slice-start.1 = ((s8[16777216]{0:T(1024)(128)(4,1)}), s8[4194304]{0:T(1024)(128)(4,1)S(1)}, s32[]{:S(2)}) async-start(s8[16777216]{0:T(1024)(128)(4,1)} %bitcast.111), calls=%async_computation.4 | async-start | bytes 8388608
  88.6 7.5 %slice-start.2 = ((s8[16777216]{0:T(1024)(128)(4,1)}), s8[4194304]{0:T(1024)(128)(4,1)S(1)}, s32[]{:S(2)}) async-start(s8[16777216]{0:T(1024)(128)(4,1)} %bitcast.111), calls=%async_computation.5 | async-start | bytes 8388608
  89.3 6.9 %slice-start.3 = ((s8[16777216]{0:T(1024)(128)(4,1)}), s8[4194304]{0:T(1024)(128)(4,1)S(1)}, s32[]{:S(2)}) async-start(s8[16777216]{0:T(1024)(128)(4,1)} %bitcast.111), calls=%async_computation.6 | async-start | bytes 8388608
  91.1 25.5 %collective-permute-start.2 = (f32[256,512]{0,1:T(8,128)S(1)}, f32[256,512]{0,1:T(8,128)S(1)}, u32[]{:S(2)}, u32[]{:S(2)}) collective-permute-start(f32[256,512]{0,1:T(8,128)S(1)} %fusion.11), channel_id=1, source_target_pairs={{0,96},{32,0},{64,32},{96,64},{1,97},{33,1},{65,33},{97,65},{2,98}... | collective-permute-start | bytes 1572872 | tf_op jit(solution)/shard_map/ppermute | solution.py:75
  93.8 22.8 %collective-permute-start.1 = (f32[256,512]{0,1:T(8,128)S(1)}, f32[256,512]{0,1:T(8,128)S(1)}, u32[]{:S(2)}, u32[]{:S(2)}) collective-permute-start(f32[256,512]{0,1:T(8,128)S(1)} %fusion.11), channel_id=1, source_target_pairs={{0,64},{32,96},{64,0},{96,32},{1,65},{33,97},{65,1},{97,33},{2,66}... | collective-permute-start | bytes 1572872 | tf_op jit(solution)/shard_map/ppermute | solution.py:75
  94.6 25.7 %collective-permute-start = (f32[256,512]{0,1:T(8,128)S(1)}, f32[256,512]{0,1:T(8,128)}, u32[]{:S(2)}, u32[]{:S(2)}) collective-permute-start(f32[256,512]{0,1:T(8,128)S(1)} %fusion.11), channel_id=1, source_target_pairs={{0,32},{32,64},{64,96},{96,0},{1,33},{33,65},{65,97},{97,1},{2,34}... | collective-permute-start | bytes 1572872 | tf_op jit(solution)/shard_map/ppermute | solution.py:75
  130.6 0.7 copy-start
  216.7 1.9 copy-start.1
Sparse Core Ops, SparseCore 0:
  9.6 75.2 all-gather.2
  130.7 77.8 reduce-scatter.1

commit v15 on v12

--- a/solution.py
+++ b/solution.py
@@ -70,9 +70,11 @@
         "cnk,cmk->nm", pivot_rows, col_rows, preferred_element_type=jnp.float32
     )
     pivot_part = extra
-    for shift in range(1, row_count):
-        pairs = [(i, (i + shift) % row_count) for i in range(row_count)]
-        pivot_part = pivot_part + lax.ppermute(extra, "row", pairs)
+    step = 1
+    while step < row_count:
+        pairs = [(i, i ^ step) for i in range(row_count)]
+        pivot_part = pivot_part + lax.ppermute(pivot_part, "row", pairs)
+        step *= 2
     main_rows = col_rows + (extra[:1, :1] * 0).astype(col_rows.dtype)[None]
     main = jnp.einsum(
         "cutk,cmk->cutm", tiles4, main_rows, preferred_element_type=jnp.float32

time: 225 us -> 237 us (1.053)
  waiting for transfers between devices: 33.9 us -> 44.6 us
  matrix products: 19.9 us -> 23.8 us
    ppermute x3 -> x2, waiting for transfers between devices: 0.98 us -> 11.1 us  [shards(): pivot_part = pivot_part + lax.ppermute(pivot_part, 'row', pairs)]
    dot_general x1, matrix products: 11.1 us -> 15 us  [shards(): jnp.einsum('cutk,cmk->cutm', tiles4, main_rows, preferred_element_type=jn...]
    ppermute x3 -> x2, starting transfers between devices: 5.61 us -> 4.53 us  [shards(): pivot_part = pivot_part + lax.ppermute(pivot_part, 'row', pairs)]
  transfers between devices with their start and end apart: 5 -> 4, of which waited for: 3 -> 2; matrix products, arithmetic and copies ran while one was open for 39% -> 39% of each run, Pallas kernels for 0% -> 0%
where the time goes in v15:
time: 237 us; the launch traced here: 236 us
  other arithmetic  58.8 us (25%)
  between operations  47.2 us (20%)
  waiting for transfers between devices  44.6 us (19%)
  local copies, waits for them, and re-layouts  30.7 us (13%)
  blocking collectives  25.9 us (11%)
  matrix products  23.8 us (10%)
  starting transfers between devices  4.57 us (2%)
    another operation x7, other arithmetic, shards(): lead = jnp.tril(jnp.linalg.cholesky(front00))  34.6 us
    all_gather x1, waiting for transfers between devices, shards(): gathered = lax.all_gather(child_factors, 'col', axis=1, tiled=True)  32.8 us
    all_gather x1, blocking collectives, shards(): full_diag = lax.all_gather(root_diag, 'col', axis=0, tiled=True)  25.9 us
    another operation x3, other arithmetic, shards(): lax.linalg.triangular_solve(lead, jnp.eye(lead_rows, dtype=jnp.float32),...  19.9 us
    dot_general x1, matrix products, shards(): jnp.einsum('cutk,cmk->cutm', tiles4, main_rows, preferred_element_type=jn...  15 us
    ppermute x2, waiting for transfers between devices, shards(): pivot_part = pivot_part + lax.ppermute(pivot_part, 'row', pairs)  11.1 us
    reshape x1, local copies, waits for them, and re-layouts, shards(): main = main.reshape(n_child * tiles_child, TILE, n_cols)  8.99 us
    gather x1, local copies, waits for them, and re-layouts, shards(): main = jnp.take(main, flat_order, axis=0, mode='clip')  7.69 us
  transfers between devices with their start and end apart: 4, of which 2 were waited for; matrix products, arithmetic and copies ran while one was open for 39% of the time, Pallas kernels for 0%

profile of v15, /device:TPU:0, one launch (start us, length us, event | category | flops | bytes accessed | tf_op | source)
XLA Modules:
  0.0 235.6 jit_solution(3004074441929614610)
XLA Ops:
  6.5 0.7 all-gather.3.cloned.1.call-update
  7.3 25.9 %all-gather = f32[32,1,256]{2,1,0:T(1,128)S(1)} all-gather(f32[1,1,256]{2,1,0:T(1,128)} %bitcast.169), channel_id=1, replica_groups=mesh['row'=4,'col'=32] {'col'}, dimensions={0}, use_global_device_ids=true | all-gather | bytes 33792 | tf_op jit(solution)/shard_map/all_gather | solution.py:32
  33.2 0.5 slice.191
  34.4 0.9 fusion.51
  35.3 0.7 fusion.61
  46.1 0.9 compare_reduce_fusion
  52.2 32.8 %all-gather.3.cloned.1.call-done = bf16[2,2048,2048]{2,1,0:T(8,128)(2,1)} async-done(((bf16[2,64,2048]{2,1,0:T(8,128)(2,1)}), bf16[2,2048,2048]{2,1,0:T(8,128)(2,1)}) %all-gather.3.cloned.1.call-update) | async-done | bytes 16777232 | tf_op jit(solution)/shard_map/all_gather | solution.py:29
  84.9 2.9 %dynamic-slice_bitcast_fusion.7 = (bf16[1,128,2048]{2,1,0:T(8,128)(2,1)S(1)}, bf16[1,128,2048]{2,1,0:T(8,128)(2,1)S(1)}, bf16[1,128,2048]{2,1,0:T(8,128)(2,1)S(1...) fusion(bf16[2,16,128,2048]{3,2,1,0:T(8,128)(2,1)} %bitcast.163,, ...), kind=kLoop, calls=%fused_computation.30 | loop fusion | bytes 8388640 | tf_op jit(solution)/shard_map/stack;squeeze | solution.py:53
  87.9 0.6 pad_maximum_fusion
  88.5 0.6 maximum_select_fusion
  89.1 1.3 fusion.10
  90.4 0.7 copy-done.1
  91.1 1.5 collective-permute-start
  92.6 0.2 convert_reduce_fusion
  92.9 0.5 slice.195
  94.1 11.1 %collective-permute-done = f32[256,512]{0,1:T(8,128)S(1)} collective-permute-done((f32[256,512]{0,1:T(8,128)S(1)}, f32[256,512]{0,1:T(8,128)S(1)}, u32[]{:S(2)}, u32[]{:S(2)}) %collective-permute-start) | collective-permute-done | bytes 524320 | tf_op jit(solution)/shard_map/ppermute | solution.py:76
  105.3 3.1 %collective-permute-start.1 = (f32[256,512]{0,1:T(8,128)S(1)}, f32[256,512]{0,1:T(8,128)S(1)}, u32[]{:S(2)}, u32[]{:S(2)}) collective-permute-start(f32[256,512]{0,1:T(8,128)S(1)} %add.261), channel_id=1, source_target_pairs={{0,64},{32,96},{64,0},{96,32},{1,65},{33,97},{65,1},{97,33},{2,66}... | collective-permute-start | bytes 1572872 | tf_op jit(solution)/shard_map/ppermute | solution.py:76
  108.3 15.0 %fusion = f32[2,512,16,128]{3,1,2,0:T(8,128)} fusion(bf16[2,16,128,2048]{3,2,1,0:T(8,128)(2,1)} %bitcast.164, bf16[2,512,2048]{2,1,0:T(8,128)(2,1)} %copy-done.1, bf16[]{:T(256)} %bitcast.31), kind=kOutput, calls=%fused_computation.5 | convolution fusion | flops 8598323200 | bytes 29360130 | tf_op jit(solution)/shard_map/cutk,cmk->cutm/dot_general | solution.py:79
  123.3 9.0 %copy.57 = f32[32,128,512]{2,1,0:T(8,128)} copy(f32[32,128,512]{1,2,0:T(8,128)} %bitcast.152) | data formatting | bytes 16777216 | tf_op jit(solution)/shard_map/reshape | solution.py:82
  132.4 0.5 slice.196
  133.7 7.7 %gather_fusion = f32[32,128,512]{2,1,0:T(8,128)} fusion(f32[32,128,512]{2,1,0:T(8,128)} %copy.57, s32[1024]{0:T(1024)S(1)} %pad_clamp_fusion), kind=kCustom, calls=%fused_computation | custom fusion | bytes 16777344 | tf_op jit(solution)/shard_map/jit(_take)/gather | solution.py:87
  141.6 0.7 gather_fusion.1
  142.3 0.1 fusion.52
  142.4 0.7 fusion.60
  158.1 0.1 copy.50
  158.3 11.7 %cholesky.49 = f32[128,128]{1,0:T(8,128)S(1)} custom-call(f32[128,128]{1,0:T(8,128)S(1)} %cholesky.115), custom_call_target="Cholesky" | custom-call | tf_op jit(solution)/shard_map/jit(cholesky)/cholesky | solution.py:99
  170.0 0.1 copy.51
  170.2 9.8 %custom-call.14 = f32[1,128,128]{1,2,0:T(8,128)S(1)} custom-call(f32[1,128,128]{2,1,0:T(8,128)S(1)} %get-tuple-element.54), custom_call_target="InvertDiagBlocksLowerTriangular" | custom-call | tf_op jit(solution)/shard_map/jit(cholesky)/cholesky | solution.py:99
  180.0 0.2 fusion.36
  180.3 0.3 convolution_subtract_fusion.2
  180.6 11.7 %cholesky.103 = f32[128,128]{1,0:T(8,128)S(1)} custom-call(f32[128,128]{1,0:T(8,128)S(1)} %convolution_subtract_fusion.2), custom_call_target="Cholesky" | custom-call | tf_op jit(solution)/shard_map/jit(cholesky)/cholesky | solution.py:99
  192.4 0.7 compare_reduce_fusion.1
  193.1 0.6 compare_reduce_fusion.2
  195.2 4.3 %while.1 = (s32[]{:T(128)}, f32[256,256]{0,1:T(8,128)S(1)}, s32[2,2]{1,0:T(2,128)S(1)}, f32[2,128,128]{2,1,0:T(8,128)S(1)}, s32[]{:T(128)}) while((s32[]{:T(128)}, f32[256,256]{0,1:T(8,128)S(1)}, s32[2,2]{1,0:T(2,128)S(1)}, f32[2,128,128]{2,1,0:T(8,128)S(1)}, s32[]{:T(128)}) %tuple.49), condition=%wide.while_cond, body=%wide.while_body.sunk | while | flops 2 | bytes 393321 | solution.py:100
  195.2 0.6 fusion.71
  195.8 1.4 dynamic-slice.7
  197.4 0.6 fusion.71
  198.0 1.4 dynamic-slice.7
  199.5 19.9 %custom-call.15 = f32[2,128,128]{1,2,0:T(8,128)S(1)} custom-call(f32[2,128,128]{2,1,0:T(8,128)S(1)} %get-tuple-element.12), custom_call_target="InvertDiagBlocksLowerTriangular" | custom-call | tf_op jit(solution)/shard_map/triangular_solve | solution.py:100
  219.4 0.1 copy.54
  219.5 0.3 fusion.31
  219.8 0.3 convolution_subtract_fusion.1
  220.1 0.3 fusion.34
  220.5 0.4 fusion.13
  220.9 0.5 broadcast_in_dim.119
  221.5 1.1 copy-done.2
  223.0 1.9 bitcast_select_fusion
  224.9 3.8 %fusion.4 = f32[2048,256]{1,0:T(8,128)} fusion(f32[2048,256]{1,0:T(8,128)S(1)} %get-tuple-element.71, f32[2048,256]{1,0:T(8,128)S(1)} %get-tuple-element.72, f32[256,256]{1,0:T(8,128)S(1)} %fusion.13, f32[2048,512]{1,0:T(8,128)S(1)} %bitcast.151, f32[256]{0:T(256)S(1)} %copy-done.3, s32[256]{0:T(256)S(1)} %iota_add_fusion, s32[2048]{0:T(1024)S(1)} %fusion.47, ...), kind=kOutput, calls=%fused_computation.10 | convolution fusion | flops 1613758464 | bytes 8663041 | tf_op jit(solution)/shard_map/dot_general | solution.py:129
  (63 shorter events, 2.2 us)
Async XLA Ops:
  6.5 78.4 %all-gather.3.cloned.1.call-start = ((), (), s32[]{:S(2)}) async-start(), calls=%async_computation.1 | async-start | bytes 17301504 | tf_op jit(solution)/shard_map/all_gather | solution.py:29
  7.3 213.7 %reduce-scatter.2.cloned.1.call-start = ((), (), s32[]{:S(2)}) async-start(), calls=%async_computation.2 | async-start | bytes 10485760 | tf_op jit(solution)/shard_map/reduce_scatter | solution.py:88
  89.1 2.0 copy-start.1
  89.1 3.4 %copy-start = (s32[2,16]{1,0:T(2,128)S(1)}, s32[2,16]{1,0:T(2,128)}, u32[]{:S(2)}) copy-start(s32[2,16]{1,0:T(2,128)} %param.4) | copy-start | bytes 388
  91.1 14.1 %collective-permute-start = (f32[256,512]{0,1:T(8,128)S(1)}, f32[256,512]{0,1:T(8,128)S(1)}, u32[]{:S(2)}, u32[]{:S(2)}) collective-permute-start(f32[256,512]{0,1:T(8,128)S(1)} %fusion.10), channel_id=1, source_target_pairs={{0,32},{32,0},{64,96},{96,64},{1,33},{33,1},{65,97},{97,65},{2,34}... | collective-permute-start | bytes 1572872 | tf_op jit(solution)/shard_map/ppermute | solution.py:76
  105.3 27.0 %collective-permute-start.1 = (f32[256,512]{0,1:T(8,128)S(1)}, f32[256,512]{0,1:T(8,128)S(1)}, u32[]{:S(2)}, u32[]{:S(2)}) collective-permute-start(f32[256,512]{0,1:T(8,128)S(1)} %add.261), channel_id=1, source_target_pairs={{0,64},{32,96},{64,0},{96,32},{1,65},{33,97},{65,1},{97,33},{2,66}... | collective-permute-start | bytes 1572872 | tf_op jit(solution)/shard_map/ppermute | solution.py:76
  220.9 1.6 copy-start.2
  222.9 2.1 copy-start.3
Sparse Core Ops, SparseCore 0:
  9.6 75.2 all-gather.2
  141.5 78.1 reduce-scatter.1

commit v16 on v13

--- a/solution.py
+++ b/solution.py
@@ -49,10 +49,13 @@
     my_tiles = lax.dynamic_slice_in_dim(order, row_index * per_group, per_group, axis=1)
     my_root = jnp.take_along_axis(child_tiles, my_tiles, axis=1)
     my_local = (my_root * TILE // block_size) // row_count * tiles_block + my_root % tiles_block
-    n_slots = where_at.size
-    all_index = jnp.concatenate([where_at.reshape(-1), my_local.reshape(-1)]) + diag_edge
-    where_at = all_index[:n_slots].reshape(where_at.shape)
-    my_local = all_index[n_slots:].reshape(my_local.shape)
+    tile_ids = jnp.arange(loc_tiles, dtype=jnp.int32)
+    seen = sum(
+        lax.dynamic_index_in_dim(tile_ids, my_local[child, slot], 0, keepdims=False)
+        for child in range(n_child)
+        for slot in range(per_group)
+    )
+    where_at = where_at + diag_edge * (1 + seen)
     present = jnp.any(match, axis=1)
     col_rows = jnp.stack(
         [

time: 225 us -> 225 us (level)
    all_gather x1, waiting for transfers between devices: 29.6 us -> 13.9 us  [shards(): gathered = lax.all_gather(child_factors, 'col', axis=1, tiled=True)]
    reduce_scatter x1, waiting for transfers between devices: 1.66 us -> 16.9 us  [shards(): lax.psum_scatter(main.reshape(row_count * n_child * per_group * TILE, n_c...]
where the time goes in v16:
time: 225 us; the launch traced here: 223 us
  other arithmetic  60.5 us (27%)
  between operations  47.6 us (21%)
  waiting for transfers between devices  32.5 us (14%)
  local copies, waits for them, and re-layouts  30.9 us (14%)
  blocking collectives  26 us (12%)
  matrix products  19.9 us (9%)
  starting transfers between devices  5.65 us (3%)
    another operation x7, other arithmetic, shards(): lead = jnp.tril(jnp.linalg.cholesky(front00))  34.6 us
    all_gather x1, blocking collectives, shards(): full_diag = lax.all_gather(root_diag, 'col', axis=0, tiled=True)  26 us
    another operation x3, other arithmetic, shards(): lax.linalg.triangular_solve(lead, jnp.eye(lead_rows, dtype=jnp.float32),...  19.9 us
    reduce_scatter x1, waiting for transfers between devices, shards(): lax.psum_scatter(main.reshape(row_count * n_child * per_group * TILE, n_c...  16.9 us
    all_gather x1, waiting for transfers between devices, shards(): gathered = lax.all_gather(child_factors, 'col', axis=1, tiled=True)  13.9 us
    dot_general x1, matrix products, shards(): jnp.einsum('cutk,cmk->cutm', tiles4, main_rows, preferred_element_type=jn...  11.1 us
    reshape x1, local copies, waits for them, and re-layouts, shards(): main = main.reshape(n_child * tiles_child, TILE, n_cols)  8.99 us
    gather x1, local copies, waits for them, and re-layouts, shards(): main = jnp.take(main, flat_order, axis=0, mode='clip')  7.68 us
  transfers between devices with their start and end apart: 5, of which 3 were waited for; matrix products, arithmetic and copies ran while one was open for 39% of the time, Pallas kernels for 0%

profile of v16, /device:TPU:0, one launch (start us, length us, event | category | flops | bytes accessed | tf_op | source)
XLA Modules:
  0.0 223.2 jit_solution(523852464636578978)
XLA Ops:
  6.5 0.7 all-gather.3.cloned.1.call-update
  7.3 0.7 fusion.54
  8.0 0.2 convert_reduce_fusion
  8.5 1.3 gather_fusion.1
  10.0 0.7 fusion.61
  25.8 26.0 %all-gather = f32[32,1,256]{2,1,0:T(1,128)S(1)} all-gather(f32[1,1,256]{2,1,0:T(1,128)} %bitcast.173), channel_id=1, replica_groups=mesh['row'=4,'col'=32] {'col'}, dimensions={0}, use_global_device_ids=true | all-gather | bytes 33792 | tf_op jit(solution)/shard_map/all_gather | solution.py:32
  51.9 0.5 slice.199
  53.2 0.9 fusion.51
  54.0 0.7 fusion.60
  64.9 0.9 compare_reduce_fusion
  71.0 13.9 %all-gather.3.cloned.1.call-done = bf16[2,2048,2048]{2,1,0:T(8,128)(2,1)} async-done(((bf16[2,64,2048]{2,1,0:T(8,128)(2,1)}), bf16[2,2048,2048]{2,1,0:T(8,128)(2,1)}) %all-gather.3.cloned.1.call-update) | async-done | bytes 16777232 | tf_op jit(solution)/shard_map/all_gather | solution.py:29
  84.9 3.1 %dynamic-slice_bitcast_fusion.7 = (bf16[1,128,2048]{2,1,0:T(8,128)(2,1)S(1)}, bf16[1,128,2048]{2,1,0:T(8,128)(2,1)S(1)}, bf16[1,128,2048]{2,1,0:T(8,128)(2,1)S(1...) fusion(bf16[2,16,128,2048]{3,2,1,0:T(8,128)(2,1)} %bitcast.165,, ...), kind=kLoop, calls=%fused_computation.31 | loop fusion | bytes 8388640 | tf_op jit(solution)/shard_map/stack;squeeze | solution.py:62
  88.0 0.6 pad_maximum_fusion
  88.6 0.6 maximum_select_fusion
  89.2 1.3 fusion.10
  90.5 0.5 slice.203
  91.0 1.5 collective-permute-start
  92.5 2.7 %collective-permute-start.1 = (f32[256,512]{0,1:T(8,128)S(1)}, f32[256,512]{0,1:T(8,128)S(1)}, u32[]{:S(2)}, u32[]{:S(2)}) collective-permute-start(f32[256,512]{0,1:T(8,128)S(1)} %fusion.10), channel_id=1, source_target_pairs={{0,64},{32,96},{64,0},{96,32},{1,65},{33,97},{65,1},{97,33},{2,66}... | collective-permute-start | bytes 1572872 | tf_op jit(solution)/shard_map/ppermute | solution.py:84
  95.2 1.5 collective-permute-start.2
  97.3 11.1 %fusion = f32[2,512,16,128]{3,1,2,0:T(8,128)} fusion(bf16[2,16,128,2048]{3,2,1,0:T(8,128)(2,1)S(1)} %bitcast.168, bf16[2,512,2048]{2,1,0:T(8,128)(2,1)S(1)} %maximum_select_fusion, bf16[]{:T(256)} %bitcast.42), kind=kOutput, calls=%fused_computation.5 | convolution fusion | flops 8598323200 | bytes 29360130 | tf_op jit(solution)/shard_map/cutk,cmk->cutm/dot_general | solution.py:86
  108.4 9.0 %copy.67 = f32[32,128,512]{2,1,0:T(8,128)} copy(f32[32,128,512]{1,2,0:T(8,128)} %bitcast.154) | data formatting | bytes 16777216 | tf_op jit(solution)/shard_map/reshape | solution.py:89
  117.4 1.0 collective-permute-done.1
  118.4 1.2 add_add_fusion
  119.6 0.5 slice.204
  121.0 7.7 %gather_fusion = f32[32,128,512]{2,1,0:T(8,128)} fusion(f32[32,128,512]{2,1,0:T(8,128)} %copy.67, s32[1024]{0:T(1024)S(1)} %pad_clamp_fusion), kind=kCustom, calls=%fused_computation | custom fusion | bytes 16777344 | tf_op jit(solution)/shard_map/jit(_take)/gather | solution.py:94
  128.8 0.1 copy.60
  129.0 11.7 %cholesky.49 = f32[128,128]{1,0:T(8,128)S(1)} custom-call(f32[128,128]{1,0:T(8,128)S(1)} %cholesky.115), custom_call_target="Cholesky" | custom-call | tf_op jit(solution)/shard_map/jit(cholesky)/cholesky | solution.py:106
  140.9 9.8 %custom-call.14 = f32[1,128,128]{1,2,0:T(8,128)S(1)} custom-call(f32[1,128,128]{2,1,0:T(8,128)S(1)} %get-tuple-element.54), custom_call_target="InvertDiagBlocksLowerTriangular" | custom-call | tf_op jit(solution)/shard_map/jit(cholesky)/cholesky | solution.py:106
  150.7 0.2 fusion.36
  151.0 0.3 convolution_subtract_fusion.2
  151.3 11.7 %cholesky.103 = f32[128,128]{1,0:T(8,128)S(1)} custom-call(f32[128,128]{1,0:T(8,128)S(1)} %convolution_subtract_fusion.2), custom_call_target="Cholesky" | custom-call | tf_op jit(solution)/shard_map/jit(cholesky)/cholesky | solution.py:106
  163.1 0.7 compare_reduce_fusion.1
  163.8 0.6 compare_reduce_fusion.2
  165.9 4.3 %while.1 = (s32[]{:T(128)}, f32[256,256]{0,1:T(8,128)S(1)}, s32[2,2]{1,0:T(2,128)S(1)}, f32[2,128,128]{2,1,0:T(8,128)S(1)}, s32[]{:T(128)}) while((s32[]{:T(128)}, f32[256,256]{0,1:T(8,128)S(1)}, s32[2,2]{1,0:T(2,128)S(1)}, f32[2,128,128]{2,1,0:T(8,128)S(1)}, s32[]{:T(128)}) %tuple.49), condition=%wide.while_cond, body=%wide.while_body.sunk | while | flops 2 | bytes 393321 | solution.py:107
  166.0 0.6 fusion.71
  166.5 1.4 dynamic-slice.7
  168.1 0.6 fusion.71
  168.7 1.4 dynamic-slice.7
  170.2 19.9 %custom-call.15 = f32[2,128,128]{1,2,0:T(8,128)S(1)} custom-call(f32[2,128,128]{2,1,0:T(8,128)S(1)} %get-tuple-element.12), custom_call_target="InvertDiagBlocksLowerTriangular" | custom-call | tf_op jit(solution)/shard_map/triangular_solve | solution.py:107
  190.3 0.3 fusion.31
  190.5 0.3 convolution_subtract_fusion.1
  190.9 0.3 fusion.34
  191.2 0.4 fusion.13
  191.6 16.9 %reduce-scatter.2.cloned.1.call-done = f32[1024,512]{1,0:T(8,128)} async-done(((f32[4096,512]{1,0:T(8,128)}), f32[1024,512]{1,0:T(8,128)}) %reduce-scatter.2.cloned.1.call-update) | async-done | bytes 2097168 | tf_op jit(solution)/shard_map/reduce_scatter | solution.py:95
  208.5 0.5 broadcast_in_dim.121
  209.0 1.1 copy-done
  210.6 1.9 bitcast_select_fusion
  212.5 3.8 %fusion.4 = f32[2048,256]{1,0:T(8,128)} fusion(f32[2048,256]{1,0:T(8,128)S(1)} %get-tuple-element.71, f32[2048,256]{1,0:T(8,128)S(1)} %get-tuple-element.72, f32[256,256]{1,0:T(8,128)S(1)} %fusion.13, f32[2048,512]{1,0:T(8,128)S(1)} %bitcast.153, f32[256]{0:T(256)S(1)} %copy-done.1, s32[256]{0:T(256)S(1)} %iota_add_fusion, s32[2048]{0:T(1024)S(1)} %fusion.47, ...), kind=kOutput, calls=%fused_computation.10 | convolution fusion | flops 1613758464 | bytes 8663041 | tf_op jit(solution)/shard_map/dot_general | solution.py:133
  (69 shorter events, 2.3 us)
Async XLA Ops:
  6.5 78.3 %all-gather.3.cloned.1.call-start = ((), (), s32[]{:S(2)}) async-start(), calls=%async_computation.1 | async-start | bytes 17301504 | tf_op jit(solution)/shard_map/all_gather | solution.py:29
  7.3 201.2 %reduce-scatter.2.cloned.1.call-start = ((), (), s32[]{:S(2)}) async-start(), calls=%async_computation.2 | async-start | bytes 10485760 | tf_op jit(solution)/shard_map/reduce_scatter | solution.py:95
  84.9 12.4 %slice-start = ((s8[16777216]{0:T(1024)(128)(4,1)}), s8[4194304]{0:T(1024)(128)(4,1)S(1)}, s32[]{:S(2)}) async-start(s8[16777216]{0:T(1024)(128)(4,1)} %bitcast.166), calls=%async_computation.3 | async-start | bytes 8388608
  88.0 9.3 %slice-start.1 = ((s8[16777216]{0:T(1024)(128)(4,1)}), s8[4194304]{0:T(1024)(128)(4,1)S(1)}, s32[]{:S(2)}) async-start(s8[16777216]{0:T(1024)(128)(4,1)} %bitcast.166), calls=%async_computation.4 | async-start | bytes 8388608
  88.6 8.7 %slice-start.2 = ((s8[16777216]{0:T(1024)(128)(4,1)}), s8[4194304]{0:T(1024)(128)(4,1)S(1)}, s32[]{:S(2)}) async-start(s8[16777216]{0:T(1024)(128)(4,1)} %bitcast.166), calls=%async_computation.5 | async-start | bytes 8388608
  89.2 8.1 %slice-start.3 = ((s8[16777216]{0:T(1024)(128)(4,1)}), s8[4194304]{0:T(1024)(128)(4,1)S(1)}, s32[]{:S(2)}) async-start(s8[16777216]{0:T(1024)(128)(4,1)} %bitcast.166), calls=%async_computation.6 | async-start | bytes 8388608
  91.0 26.4 %collective-permute-start = (f32[256,512]{0,1:T(8,128)S(1)}, f32[256,512]{0,1:T(8,128)S(1)}, u32[]{:S(2)}, u32[]{:S(2)}) collective-permute-start(f32[256,512]{0,1:T(8,128)S(1)} %fusion.10), channel_id=1, source_target_pairs={{0,32},{32,64},{64,96},{96,0},{1,33},{33,65},{65,97},{97,1},{2,34}... | collective-permute-start | bytes 1572872 | tf_op jit(solution)/shard_map/ppermute | solution.py:84
  92.5 25.9 %collective-permute-start.1 = (f32[256,512]{0,1:T(8,128)S(1)}, f32[256,512]{0,1:T(8,128)S(1)}, u32[]{:S(2)}, u32[]{:S(2)}) collective-permute-start(f32[256,512]{0,1:T(8,128)S(1)} %fusion.10), channel_id=1, source_target_pairs={{0,64},{32,96},{64,0},{96,32},{1,65},{33,97},{65,1},{97,33},{2,66}... | collective-permute-start | bytes 1572872 | tf_op jit(solution)/shard_map/ppermute | solution.py:84
  95.2 23.2 %collective-permute-start.2 = (f32[256,512]{0,1:T(8,128)S(1)}, f32[256,512]{0,1:T(8,128)}, u32[]{:S(2)}, u32[]{:S(2)}) collective-permute-start(f32[256,512]{0,1:T(8,128)S(1)} %fusion.10), channel_id=1, source_target_pairs={{0,96},{32,0},{64,32},{96,64},{1,97},{33,1},{65,33},{97,65},{2,98}... | collective-permute-start | bytes 1572872 | tf_op jit(solution)/shard_map/ppermute | solution.py:84
  208.5 1.6 copy-start
  210.4 2.1 copy-start.1
Sparse Core Ops, SparseCore 0:
  9.6 75.1 all-gather.2
  128.8 79.6 reduce-scatter.1

commit v17 on v16

--- a/solution.py
+++ b/solution.py
@@ -79,9 +79,12 @@
         "cnk,cmk->nm", pivot_rows, col_rows, preferred_element_type=jnp.float32
     )
     pivot_part = extra
+    arrived = 0.0
     for shift in range(1, row_count):
         pairs = [(i, (i + shift) % row_count) for i in range(row_count)]
-        pivot_part = pivot_part + lax.ppermute(extra, "row", pairs)
+        moved = lax.ppermute(extra, "row", pairs)
+        arrived = arrived + moved[0, 0]
+        pivot_part = pivot_part + moved
     main_rows = col_rows + (extra[:1, :1] * 0).astype(col_rows.dtype)[None]
     main = jnp.einsum(
         "cutk,cmk->cutm", tiles4, main_rows, preferred_element_type=jnp.float32
@@ -90,7 +93,7 @@
     child_base = (jnp.arange(n_child, dtype=jnp.int32) * tiles_child)[:, None]
     flat_order = (order + child_base).reshape(n_child, row_count, per_group)
     flat_order = jnp.transpose(flat_order, (1, 0, 2)).reshape(-1)
-    flat_order = flat_order + (pivot_part[0, 0] * 0).astype(jnp.int32)
+    flat_order = flat_order + (arrived * 0).astype(jnp.int32)
     main = jnp.take(main, flat_order, axis=0, mode="clip")
     mine = lax.psum_scatter(
         main.reshape(row_count * n_child * per_group * TILE, n_cols),

time: 225 us -> 226 us (level)
    reduce_scatter x1, waiting for transfers between devices: 16.9 us -> 13.8 us  [shards(): lax.psum_scatter(main.reshape(row_count * n_child * per_group * TILE, n_c...]
    ppermute x3, waiting for transfers between devices: 1.01 us -> 3.63 us  [shards(): moved = lax.ppermute(extra, 'row', pairs)]
  transfers between devices with their start and end apart: 5 -> 5, of which waited for: 3 -> 3; matrix products, arithmetic and copies ran while one was open for 39% -> 40% of each run, Pallas kernels for 0% -> 0%
where the time goes in v17:
time: 226 us; the launch traced here: 225 us
  other arithmetic  60.5 us (27%)
  between operations  48.9 us (22%)
  local copies, waits for them, and re-layouts  32.6 us (14%)
  waiting for transfers between devices  32 us (14%)
  blocking collectives  26 us (12%)
  matrix products  19.9 us (9%)
  starting transfers between devices  4.44 us (2%)
    another operation x7, other arithmetic, shards(): lead = jnp.tril(jnp.linalg.cholesky(front00))  34.6 us
    all_gather x1, blocking collectives, shards(): full_diag = lax.all_gather(root_diag, 'col', axis=0, tiled=True)  26 us
    another operation x3, other arithmetic, shards(): lax.linalg.triangular_solve(lead, jnp.eye(lead_rows, dtype=jnp.float32),...  19.9 us
    all_gather x1, waiting for transfers between devices, shards(): gathered = lax.all_gather(child_factors, 'col', axis=1, tiled=True)  13.9 us
    reduce_scatter x1, waiting for transfers between devices, shards(): lax.psum_scatter(main.reshape(row_count * n_child * per_group * TILE, n_c...  13.8 us
    dot_general x1, matrix products, shards(): jnp.einsum('cutk,cmk->cutm', tiles4, main_rows, preferred_element_type=jn...  11.1 us
    reshape x1, local copies, waits for them, and re-layouts, shards(): main = main.reshape(n_child * tiles_child, TILE, n_cols)  8.99 us
    gather x1, local copies, waits for them, and re-layouts, shards(): main = jnp.take(main, flat_order, axis=0, mode='clip')  7.68 us
  transfers between devices with their start and end apart: 5, of which 3 were waited for; matrix products, arithmetic and copies ran while one was open for 40% of the time, Pallas kernels for 0%

profile of v17, /device:TPU:0, one launch (start us, length us, event | category | flops | bytes accessed | tf_op | source)
XLA Modules:
  0.0 224.5 jit_solution(15655266103085145612)
XLA Ops:
  6.5 0.7 all-gather.3.cloned.1.call-update
  7.3 0.7 fusion.54
  8.5 1.3 gather_fusion.1
  10.1 0.7 fusion.61
  25.9 26.0 %all-gather = f32[32,1,256]{2,1,0:T(1,128)S(1)} all-gather(f32[1,1,256]{2,1,0:T(1,128)} %bitcast.173), channel_id=1, replica_groups=mesh['row'=4,'col'=32] {'col'}, dimensions={0}, use_global_device_ids=true | all-gather | bytes 33792 | tf_op jit(solution)/shard_map/all_gather | solution.py:32
  52.0 0.5 slice.207
  53.2 0.9 fusion.51
  54.1 0.7 fusion.60
  64.9 0.9 compare_reduce_fusion
  71.0 13.9 %all-gather.3.cloned.1.call-done = bf16[2,2048,2048]{2,1,0:T(8,128)(2,1)} async-done(((bf16[2,64,2048]{2,1,0:T(8,128)(2,1)}), bf16[2,2048,2048]{2,1,0:T(8,128)(2,1)}) %all-gather.3.cloned.1.call-update) | async-done | bytes 16777232 | tf_op jit(solution)/shard_map/all_gather | solution.py:29
  84.9 3.1 %dynamic-slice_bitcast_fusion.7 = (bf16[1,128,2048]{2,1,0:T(8,128)(2,1)S(1)}, bf16[1,128,2048]{2,1,0:T(8,128)(2,1)S(1)}, bf16[1,128,2048]{2,1,0:T(8,128)(2,1)S(1...) fusion(bf16[2,16,128,2048]{3,2,1,0:T(8,128)(2,1)} %bitcast.165,, ...), kind=kLoop, calls=%fused_computation.31 | loop fusion | bytes 8388640 | tf_op jit(solution)/shard_map/stack;squeeze | solution.py:62
  88.0 0.6 pad_maximum_fusion
  88.6 0.6 maximum_select_fusion
  89.2 1.3 fusion.10
  90.5 0.5 slice.211
  91.0 2.7 %collective-permute-start.2 = (f32[256,512]{0,1:T(8,128)S(1)}, f32[256,512]{0,1:T(8,128)S(1)}, u32[]{:S(2)}, u32[]{:S(2)}) collective-permute-start(f32[256,512]{0,1:T(8,128)S(1)} %fusion.10), channel_id=1, source_target_pairs={{0,96},{32,0},{64,32},{96,64},{1,97},{33,1},{65,33},{97,65},{2,98}... | collective-permute-start | bytes 1572872 | tf_op jit(solution)/shard_map/ppermute | solution.py:85
  93.7 0.8 collective-permute-start.1
  94.6 0.9 collective-permute-start
  96.1 11.1 %fusion = f32[2,512,16,128]{3,1,2,0:T(8,128)} fusion(bf16[2,16,128,2048]{3,2,1,0:T(8,128)(2,1)S(1)} %bitcast.168, bf16[2,512,2048]{2,1,0:T(8,128)(2,1)S(1)} %maximum_select_fusion, bf16[]{:T(256)} %bitcast.42), kind=kOutput, calls=%fused_computation.5 | convolution fusion | flops 8598323200 | bytes 29360130 | tf_op jit(solution)/shard_map/cutk,cmk->cutm/dot_general | solution.py:89
  107.2 9.0 %copy.67 = f32[32,128,512]{2,1,0:T(8,128)} copy(f32[32,128,512]{1,2,0:T(8,128)} %bitcast.154) | data formatting | bytes 16777216 | tf_op jit(solution)/shard_map/reshape | solution.py:92
  116.2 0.5 slice.213
  116.7 3.6 %collective-permute-done = f32[256,512]{0,1:T(8,128)} collective-permute-done((f32[256,512]{0,1:T(8,128)S(1)}, f32[256,512]{0,1:T(8,128)}, u32[]{:S(2)}, u32[]{:S(2)}) %collective-permute-start) | collective-permute-done | bytes 524320 | tf_op jit(solution)/shard_map/ppermute | solution.py:85
  120.4 1.2 slice.212
  122.9 0.5 slice.214
  124.2 7.7 %gather_fusion = f32[32,128,512]{2,1,0:T(8,128)} fusion(f32[32,128,512]{2,1,0:T(8,128)} %copy.67, s32[1024]{0:T(1024)S(1)} %pad_clamp_fusion), kind=kCustom, calls=%fused_computation | custom fusion | bytes 16777344 | tf_op jit(solution)/shard_map/jit(_take)/gather | solution.py:97
  132.0 1.2 add_add_fusion
  133.4 11.7 %cholesky.49 = f32[128,128]{1,0:T(8,128)S(1)} custom-call(f32[128,128]{1,0:T(8,128)S(1)} %cholesky.115), custom_call_target="Cholesky" | custom-call | tf_op jit(solution)/shard_map/jit(cholesky)/cholesky | solution.py:109
  145.3 9.8 %custom-call.14 = f32[1,128,128]{1,2,0:T(8,128)S(1)} custom-call(f32[1,128,128]{2,1,0:T(8,128)S(1)} %get-tuple-element.54), custom_call_target="InvertDiagBlocksLowerTriangular" | custom-call | tf_op jit(solution)/shard_map/jit(cholesky)/cholesky | solution.py:109
  155.1 0.2 fusion.36
  155.4 0.3 convolution_subtract_fusion.2
  155.7 11.7 %cholesky.103 = f32[128,128]{1,0:T(8,128)S(1)} custom-call(f32[128,128]{1,0:T(8,128)S(1)} %convolution_subtract_fusion.2), custom_call_target="Cholesky" | custom-call | tf_op jit(solution)/shard_map/jit(cholesky)/cholesky | solution.py:109
  167.5 0.6 compare_reduce_fusion.2
  168.2 0.7 compare_reduce_fusion.1
  170.5 4.3 %while.1 = (s32[]{:T(128)}, f32[256,256]{0,1:T(8,128)S(1)}, s32[2,2]{1,0:T(2,128)S(1)}, f32[2,128,128]{2,1,0:T(8,128)S(1)}, s32[]{:T(128)}) while((s32[]{:T(128)}, f32[256,256]{0,1:T(8,128)S(1)}, s32[2,2]{1,0:T(2,128)S(1)}, f32[2,128,128]{2,1,0:T(8,128)S(1)}, s32[]{:T(128)}) %tuple.49), condition=%wide.while_cond, body=%wide.while_body.sunk | while | flops 2 | bytes 393329 | solution.py:110
  170.5 0.6 fusion.71
  171.1 1.4 dynamic-slice.7
  172.7 0.6 fusion.71
  173.2 1.4 dynamic-slice.7
  174.8 19.9 %custom-call.15 = f32[2,128,128]{1,2,0:T(8,128)S(1)} custom-call(f32[2,128,128]{2,1,0:T(8,128)S(1)} %get-tuple-element.12), custom_call_target="InvertDiagBlocksLowerTriangular" | custom-call | tf_op jit(solution)/shard_map/triangular_solve | solution.py:110
  194.7 0.3 fusion.31
  195.0 0.3 convolution_subtract_fusion.1
  195.3 0.3 fusion.34
  195.6 0.4 fusion.13
  196.0 13.8 %reduce-scatter.2.cloned.1.call-done = f32[1024,512]{1,0:T(8,128)} async-done(((f32[4096,512]{1,0:T(8,128)}), f32[1024,512]{1,0:T(8,128)}) %reduce-scatter.2.cloned.1.call-update) | async-done | bytes 2097168 | tf_op jit(solution)/shard_map/reduce_scatter | solution.py:98
  209.8 0.5 broadcast_in_dim.121
  210.3 1.1 copy-done
  211.9 1.9 bitcast_select_fusion
  213.8 3.8 %fusion.4 = f32[2048,256]{1,0:T(8,128)} fusion(f32[2048,256]{1,0:T(8,128)S(1)} %get-tuple-element.71, f32[2048,256]{1,0:T(8,128)S(1)} %get-tuple-element.72, f32[256,256]{1,0:T(8,128)S(1)} %fusion.13, f32[2048,512]{1,0:T(8,128)S(1)} %bitcast.153, f32[256]{0:T(256)S(1)} %copy-done.1, s32[256]{0:T(256)S(1)} %iota_add_fusion, s32[2048]{0:T(1024)S(1)} %fusion.47, ...), kind=kOutput, calls=%fused_computation.10 | convolution fusion | flops 1613758464 | bytes 8663041 | tf_op jit(solution)/shard_map/dot_general | solution.py:136
  (71 shorter events, 2.7 us)
Async XLA Ops:
  6.5 78.3 %all-gather.3.cloned.1.call-start = ((), (), s32[]{:S(2)}) async-start(), calls=%async_computation.1 | async-start | bytes 17301504 | tf_op jit(solution)/shard_map/all_gather | solution.py:29
  7.3 202.6 %reduce-scatter.2.cloned.1.call-start = ((), (), s32[]{:S(2)}) async-start(), calls=%async_computation.2 | async-start | bytes 10485760 | tf_op jit(solution)/shard_map/reduce_scatter | solution.py:98
  84.9 11.2 %slice-start = ((s8[16777216]{0:T(1024)(128)(4,1)}), s8[4194304]{0:T(1024)(128)(4,1)S(1)}, s32[]{:S(2)}) async-start(s8[16777216]{0:T(1024)(128)(4,1)} %bitcast.166), calls=%async_computation.3 | async-start | bytes 8388608
  88.0 8.1 %slice-start.1 = ((s8[16777216]{0:T(1024)(128)(4,1)}), s8[4194304]{0:T(1024)(128)(4,1)S(1)}, s32[]{:S(2)}) async-start(s8[16777216]{0:T(1024)(128)(4,1)} %bitcast.166), calls=%async_computation.4 | async-start | bytes 8388608
  88.6 7.5 %slice-start.2 = ((s8[16777216]{0:T(1024)(128)(4,1)}), s8[4194304]{0:T(1024)(128)(4,1)S(1)}, s32[]{:S(2)}) async-start(s8[16777216]{0:T(1024)(128)(4,1)} %bitcast.166), calls=%async_computation.5 | async-start | bytes 8388608
  89.2 6.9 %slice-start.3 = ((s8[16777216]{0:T(1024)(128)(4,1)}), s8[4194304]{0:T(1024)(128)(4,1)S(1)}, s32[]{:S(2)}) async-start(s8[16777216]{0:T(1024)(128)(4,1)} %bitcast.166), calls=%async_computation.6 | async-start | bytes 8388608
  91.0 31.8 %collective-permute-start.2 = (f32[256,512]{0,1:T(8,128)S(1)}, f32[256,512]{0,1:T(8,128)S(1)}, u32[]{:S(2)}, u32[]{:S(2)}) collective-permute-start(f32[256,512]{0,1:T(8,128)S(1)} %fusion.10), channel_id=1, source_target_pairs={{0,96},{32,0},{64,32},{96,64},{1,97},{33,1},{65,33},{97,65},{2,98}... | collective-permute-start | bytes 1572872 | tf_op jit(solution)/shard_map/ppermute | solution.py:85
  93.7 22.5 %collective-permute-start.1 = (f32[256,512]{0,1:T(8,128)S(1)}, f32[256,512]{0,1:T(8,128)S(1)}, u32[]{:S(2)}, u32[]{:S(2)}) collective-permute-start(f32[256,512]{0,1:T(8,128)S(1)} %fusion.10), channel_id=1, source_target_pairs={{0,64},{32,96},{64,0},{96,32},{1,65},{33,97},{65,1},{97,33},{2,66}... | collective-permute-start | bytes 1572872 | tf_op jit(solution)/shard_map/ppermute | solution.py:85
  94.6 25.8 %collective-permute-start = (f32[256,512]{0,1:T(8,128)S(1)}, f32[256,512]{0,1:T(8,128)}, u32[]{:S(2)}, u32[]{:S(2)}) collective-permute-start(f32[256,512]{0,1:T(8,128)S(1)} %fusion.10), channel_id=1, source_target_pairs={{0,32},{32,64},{64,96},{96,0},{1,33},{33,65},{65,97},{97,1},{2,34}... | collective-permute-start | bytes 1572872 | tf_op jit(solution)/shard_map/ppermute | solution.py:85
  209.8 1.6 copy-start
  211.7 2.1 copy-start.1
Sparse Core Ops, SparseCore 0:
  9.6 75.1 all-gather.2
  132.0 77.7 reduce-scatter.1
